TPU v7x, 256 devices: a whole 4x4x8 slice. The times are simulated.
256 devices in a mesh: tm: 64 (over x, z_lo, y), feed: 4 (over z_hi, core).
Axes of the slice: x: 4, y: 4, z: 8 (z_hi: 2, z_lo: 4; z = z_hi * 4 + z_lo), core: 2. Of those that a mesh axis runs over, the one named last changes fastest.
Arguments:
- voltages: bfloat16 [1024, 131072], P('feed', 'tm'), may hold values from -6 to 6
- coefficients: float32 [16, 2048], replicated, may hold values from -1.5 to 1.5
- beam_weights: bfloat16 [1024, 1024, 2, 512], P('tm', 'feed'), may hold values from -0.1875 to 0.1875
Outputs:
- beam_power: float32 [8, 1024, 512], P(None, 'tm', 'feed')
All inputs are finite; a program needn't handle non-finite values.
Results may differ from a plain program's by a relative error of at most 0.0025.
Values may be sent and summed in bfloat16 or wider, within the bound.
No kernel may reach another device: no remote copies, remote signals or barrier semaphores. Data moves between devices by JAX's collectives and lax.ppermute only.
A program may use at most 128 MiB of HBM per device.

v0:
```python
import math

import jax
import jax.numpy as jnp
from jax import lax
from jax.sharding import PartitionSpec as P

INTEG = 8


def dft_rows(frame_len, n_groups):
    channels = frame_len // 2
    inner = 64
    outer = frame_len // inner
    cols = 2 * channels
    col = lax.broadcasted_iota(jnp.int32, (cols, 1), 0)
    per_group = channels // n_groups
    group = col // (2 * per_group)
    channel = group * per_group + (col % (2 * per_group)) // 2
    part = col % 2
    step = 2.0 * math.pi / frame_len
    high = lax.broadcasted_iota(jnp.int32, (1, outer), 1)
    low = lax.broadcasted_iota(jnp.int32, (1, inner), 1)
    high_angle = step * ((inner * high * channel) % frame_len).astype(jnp.float32)
    low_angle = step * ((low * channel) % frame_len).astype(jnp.float32)
    cos_high = jnp.cos(high_angle)
    sin_high = jnp.sin(high_angle)
    first = jnp.where(part == 0, cos_high, -sin_high)
    second = jnp.where(part == 0, sin_high, cos_high)
    cos_low = jnp.cos(low_angle)
    sin_low = jnp.sin(low_angle)
    norming = 1.0 / math.sqrt(frame_len)
    table = (
        first[:, :, None] * cos_low[:, None, :] - second[:, :, None] * sin_low[:, None, :]
    ) * norming
    return table.reshape(cols, frame_len).astype(jnp.bfloat16)


def polyphase(extended, coefficients, frames):
    tap_count = coefficients.shape[0]
    running = jnp.zeros((extended.shape[0], frames, extended.shape[2]), jnp.float32)
    for tap_index in range(tap_count):
        running = running + coefficients[tap_index][None, None, :] * extended[
            :, tap_index : tap_index + frames, :
        ].astype(jnp.float32)
    return running.astype(jnp.bfloat16)


def halve(value, axis, flip):
    count = lax.axis_size(axis)
    own = lax.axis_index(axis) // flip % 2
    pairs = [(i, i ^ flip) for i in range(count)]
    above = count // (2 * flip)
    lead = value.shape[0]
    split = value.reshape(above, 2, lead // (2 * above), *value.shape[1:])
    kept = lax.dynamic_index_in_dim(split, own, 1, keepdims=False)
    sent = lax.dynamic_index_in_dim(split, 1 - own, 1, keepdims=False)
    summed = kept + lax.ppermute(sent, axis, pairs)
    return summed.reshape(lead // 2, *value.shape[1:])


def local(voltages, coefficients, beam_weights):
    n_tm = lax.axis_size("tm")
    n_feed = lax.axis_size("feed")
    feeds_here, samples = voltages.shape
    tap_count, frame_len = coefficients.shape
    frames_here = samples // frame_len
    total_frames = n_tm * frames_here
    per_dev = feeds_here // n_tm

    blocks = voltages.reshape(n_tm, per_dev, samples)
    blocks = lax.all_to_all(blocks, "tm", 0, 0, tiled=True)
    frames = blocks.reshape(n_tm, per_dev, frames_here, frame_len)
    frames = jnp.transpose(frames, (1, 0, 2, 3)).reshape(per_dev, total_frames, frame_len)
    padding = jnp.zeros((per_dev, tap_count - 1, frame_len), frames.dtype)
    extended = jnp.concatenate([frames, padding], axis=1)
    filtered = polyphase(extended, coefficients, total_frames)

    table = dft_rows(frame_len, n_tm)
    spectra = jnp.einsum(
        "jk,mk->jm",
        table,
        filtered.reshape(per_dev * total_frames, frame_len),
        preferred_element_type=jnp.float32,
    ).astype(jnp.bfloat16)
    cols = table.shape[0]
    group_cols = cols // n_tm
    per_group = group_cols // 2
    spectra = spectra.reshape(n_tm, group_cols, per_dev * total_frames)
    turned = lax.all_to_all(spectra, "tm", 0, 0, tiled=True)
    turned = turned.reshape(n_tm, per_group, 2, per_dev, total_frames)
    turned = jnp.transpose(turned, (1, 0, 3, 2, 4)).reshape(per_group, feeds_here, 2, total_frames)
    real_part = turned[:, :, 0]
    imag_part = turned[:, :, 1]
    for_real = jnp.stack([real_part, -imag_part], axis=2)
    for_imag = jnp.stack([imag_part, real_part], axis=2)
    paired = jnp.concatenate([for_real, for_imag], axis=3).reshape(
        per_group, feeds_here * 2, 2 * total_frames
    )
    weights = beam_weights.reshape(per_group, feeds_here * 2, beam_weights.shape[3])
    beams = jnp.einsum("ckb,ckn->bcn", weights, paired, preferred_element_type=jnp.float32)
    flip = 1
    while flip < n_feed:
        beams = halve(beams, "feed", flip)
        flip *= 2
    beams = beams.reshape(beams.shape[0], per_group, 2, total_frames)
    energy = jnp.sum(beams * beams, axis=2)
    binned = jnp.mean(
        energy.reshape(energy.shape[0], per_group, total_frames // INTEG, INTEG), axis=3
    )
    return jnp.transpose(binned, (2, 1, 0))


def solution(mesh):
    placed = (P("feed", "tm"), P(), P("tm", "feed", None, None))
    return jax.shard_map(
        local, mesh=mesh, in_specs=placed, out_specs=P(None, "tm", "feed"), check_vma=False
    )
```

profile of v0, /device:TPU:1, one launch (start us, length us, event | category | flops | bytes accessed | tf_op | source)
XLA Modules:
  0.0 182.9 jit_solution(5151068268653492912)
XLA Ops:
  0.0 0.0 copy-start.2
  0.0 2.3 %reshape.331 = bf16[64,4,2048]{2,1,0:T(4,128)(2,1)} reshape(bf16[256,2048]{1,0:T(8,128)(2,1)} %param.3) | data formatting | bytes 2097152 | tf_op jit(solution)/shard_map/reshape | solution.py:71
  2.3 12.6 %all-to-all-start = ((bf16[64,4,2048]{2,1,0:T(4,128)(2,1)}), bf16[64,4,2048]{2,1,0:T(4,128)(2,1)S(1)}, u32[]{:S(2)}, u32[]{:S(2)}) async-start(bf16[64,4,2048]{2,1,0:T(4,128)(2,1)} %reshape.331), calls=%async_computation | async-start | bytes 2097152 | tf_op jit(solution)/shard_map/all_to_all | solution.py:72
  14.9 0.0 copy-done.2
  14.9 0.1 fusion.33
  15.0 1.1 negate_select_fusion.3
  16.2 2.0 %fusion.11 = (f32[2048,64]{0,1:T(8,128)S(1)}, f32[2048,64]{0,1:T(8,128)S(1)}) fusion(s32[2048]{0:T(1024)S(1)} %fusion.23), kind=kLoop, calls=%fused_computation.30 | loop fusion | flops 1835008 | bytes 1056768 | tf_op jit(solution)/shard_map/cos | solution.py:30
  18.2 6.2 %multiply_convert_fusion = bf16[2048,32,64]{0,2,1:T(8,128)(2,1)} fusion(f32[2048,64]{0,1:T(8,128)S(1)} %get-tuple-element.29, f32[2048,32]{0,1:T(8,128)S(1)} %get-tuple-element.27, f32[2048,64]{0,1:T(8,128)S(1)} %get-tuple-element.28, f32[2048,32]{0,1:T(8,128)S(1)} %get-tuple-element.26), kind=kLoop, calls=%fused_computation | loop fusion | flops 20971520 | bytes 9961472 | tf_op jit(solution)/shard_map/convert_element_type | solution.py:36
  24.4 18.6 %all-to-all-done = bf16[64,4,2048]{2,1,0:T(4,128)(2,1)S(1)} async-done(((bf16[64,4,2048]{2,1,0:T(4,128)(2,1)}), bf16[64,4,2048]{2,1,0:T(4,128)(2,1)S(1)}, u32[]{:S(2)}, u32[]{:S(2)}) %all-to-all-start) | async-done | bytes 1048608 | tf_op jit(solution)/shard_map/all_to_all | solution.py:72
  43.0 8.3 %add_convert_fusion = bf16[4,64,2048]{2,0,1:T(4,128)(2,1)S(1)} fusion(bf16[4,64,2048]{2,0,1:T(4,128)(2,1)S(1)} %bitcast.46, f32[2048]{0:T(1024)S(1)} %bitcast.63, f32[2048]{0:T(1024)S(1)} %bitcast.64, f32[2048]{0:T(1024)S(1)} %bitcast.50, f32[2048]{0:T(1024)S(1)} %bitcast.51, f32[2048]{0:T(1024)S(1)} %bitcast.52, f32[2048]{0:T(1024)S(1)} %bitcast.53, ...), kind=kLoop, calls=%fused_computation.5 | loop fusion | flops 25165824 | bytes 2228224 | tf_op jit(solution)/shard_map/convert_element_type | solution.py:46
  51.3 0.6 copy.10
  51.9 7.0 %convolution_convert_fusion = bf16[2048,256]{1,0:T(8,128)(2,1)} fusion(bf16[2048,2048]{0,1:T(8,128)(2,1)} %bitcast.44, bf16[256,2048]{1,0:T(8,128)(2,1)S(1)} %bitcast.48), kind=kOutput, calls=%fused_computation.1 | convolution fusion | flops 2148007936 | bytes 10485760 | tf_op jit(solution)/shard_map/jk,mk->jm/dot_general | solution.py:80
  58.8 6.1 %all-to-all-start.1 = ((bf16[64,32,256]{2,1,0:T(8,128)(2,1)}), bf16[64,32,256]{2,1,0:T(8,128)(2,1)S(1)}, u32[]{:S(2)}, u32[]{:S(2)}) async-start(bf16[64,32,256]{2,1,0:T(8,128)(2,1)} %bitcast.23), calls=%async_computation.1 | async-start | bytes 2097152 | tf_op jit(solution)/shard_map/all_to_all | solution.py:90
  64.9 13.1 %reshape.339 = bf16[16,512,512]{2,1,0:T(8,128)(2,1)} reshape(bf16[16,256,2,512]{3,2,1,0:T(2,128)(2,1)} %param.5) | data formatting | bytes 16777216 | tf_op jit(solution)/shard_map/reshape | solution.py:100
  78.1 14.7 %all-to-all-done.1 = bf16[64,32,256]{2,1,0:T(8,128)(2,1)S(1)} async-done(((bf16[64,32,256]{2,1,0:T(8,128)(2,1)}), bf16[64,32,256]{2,1,0:T(8,128)(2,1)S(1)}, u32[]{:S(2)}, u32[]{:S(2)}) %all-to-all-start.1) | async-done | bytes 1048608 | tf_op jit(solution)/shard_map/all_to_all | solution.py:90
  92.8 0.8 reshape.336
  93.7 0.6 copy.11
  94.3 0.0 copy-start
  94.3 0.3 slice_negate_fusion
  94.6 1.2 maximum_maximum_fusion
  95.8 1.9 %copy-done = bf16[16,512,512]{2,1,0:T(8,128)(2,1)S(1)} copy-done((bf16[16,512,512]{2,1,0:T(8,128)(2,1)S(1)}, bf16[16,512,512]{2,1,0:T(8,128)(2,1)}, u32[]{:S(2)}) %copy-start) | copy-done | bytes 8388632
  97.7 3.6 %convolution_bitcast_fusion = f32[512,16,128]{0,2,1:T(8,128)} fusion(bf16[16,512,512]{2,1,0:T(8,128)(2,1)S(1)} %copy-done, bf16[16,512,128]{2,0,1:T(8,128)(2,1)S(1)} %bitcast.42), kind=kOutput, calls=%fused_computation.2 | convolution fusion | flops 1073741824 | bytes 14680064 | tf_op jit(solution)/shard_map/ckb,ckn->bcn/dot_general | solution.py:101
  101.3 5.9 %reshape.340 = f32[2,2,128,16,128]{2,1,0,4,3:T(2,128)} reshape(f32[512,16,128]{0,2,1:T(8,128)} %convolution_bitcast_fusion) | data formatting | bytes 8388608 | tf_op jit(solution)/shard_map/reshape | solution.py:55
  107.1 9.2 %constant_dynamic-slice_fusion.1 = (f32[2,1,128,16,128]{2,1,0,4,3:T(1,128)}, f32[2,1,128,16,128]{2,1,0,4,3:T(1,128)S(1)}) fusion(f32[2,2,128,16,128]{2,1,0,4,3:T(2,128)} %reshape.340, s32[]{:T(128)S(6)} %select_n.119, s32[]{:T(128)S(6)} %select_n.118), kind=kLoop, calls=%fused_computation.65 | loop fusion | bytes 8388616 | tf_op jit(solution)/shard_map/jit(dynamic_index_in_dim)/dynamic_slice | solution.py:57
  116.3 2.4 %collective-permute-start = (f32[2,128,16,128]{1,0,3,2:T(2,128)}, f32[2,128,16,128]{1,0,3,2:T(2,128)}, u32[]{:S(2)}, u32[]{:S(2)}) collective-permute-start(f32[2,128,16,128]{1,0,3,2:T(2,128)} %bitcast.30), channel_id=1, source_target_pairs={{0,1},{1,0},{2,3},{3,2},{4,5},{5,4},{6,7},{7,6},{8,9},{9,8},{10,11... | collective-permute-start | bytes 6291464 | tf_op jit(solution)/shard_map/ppermute | solution.py:58
  118.7 4.1 %collective-permute-done = f32[2,128,16,128]{1,0,3,2:T(2,128)} collective-permute-done((f32[2,128,16,128]{1,0,3,2:T(2,128)}, f32[2,128,16,128]{1,0,3,2:T(2,128)}, u32[]{:S(2)}, u32[]{:S(2)}) %collective-permute-start) | collective-permute-done | bytes 2097184 | tf_op jit(solution)/shard_map/ppermute | solution.py:58
  122.9 2.7 %add.167 = f32[2,128,16,128]{1,0,3,2:T(2,128)S(1)} add(f32[2,128,16,128]{1,0,3,2:T(2,128)S(1)} %bitcast.43, f32[2,128,16,128]{1,0,3,2:T(2,128)} %collective-permute-done) | non-fusion elementwise | flops 524288 | bytes 6291456 | tf_op jit(solution)/shard_map/add | solution.py:58
  125.5 0.0 copy-start.1
  125.6 1.3 copy-done.1
  126.9 1.1 constant_dynamic-slice_fusion
  128.0 4.3 %collective-permute-start.1 = (f32[1,128,16,128]{1,0,3,2:T(1,128)S(1)}, f32[1,128,16,128]{1,0,3,2:T(1,128)S(1)}, u32[]{:S(2)}, u32[]{:S(2)}) collective-permute-start(f32[1,128,16,128]{1,0,3,2:T(1,128)S(1)} %constant_dynamic-slice_fusion), channel_id=1, source_target_pairs={{0,2},{1,3},{2,0},{3,1},{4,6},{5,7},{6,4},{7,5},{8,10},{9,11},{10,... | collective-permute-start | bytes 3145736 | tf_op jit(solution)/shard_map/ppermute | solution.py:58
  132.3 46.7 %collective-permute-done.1 = f32[1,128,16,128]{1,0,3,2:T(1,128)S(1)} collective-permute-done((f32[1,128,16,128]{1,0,3,2:T(1,128)S(1)}, f32[1,128,16,128]{1,0,3,2:T(1,128)S(1)}, u32[]{:S(2)}, u32[]{:S(2)}) %collective-permute-start.1) | collective-permute-done | bytes 1048608 | tf_op jit(solution)/shard_map/ppermute | solution.py:58
  179.0 3.0 %add_multiply_fusion = f32[1,128,16,128]{1,0,3,2:T(1,128)S(1)} fusion(f32[1,128,16,128]{1,0,3,2:T(1,128)S(1)} %collective-permute-done.1, f32[2,128,16,128]{1,0,3,2:T(2,128)} %copy-done.1, s32[]{:T(128)S(6)} %select_n.122), kind=kLoop, calls=%fused_computation.6 | loop fusion | flops 524288 | bytes 3145732 | tf_op jit(solution)/shard_map/mul | solution.py:107
  182.0 0.1 reduce_sum.18
  182.1 0.1 bitcast_reduce_fusion
  182.2 0.6 copy.13
  (4 shorter events, 0.0 us)
Async XLA Ops:
  0.0 14.9 %copy-start.2 = (f32[16,2048]{1,0:T(8,128)S(1)}, f32[16,2048]{1,0:T(8,128)}, u32[]{:S(2)}) copy-start(f32[16,2048]{1,0:T(8,128)} %param.4) | copy-start | bytes 393220
  2.3 40.7 %all-to-all-start = ((bf16[64,4,2048]{2,1,0:T(4,128)(2,1)}), bf16[64,4,2048]{2,1,0:T(4,128)(2,1)S(1)}, u32[]{:S(2)}, u32[]{:S(2)}) async-start(bf16[64,4,2048]{2,1,0:T(4,128)(2,1)} %reshape.331), calls=%async_computation | async-start | bytes 2097152 | tf_op jit(solution)/shard_map/all_to_all | solution.py:72
  58.8 34.0 %all-to-all-start.1 = ((bf16[64,32,256]{2,1,0:T(8,128)(2,1)}), bf16[64,32,256]{2,1,0:T(8,128)(2,1)S(1)}, u32[]{:S(2)}, u32[]{:S(2)}) async-start(bf16[64,32,256]{2,1,0:T(8,128)(2,1)} %bitcast.23), calls=%async_computation.1 | async-start | bytes 2097152 | tf_op jit(solution)/shard_map/all_to_all | solution.py:90
  94.3 3.4 %copy-start = (bf16[16,512,512]{2,1,0:T(8,128)(2,1)S(1)}, bf16[16,512,512]{2,1,0:T(8,128)(2,1)}, u32[]{:S(2)}) copy-start(bf16[16,512,512]{2,1,0:T(8,128)(2,1)} %reshape.339) | copy-start | bytes 25165828
  116.3 6.5 %collective-permute-start = (f32[2,128,16,128]{1,0,3,2:T(2,128)}, f32[2,128,16,128]{1,0,3,2:T(2,128)}, u32[]{:S(2)}, u32[]{:S(2)}) collective-permute-start(f32[2,128,16,128]{1,0,3,2:T(2,128)} %bitcast.30), channel_id=1, source_target_pairs={{0,1},{1,0},{2,3},{3,2},{4,5},{5,4},{6,7},{7,6},{8,9},{9,8},{10,11... | collective-permute-start | bytes 6291464 | tf_op jit(solution)/shard_map/ppermute | solution.py:58
  125.5 1.3 copy-start.1
  128.0 51.0 %collective-permute-start.1 = (f32[1,128,16,128]{1,0,3,2:T(1,128)S(1)}, f32[1,128,16,128]{1,0,3,2:T(1,128)S(1)}, u32[]{:S(2)}, u32[]{:S(2)}) collective-permute-start(f32[1,128,16,128]{1,0,3,2:T(1,128)S(1)} %constant_dynamic-slice_fusion), channel_id=1, source_target_pairs={{0,2},{1,3},{2,0},{3,1},{4,6},{5,7},{6,4},{7,5},{8,10},{9,11},{10,... | collective-permute-start | bytes 3145736 | tf_op jit(solution)/shard_map/ppermute | solution.py:58
where the time goes:
time: 184 us; the launch traced here: 183 us
  waiting for transfers between devices  84.2 us (46%)
  local copies, waits for them, and re-layouts  37.7 us (20%)
  starting transfers between devices  25.3 us (14%)
  other arithmetic  25 us (14%)
  matrix products  10.6 us (6%)
    ppermute x2, waiting for transfers between devices, halve(): summed = kept + lax.ppermute(sent, axis, pairs)  50.8 us
    all_to_all x1, waiting for transfers between devices, local(): blocks = lax.all_to_all(blocks, 'tm', 0, 0, tiled=True)  18.6 us
    all_to_all x1, waiting for transfers between devices, local(): turned = lax.all_to_all(spectra, 'tm', 0, 0, tiled=True)  14.7 us
    reshape x1, local copies, waits for them, and re-layouts, local(): beam_weights.reshape(per_group, feeds_here * 2, beam_weights.shape[3])  13.1 us
    all_to_all x1, starting transfers between devices, local(): blocks = lax.all_to_all(blocks, 'tm', 0, 0, tiled=True)  12.6 us
    dynamic_slice x1, local copies, waits for them, and re-layouts, halve(): sent = lax.dynamic_index_in_dim(split, 1 - own, 1, keepdims=False)  9.2 us
    convert_element_type x1, other arithmetic, polyphase(): return running.astype(jnp.bfloat16)  8.27 us
    dot_general x1, matrix products, local(): jnp.einsum('jk,mk->jm', table, filtered.reshape(per_dev * total_frames, f...  6.98 us
  transfers between devices with their start and end apart: 4, of which 4 were waited for; matrix products, arithmetic and copies ran while one was open for 12% of the time, Pallas kernels for 0%

commit v1 on v0

v1 whole, which is shorter than its diff:
```python
import math

import jax
import jax.numpy as jnp
from jax import lax
from jax.sharding import PartitionSpec as P

INTEG = 8


def dft_rows(frame_len, n_groups, n_halves):
    channels = frame_len // 2
    inner = 64
    outer = frame_len // inner
    cols = 2 * channels
    col = lax.broadcasted_iota(jnp.int32, (cols, 1), 0)
    per_group = channels // n_groups
    per_half = per_group // n_halves
    half = col // (2 * channels // n_halves)
    group = col % (2 * channels // n_halves) // (2 * per_half)
    channel = group * per_group + half * per_half + (col % (2 * per_half)) // 2
    part = col % 2
    step = 2.0 * math.pi / frame_len
    high = lax.broadcasted_iota(jnp.int32, (1, outer), 1)
    low = lax.broadcasted_iota(jnp.int32, (1, inner), 1)
    high_angle = step * ((inner * high * channel) % frame_len).astype(jnp.float32)
    low_angle = step * ((low * channel) % frame_len).astype(jnp.float32)
    cos_high = jnp.cos(high_angle)
    sin_high = jnp.sin(high_angle)
    first = jnp.where(part == 0, cos_high, -sin_high)
    second = jnp.where(part == 0, sin_high, cos_high)
    cos_low = jnp.cos(low_angle)
    sin_low = jnp.sin(low_angle)
    norming = 1.0 / math.sqrt(frame_len)
    table = (
        first[:, :, None] * cos_low[:, None, :] - second[:, :, None] * sin_low[:, None, :]
    ) * norming
    return table.reshape(cols, frame_len).astype(jnp.bfloat16)


def polyphase(extended, coefficients, frames):
    tap_count = coefficients.shape[0]
    running = jnp.zeros((extended.shape[0], frames, extended.shape[2]), jnp.float32)
    for tap_index in range(tap_count):
        running = running + coefficients[tap_index][None, None, :] * extended[
            :, tap_index : tap_index + frames, :
        ].astype(jnp.float32)
    return running.astype(jnp.bfloat16)


def exchange(blocks, axis, flip):
    count = lax.axis_size(axis)
    bit = lax.axis_index(axis) // flip % 2
    from_low = [(i, i ^ flip) for i in range(count) if i // flip % 2 == 0]
    from_high = [(i, i ^ flip) for i in range(count) if i // flip % 2 == 1]
    to_high = lax.ppermute(blocks[1], axis, from_low)
    to_low = lax.ppermute(blocks[0], axis, from_high)
    return jnp.where(bit == 0, blocks[0], blocks[1]) + to_high + to_low


def local(voltages, coefficients, beam_weights):
    n_tm = lax.axis_size("tm")
    n_feed = lax.axis_size("feed")
    feeds_here, samples = voltages.shape
    tap_count, frame_len = coefficients.shape
    frames_here = samples // frame_len
    total_frames = n_tm * frames_here
    per_dev = feeds_here // n_tm

    blocks = voltages.reshape(n_tm, per_dev, samples)
    blocks = lax.all_to_all(blocks, "tm", 0, 0, tiled=True)
    frames = blocks.reshape(n_tm, per_dev, frames_here, frame_len)
    frames = jnp.transpose(frames, (1, 0, 2, 3)).reshape(per_dev, total_frames, frame_len)
    padding = jnp.zeros((per_dev, tap_count - 1, frame_len), frames.dtype)
    extended = jnp.concatenate([frames, padding], axis=1)
    filtered = polyphase(extended, coefficients, total_frames)

    n_halves = 2
    table = dft_rows(frame_len, n_tm, n_halves)
    cols = table.shape[0]
    group_cols = cols // n_tm // n_halves
    per_half = group_cols // 2
    samples_flat = filtered.reshape(per_dev * total_frames, frame_len)
    beam_count = beam_weights.shape[3]
    per_out = beam_count // n_feed
    binned_parts = []
    for half in range(n_halves):
        rows = table[half * (cols // n_halves) : (half + 1) * (cols // n_halves)]
        spectra = jnp.einsum(
            "jk,mk->jm", rows, samples_flat, preferred_element_type=jnp.float32
        ).astype(jnp.bfloat16)
        spectra = spectra.reshape(n_tm, group_cols, per_dev * total_frames)
        turned = lax.all_to_all(spectra, "tm", 0, 0, tiled=True)
        turned = turned.reshape(n_tm, per_half, 2, per_dev, total_frames)
        turned = jnp.transpose(turned, (1, 0, 3, 2, 4)).reshape(
            per_half, feeds_here, 2, total_frames
        )
        real_part = turned[:, :, 0]
        imag_part = turned[:, :, 1]
        for_real = jnp.stack([real_part, -imag_part], axis=2)
        for_imag = jnp.stack([imag_part, real_part], axis=2)
        paired = jnp.concatenate([for_real, for_imag], axis=3).reshape(
            per_half, feeds_here * 2, 2 * total_frames
        )
        weights = beam_weights[half * per_half : (half + 1) * per_half].reshape(
            per_half, feeds_here * 2, n_feed, per_out
        )
        beams = jnp.einsum("ckjb,ckn->jcbn", weights, paired, preferred_element_type=jnp.float32)
        flip = 1
        while flip < n_feed:
            split = beams.reshape(-1, 2, *beams.shape[1:])
            beams = exchange((split[:, 0], split[:, 1]), "feed", flip).reshape(
                -1, *beams.shape[1:]
            )
            flip *= 2
        summed = beams[0].reshape(per_half, per_out, 2, total_frames)
        energy = jnp.sum(summed * summed, axis=2)
        binned_parts.append(
            jnp.mean(energy.reshape(per_half, per_out, total_frames // INTEG, INTEG), axis=3)
        )
    binned = jnp.concatenate(binned_parts, axis=0)
    return jnp.transpose(binned, (2, 0, 1))


def solution(mesh):
    placed = (P("feed", "tm"), P(), P("tm", "feed", None, None))
    return jax.shard_map(
        local, mesh=mesh, in_specs=placed, out_specs=P(None, "tm", "feed"), check_vma=False
    )
```

time: 184 us -> 196 us (1.065)
  starting transfers between devices: 25.3 us -> 55.3 us
  waiting for transfers between devices: 84.2 us -> 68.3 us
  other arithmetic: 25 us -> 21.8 us
  matrix products: 10.6 us -> 8.14 us
  local copies, waits for them, and re-layouts: 37.7 us -> 39.8 us
    ppermute x2 -> x8, starting transfers between devices: 6.69 us -> 31.2 us  [the longest x4 18.9 us: exchange(): to_high = lax.ppermute(blocks[1], axis, from_low)]
    ppermute x2 -> x8, waiting for transfers between devices: 50.8 us -> 37.7 us  [the longest x4 33.2 us: exchange(): to_low = lax.ppermute(blocks[0], axis, from_high)]
    slice x0 -> x3, local copies, waits for them, and re-layouts: none -> 12.5 us  [the longest x1 8.41 us: local(): beam_weights[half * per_half:(half + 1) * per_half]]
    dynamic_slice x1 -> x0, local copies, waits for them, and re-layouts: 9.2 us -> none  [halve(): sent = lax.dynamic_index_in_dim(split, 1 - own, 1, keepdims=False)]
    all_to_all x1 -> x2, starting transfers between devices: 6.08 us -> 11.5 us  [local(): turned = lax.all_to_all(spectra, 'tm', 0, 0, tiled=True)]
    reshape x0 -> x2, other arithmetic: none -> 3.95 us  [local(): split = beams.reshape(-1, 2, *beams.shape[1:])]
    reshape x4 -> x6, local copies, waits for them, and re-layouts: 20.5 us -> 16.6 us  [the longest x2 15.2 us: local(): beam_weights[half * per_half:(half + 1) * per_half]]
    convert_element_type x1, other arithmetic: 6.18 us -> 2.84 us  [dft_rows(): return table.reshape(cols, frame_len).astype(jnp.bfloat16)]
  transfers between devices with their start and end apart: 4 -> 11, of which waited for: 4 -> 5; matrix products, arithmetic and copies ran while one was open for 12% -> 25% of each run, Pallas kernels for 0% -> 0%
where the time goes in v1:
time: 196 us; the launch traced here: 194 us
  waiting for transfers between devices  68.3 us (35%)
  starting transfers between devices  55.3 us (28%)
  local copies, waits for them, and re-layouts  39.8 us (20%)
  other arithmetic  21.8 us (11%)
  matrix products  8.14 us (4%)
    ppermute x4, waiting for transfers between devices, exchange(): to_low = lax.ppermute(blocks[0], axis, from_high)  33.2 us
    ppermute x4, starting transfers between devices, exchange(): to_high = lax.ppermute(blocks[1], axis, from_low)  18.9 us
    all_to_all x1, waiting for transfers between devices, local(): blocks = lax.all_to_all(blocks, 'tm', 0, 0, tiled=True)  18 us
    reshape x2, local copies, waits for them, and re-layouts, local(): beam_weights[half * per_half:(half + 1) * per_half]  15.2 us
    all_to_all x2, waiting for transfers between devices, local(): turned = lax.all_to_all(spectra, 'tm', 0, 0, tiled=True)  12.6 us
    all_to_all x1, starting transfers between devices, local(): blocks = lax.all_to_all(blocks, 'tm', 0, 0, tiled=True)  12.6 us
    ppermute x4, starting transfers between devices, exchange(): to_low = lax.ppermute(blocks[0], axis, from_high)  12.2 us
    all_to_all x2, starting transfers between devices, local(): turned = lax.all_to_all(spectra, 'tm', 0, 0, tiled=True)  11.5 us
  transfers between devices with their start and end apart: 11, of which 5 were waited for; matrix products, arithmetic and copies ran while one was open for 25% of the time, Pallas kernels for 0%

profile of v1, /device:TPU:1, one launch (start us, length us, event | category | flops | bytes accessed | tf_op | source)
XLA Modules:
  0.0 193.8 jit_solution(14026510412855921801)
XLA Ops:
  0.0 2.3 %reshape.438 = bf16[64,4,2048]{2,1,0:T(4,128)(2,1)} reshape(bf16[256,2048]{1,0:T(8,128)(2,1)} %param.3) | data formatting | bytes 2097152 | tf_op jit(solution)/shard_map/reshape | solution.py:70
  2.4 12.6 %all-to-all-start = ((bf16[64,4,2048]{2,1,0:T(4,128)(2,1)}), bf16[64,4,2048]{2,1,0:T(4,128)(2,1)S(1)}, u32[]{:S(2)}, u32[]{:S(2)}) async-start(bf16[64,4,2048]{2,1,0:T(4,128)(2,1)} %reshape.438), calls=%async_computation | async-start | bytes 2097152 | tf_op jit(solution)/shard_map/all_to_all | solution.py:71
  15.0 1.1 negate_select_fusion.3
  16.2 2.0 %fusion.17 = (f32[2048,64]{0,1:T(8,128)S(1)}, f32[2048,64]{0,1:T(8,128)S(1)}) fusion(s32[2048]{0:T(1024)S(1)} %fusion.35), kind=kLoop, calls=%fused_computation.51 | loop fusion | flops 1835008 | bytes 1056768 | tf_op jit(solution)/shard_map/cos | solution.py:32
  18.2 2.8 %multiply_convert_fusion = bf16[2048,32,64]{0,2,1:T(8,128)(2,1)S(1)} fusion(f32[2048,64]{0,1:T(8,128)S(1)} %get-tuple-element.42, f32[2048,32]{0,1:T(8,128)S(1)} %get-tuple-element.40, f32[2048,64]{0,1:T(8,128)S(1)} %get-tuple-element.41, f32[2048,32]{0,1:T(8,128)S(1)} %get-tuple-element.39), kind=kLoop, calls=%fused_computation | loop fusion | flops 20971520 | bytes 9961472 | tf_op jit(solution)/shard_map/convert_element_type | solution.py:38
  21.1 3.9 %fusion.51 = (bf16[1024,32,64]{0,2,1:T(8,128)(2,1)}, bf16[1024,32,64]{0,2,1:T(8,128)(2,1)}) fusion(bf16[2048,32,64]{0,2,1:T(8,128)(2,1)S(1)} %multiply_convert_fusion), kind=kLoop, calls=%fused_computation.107 | loop fusion | bytes 16777216 | tf_op jit(solution)/shard_map/slice | solution.py:88
  25.0 18.0 %all-to-all-done = bf16[64,4,2048]{2,1,0:T(4,128)(2,1)S(1)} async-done(((bf16[64,4,2048]{2,1,0:T(4,128)(2,1)}), bf16[64,4,2048]{2,1,0:T(4,128)(2,1)S(1)}, u32[]{:S(2)}, u32[]{:S(2)}) %all-to-all-start) | async-done | bytes 1048608 | tf_op jit(solution)/shard_map/all_to_all | solution.py:71
  43.0 8.3 %add_convert_fusion = bf16[4,64,2048]{2,0,1:T(4,128)(2,1)S(1)} fusion(bf16[4,64,2048]{2,0,1:T(4,128)(2,1)S(1)} %bitcast.100, f32[2048]{0:T(1024)S(1)} %bitcast.123, f32[2048]{0:T(1024)S(1)} %bitcast.124, f32[2048]{0:T(1024)S(1)} %bitcast.110, f32[2048]{0:T(1024)S(1)} %bitcast.111, f32[2048]{0:T(1024)S(1)} %bitcast.112, f32[2048]{0:T(1024)S(1)} %bitcast.113, ...), kind=kLoop, calls=%fused_computation.5 | loop fusion | flops 25165824 | bytes 2228224 | tf_op jit(solution)/shard_map/convert_element_type | solution.py:48
  51.4 0.6 copy.44
  51.9 2.1 %convolution_convert_fusion.1 = bf16[1024,256]{1,0:T(8,128)(2,1)} fusion(bf16[1024,2048]{0,1:T(8,128)(2,1)S(1)} %bitcast.104, bf16[256,2048]{1,0:T(8,128)(2,1)S(1)} %bitcast.107), kind=kOutput, calls=%fused_computation.7 | convolution fusion | flops 1074003968 | bytes 5767168 | tf_op jit(solution)/shard_map/jk,mk->jm/dot_general | solution.py:89
  54.1 6.1 %all-to-all-start.1 = ((bf16[64,16,256]{2,1,0:T(8,128)(2,1)}), bf16[64,16,256]{2,1,0:T(8,128)(2,1)S(1)}, u32[]{:S(2)}, u32[]{:S(2)}) async-start(bf16[64,16,256]{2,1,0:T(8,128)(2,1)} %bitcast.23), calls=%async_computation.1 | async-start | bytes 1048576 | tf_op jit(solution)/shard_map/all_to_all | solution.py:93
  60.2 4.3 %convolution_convert_fusion = bf16[1024,256]{1,0:T(8,128)(2,1)} fusion(bf16[1024,2048]{0,1:T(8,128)(2,1)} %bitcast.103, bf16[256,2048]{1,0:T(8,128)(2,1)S(1)} %bitcast.108), kind=kOutput, calls=%fused_computation.6 | convolution fusion | flops 1074003968 | bytes 5767168 | tf_op jit(solution)/shard_map/jk,mk->jm/dot_general | solution.py:89
  64.5 12.6 %all-to-all-done.1 = bf16[64,16,256]{2,1,0:T(8,128)(2,1)S(1)} async-done(((bf16[64,16,256]{2,1,0:T(8,128)(2,1)}), bf16[64,16,256]{2,1,0:T(8,128)(2,1)S(1)}, u32[]{:S(2)}, u32[]{:S(2)}) %all-to-all-start.1) | async-done | bytes 524320 | tf_op jit(solution)/shard_map/all_to_all | solution.py:93
  77.1 5.5 %all-to-all-start.2 = ((bf16[64,16,256]{2,1,0:T(8,128)(2,1)}), bf16[64,16,256]{2,1,0:T(8,128)(2,1)S(1)}, u32[]{:S(2)}, u32[]{:S(2)}) async-start(bf16[64,16,256]{2,1,0:T(8,128)(2,1)} %bitcast.40), calls=%async_computation.2 | async-start | bytes 1048576 | tf_op jit(solution)/shard_map/all_to_all | solution.py:93
  82.6 8.4 %fusion.52 = (bf16[8,256,2,512]{3,2,1,0:T(2,128)(2,1)}, bf16[8,256,2,512]{3,2,1,0:T(2,128)(2,1)}) fusion(bf16[16,256,2,512]{3,2,1,0:T(2,128)(2,1)} %param.5), kind=kLoop, calls=%fused_computation.108 | loop fusion | bytes 16777216 | tf_op jit(solution)/shard_map/slice | solution.py:105
  91.0 7.6 %reshape.460 = bf16[8,512,4,128]{3,2,1,0:T(4,128)(2,1)} reshape(bf16[8,256,2,512]{3,2,1,0:T(2,128)(2,1)} %get-tuple-element.7) | data formatting | bytes 8388608 | tf_op jit(solution)/shard_map/reshape | solution.py:105
  98.6 7.6 %reshape.461 = bf16[8,512,4,128]{3,2,1,0:T(4,128)(2,1)} reshape(bf16[8,256,2,512]{3,2,1,0:T(2,128)(2,1)} %get-tuple-element.8) | data formatting | bytes 8388608 | tf_op jit(solution)/shard_map/reshape | solution.py:105
  106.2 0.4 reshape.443
  106.6 0.3 copy.45
  106.9 0.4 reshape.451
  107.3 0.3 copy.54
  107.6 0.1 slice_negate_fusion
  107.9 0.6 maximum_maximum_fusion
  108.5 1.4 copy-done.1
  109.9 0.8 fusion.2
  110.8 1.2 slice_bitcast_fusion
  112.0 1.1 copy.103
  113.1 4.6 %collective-permute-start.1 = (f32[2,8,128,128]{2,3,1,0:T(8,128)}, f32[2,8,128,128]{2,3,1,0:T(8,128)}, u32[]{:S(2)}, u32[]{:S(2)}) collective-permute-start(f32[2,8,128,128]{2,3,1,0:T(8,128)} %bitcast.95), channel_id=1, source_target_pairs={{1,0},{3,2},{5,4},{7,6},{9,8},{11,10},{13,12},{15,14},{17,16},{19,... | collective-permute-start | bytes 3145736 | tf_op jit(solution)/shard_map/ppermute | solution.py:57
  117.7 1.3 collective-permute-start
  119.0 0.6 maximum_maximum_fusion.1
  119.6 0.8 fusion
  120.4 0.1 fusion.53
  120.6 1.1 copy.101
  121.7 1.1 copy.102
  122.8 5.0 %collective-permute-start.5 = (f32[2,8,128,128]{2,3,1,0:T(8,128)}, f32[2,8,128,128]{2,3,1,0:T(8,128)}, u32[]{:S(2)}, u32[]{:S(2)}) collective-permute-start(f32[2,8,128,128]{2,3,1,0:T(8,128)} %bitcast.94), channel_id=1, source_target_pairs={{1,0},{3,2},{5,4},{7,6},{9,8},{11,10},{13,12},{15,14},{17,16},{19,... | collective-permute-start | bytes 3145736 | tf_op jit(solution)/shard_map/ppermute | solution.py:57
  127.8 1.3 collective-permute-start.4
  129.1 2.1 %fusion.6 = f32[1,2,8,128,128]{3,4,1,2,0:T(8,128)S(1)} fusion(f32[2,8,128,128]{2,3,1,0:T(8,128)} %collective-permute-done.1, f32[2,8,128,128]{2,3,0,1:T(8,128)} %collective-permute-done, f32[2,8,128,128]{2,3,0,1:T(8,128)} %get-tuple-element.9, pred[]{:T(512)S(6)} %eq.33, f32[2,1,8,128,128]{3,4,1,0,2:T(8,128)S(1)} %get-tuple-element.10), kind=kLoop, calls=%fused_computation.17 | loop fusion | flops 786432 | bytes 5242881 | tf_op jit(solution)/shard_map/reshape | solution.py:111
  131.3 1.1 slice_bitcast_fusion.3
  132.4 6.9 %collective-permute-start.2 = (f32[1,8,128,128]{2,3,1,0:T(8,128)}, f32[1,8,128,128]{2,3,1,0:T(8,128)}, u32[]{:S(2)}, u32[]{:S(2)}) collective-permute-start(f32[1,8,128,128]{2,3,1,0:T(8,128)} %get-tuple-element.13), channel_id=1, source_target_pairs={{0,2},{1,3},{4,6},{5,7},{8,10},{9,11},{12,14},{13,15},{16,18},{17,... | collective-permute-start | bytes 1572872 | tf_op jit(solution)/shard_map/ppermute | solution.py:56
  139.3 1.3 collective-permute-start.3
  140.6 1.8 add_bitcast_fusion
  142.5 9.5 %collective-permute-start.6 = (f32[1,8,128,128]{2,3,1,0:T(8,128)S(1)}, f32[1,8,128,128]{2,3,1,0:T(8,128)}, u32[]{:S(2)}, u32[]{:S(2)}) collective-permute-start(f32[1,8,128,128]{2,3,1,0:T(8,128)S(1)} %get-tuple-element.18), channel_id=1, source_target_pairs={{0,2},{1,3},{4,6},{5,7},{8,10},{9,11},{12,14},{13,15},{16,18},{17,... | collective-permute-start | bytes 1572872 | tf_op jit(solution)/shard_map/ppermute | solution.py:56
  152.0 1.3 collective-permute-start.7
  153.3 3.2 %collective-permute-done.3 = f32[1,8,128,128]{2,3,1,0:T(8,128)} collective-permute-done((f32[1,8,128,128]{2,3,1,0:T(8,128)}, f32[1,8,128,128]{2,3,1,0:T(8,128)}, u32[]{:S(2)}, u32[]{:S(2)}) %collective-permute-start.3) | collective-permute-done | bytes 524320 | tf_op jit(solution)/shard_map/ppermute | solution.py:57
  156.5 4.5 %collective-permute-done.6 = f32[1,8,128,128]{2,3,1,0:T(8,128)} collective-permute-done((f32[1,8,128,128]{2,3,1,0:T(8,128)S(1)}, f32[1,8,128,128]{2,3,1,0:T(8,128)}, u32[]{:S(2)}, u32[]{:S(2)}) %collective-permute-start.6) | collective-permute-done | bytes 524320 | tf_op jit(solution)/shard_map/ppermute | solution.py:56
  161.0 30.0 %collective-permute-done.7 = f32[1,8,128,128]{2,3,1,0:T(8,128)} collective-permute-done((f32[1,8,128,128]{2,3,1,0:T(8,128)S(1)}, f32[1,8,128,128]{2,3,1,0:T(8,128)}, u32[]{:S(2)}, u32[]{:S(2)}) %collective-permute-start.7) | collective-permute-done | bytes 524320 | tf_op jit(solution)/shard_map/ppermute | solution.py:57
  191.0 1.8 add_multiply_fusion
  193.1 0.6 copy.60
  (30 shorter events, 0.6 us)
Async XLA Ops:
  0.0 16.1 %copy-start.5 = (f32[16,2048]{1,0:T(8,128)S(1)}, f32[16,2048]{1,0:T(8,128)}, u32[]{:S(2)}) copy-start(f32[16,2048]{1,0:T(8,128)} %param.4) | copy-start | bytes 393220
  2.4 40.7 %all-to-all-start = ((bf16[64,4,2048]{2,1,0:T(4,128)(2,1)}), bf16[64,4,2048]{2,1,0:T(4,128)(2,1)S(1)}, u32[]{:S(2)}, u32[]{:S(2)}) async-start(bf16[64,4,2048]{2,1,0:T(4,128)(2,1)} %reshape.438), calls=%async_computation | async-start | bytes 2097152 | tf_op jit(solution)/shard_map/all_to_all | solution.py:71
  43.0 8.9 %copy-start.4 = (bf16[1024,32,64]{0,2,1:T(8,128)(2,1)S(1)}, bf16[1024,32,64]{0,2,1:T(8,128)(2,1)}, u32[]{:S(2)}) copy-start(bf16[1024,32,64]{0,2,1:T(8,128)(2,1)} %get-tuple-element.5) | copy-start | bytes 12582916
  54.1 23.0 %all-to-all-start.1 = ((bf16[64,16,256]{2,1,0:T(8,128)(2,1)}), bf16[64,16,256]{2,1,0:T(8,128)(2,1)S(1)}, u32[]{:S(2)}, u32[]{:S(2)}) async-start(bf16[64,16,256]{2,1,0:T(8,128)(2,1)} %bitcast.23), calls=%async_computation.1 | async-start | bytes 1048576 | tf_op jit(solution)/shard_map/all_to_all | solution.py:93
  77.1 29.8 %all-to-all-start.2 = ((bf16[64,16,256]{2,1,0:T(8,128)(2,1)}), bf16[64,16,256]{2,1,0:T(8,128)(2,1)S(1)}, u32[]{:S(2)}, u32[]{:S(2)}) async-start(bf16[64,16,256]{2,1,0:T(8,128)(2,1)} %bitcast.40), calls=%async_computation.2 | async-start | bytes 1048576 | tf_op jit(solution)/shard_map/all_to_all | solution.py:93
  107.8 2.2 %copy-start.1 = (bf16[8,512,4,128]{3,2,1,0:T(4,128)(2,1)S(1)}, bf16[8,512,4,128]{3,2,1,0:T(4,128)(2,1)}, u32[]{:S(2)}) copy-start(bf16[8,512,4,128]{3,2,1,0:T(4,128)(2,1)} %reshape.460) | copy-start | bytes 12582916
  112.0 7.6 %copy-start = (bf16[8,512,4,128]{3,2,1,0:T(4,128)(2,1)S(1)}, bf16[8,512,4,128]{3,2,1,0:T(4,128)(2,1)}, u32[]{:S(2)}) copy-start(bf16[8,512,4,128]{3,2,1,0:T(4,128)(2,1)} %reshape.461) | copy-start | bytes 12582916
  113.1 16.0 %collective-permute-start.1 = (f32[2,8,128,128]{2,3,1,0:T(8,128)}, f32[2,8,128,128]{2,3,1,0:T(8,128)}, u32[]{:S(2)}, u32[]{:S(2)}) collective-permute-start(f32[2,8,128,128]{2,3,1,0:T(8,128)} %bitcast.95), channel_id=1, source_target_pairs={{1,0},{3,2},{5,4},{7,6},{9,8},{11,10},{13,12},{15,14},{17,16},{19,... | collective-permute-start | bytes 3145736 | tf_op jit(solution)/shard_map/ppermute | solution.py:57
  117.7 11.4 %collective-permute-start = (f32[2,8,128,128]{2,3,0,1:T(8,128)}, f32[2,8,128,128]{2,3,0,1:T(8,128)}, u32[]{:S(2)}, u32[]{:S(2)}) collective-permute-start(f32[2,8,128,128]{2,3,0,1:T(8,128)} %get-tuple-element.9), channel_id=1, source_target_pairs={{0,1},{2,3},{4,5},{6,7},{8,9},{10,11},{12,13},{14,15},{16,17},{18,... | collective-permute-start | bytes 3145736 | tf_op jit(solution)/shard_map/ppermute | solution.py:56
  120.6 2.2 %copy-start.2 = (f32[2,1,8,128,128]{3,4,1,0,2:T(8,128)}, f32[2,1,8,128,128]{3,4,1,0,2:T(8,128)S(1)}, u32[]{:S(2)}) copy-start(f32[2,1,8,128,128]{3,4,1,0,2:T(8,128)S(1)} %get-tuple-element.12) | copy-start | bytes 3145732
  122.8 17.8 %collective-permute-start.5 = (f32[2,8,128,128]{2,3,1,0:T(8,128)}, f32[2,8,128,128]{2,3,1,0:T(8,128)}, u32[]{:S(2)}, u32[]{:S(2)}) collective-permute-start(f32[2,8,128,128]{2,3,1,0:T(8,128)} %bitcast.94), channel_id=1, source_target_pairs={{1,0},{3,2},{5,4},{7,6},{9,8},{11,10},{13,12},{15,14},{17,16},{19,... | collective-permute-start | bytes 3145736 | tf_op jit(solution)/shard_map/ppermute | solution.py:57
  127.8 12.8 %collective-permute-start.4 = (f32[2,8,128,128]{2,3,1,0:T(8,128)}, f32[2,8,128,128]{2,3,1,0:T(8,128)}, u32[]{:S(2)}, u32[]{:S(2)}) collective-permute-start(f32[2,8,128,128]{2,3,1,0:T(8,128)} %bitcast.93), channel_id=1, source_target_pairs={{0,1},{2,3},{4,5},{6,7},{8,9},{10,11},{12,13},{14,15},{16,17},{18,... | collective-permute-start | bytes 3145736 | tf_op jit(solution)/shard_map/ppermute | solution.py:56
  131.3 9.3 %copy-start.3 = (f32[2,1,8,128,128]{3,4,1,0,2:T(8,128)S(1)}, f32[2,1,8,128,128]{3,4,1,0,2:T(8,128)}, u32[]{:S(2)}) copy-start(f32[2,1,8,128,128]{3,4,1,0,2:T(8,128)} %copy-done.2) | copy-start | bytes 3145732
  132.4 20.9 %collective-permute-start.2 = (f32[1,8,128,128]{2,3,1,0:T(8,128)}, f32[1,8,128,128]{2,3,1,0:T(8,128)}, u32[]{:S(2)}, u32[]{:S(2)}) collective-permute-start(f32[1,8,128,128]{2,3,1,0:T(8,128)} %get-tuple-element.13), channel_id=1, source_target_pairs={{0,2},{1,3},{4,6},{5,7},{8,10},{9,11},{12,14},{13,15},{16,18},{17,... | collective-permute-start | bytes 1572872 | tf_op jit(solution)/shard_map/ppermute | solution.py:56
  139.3 17.2 %collective-permute-start.3 = (f32[1,8,128,128]{2,3,1,0:T(8,128)}, f32[1,8,128,128]{2,3,1,0:T(8,128)}, u32[]{:S(2)}, u32[]{:S(2)}) collective-permute-start(f32[1,8,128,128]{2,3,1,0:T(8,128)} %get-tuple-element.14), channel_id=1, source_target_pairs={{2,0},{3,1},{6,4},{7,5},{10,8},{11,9},{14,12},{15,13},{18,16},{19,... | collective-permute-start | bytes 1572872 | tf_op jit(solution)/shard_map/ppermute | solution.py:57
  142.5 18.4 %collective-permute-start.6 = (f32[1,8,128,128]{2,3,1,0:T(8,128)S(1)}, f32[1,8,128,128]{2,3,1,0:T(8,128)}, u32[]{:S(2)}, u32[]{:S(2)}) collective-permute-start(f32[1,8,128,128]{2,3,1,0:T(8,128)S(1)} %get-tuple-element.18), channel_id=1, source_target_pairs={{0,2},{1,3},{4,6},{5,7},{8,10},{9,11},{12,14},{13,15},{16,18},{17,... | collective-permute-start | bytes 1572872 | tf_op jit(solution)/shard_map/ppermute | solution.py:56
  152.0 39.0 %collective-permute-start.7 = (f32[1,8,128,128]{2,3,1,0:T(8,128)S(1)}, f32[1,8,128,128]{2,3,1,0:T(8,128)}, u32[]{:S(2)}, u32[]{:S(2)}) collective-permute-start(f32[1,8,128,128]{2,3,1,0:T(8,128)S(1)} %get-tuple-element.19), channel_id=1, source_target_pairs={{2,0},{3,1},{6,4},{7,5},{10,8},{11,9},{14,12},{15,13},{18,16},{19,... | collective-permute-start | bytes 1572872 | tf_op jit(solution)/shard_map/ppermute | solution.py:57

commit v2 on v0

--- a/solution.py
+++ b/solution.py
@@ -46,17 +46,14 @@
     return running.astype(jnp.bfloat16)
 
 
-def halve(value, axis, flip):
+def exchange(blocks, axis, flip):
     count = lax.axis_size(axis)
-    own = lax.axis_index(axis) // flip % 2
-    pairs = [(i, i ^ flip) for i in range(count)]
-    above = count // (2 * flip)
-    lead = value.shape[0]
-    split = value.reshape(above, 2, lead // (2 * above), *value.shape[1:])
-    kept = lax.dynamic_index_in_dim(split, own, 1, keepdims=False)
-    sent = lax.dynamic_index_in_dim(split, 1 - own, 1, keepdims=False)
-    summed = kept + lax.ppermute(sent, axis, pairs)
-    return summed.reshape(lead // 2, *value.shape[1:])
+    bit = lax.axis_index(axis) // flip % 2
+    from_low = [(i, i ^ flip) for i in range(count) if i // flip % 2 == 0]
+    from_high = [(i, i ^ flip) for i in range(count) if i // flip % 2 == 1]
+    to_high = lax.ppermute(blocks[1], axis, from_low)
+    to_low = lax.ppermute(blocks[0], axis, from_high)
+    return jnp.where(bit == 0, blocks[0], blocks[1]) + to_high + to_low
 
 
 def local(voltages, coefficients, beam_weights):
@@ -97,18 +94,20 @@
     paired = jnp.concatenate([for_real, for_imag], axis=3).reshape(
         per_group, feeds_here * 2, 2 * total_frames
     )
-    weights = beam_weights.reshape(per_group, feeds_here * 2, beam_weights.shape[3])
-    beams = jnp.einsum("ckb,ckn->bcn", weights, paired, preferred_element_type=jnp.float32)
+    per_out = beam_weights.shape[3] // n_feed
+    weights = beam_weights.reshape(per_group, feeds_here * 2, n_feed, per_out)
+    beams = jnp.einsum("ckjb,ckn->jcbn", weights, paired, preferred_element_type=jnp.float32)
     flip = 1
     while flip < n_feed:
-        beams = halve(beams, "feed", flip)
+        split = beams.reshape(-1, 2, *beams.shape[1:])
+        beams = exchange((split[:, 0], split[:, 1]), "feed", flip)
         flip *= 2
-    beams = beams.reshape(beams.shape[0], per_group, 2, total_frames)
+    beams = beams.reshape(per_group, per_out, 2, total_frames)
     energy = jnp.sum(beams * beams, axis=2)
     binned = jnp.mean(
-        energy.reshape(energy.shape[0], per_group, total_frames // INTEG, INTEG), axis=3
+        energy.reshape(per_group, per_out, total_frames // INTEG, INTEG), axis=3
     )
-    return jnp.transpose(binned, (2, 1, 0))
+    return jnp.transpose(binned, (2, 0, 1))
 
 
 def solution(mesh):

time: 184 us -> 179 us (0.973)
  local copies, waits for them, and re-layouts: 37.7 us -> 28.2 us
  starting transfers between devices: 25.3 us -> 33.1 us
  waiting for transfers between devices: 84.2 us -> 82.3 us
    dynamic_slice x1 -> x0, local copies, waits for them, and re-layouts: 9.2 us -> none  [halve(): sent = lax.dynamic_index_in_dim(split, 1 - own, 1, keepdims=False)]
    ppermute x2 -> x4, starting transfers between devices: 6.69 us -> 14.5 us  [the longest x2 7.45 us: exchange(): to_high = lax.ppermute(blocks[1], axis, from_low)]
    reshape x2 -> x1, local copies, waits for them, and re-layouts: 19 us -> 14.1 us  [local(): weights = beam_weights.reshape(per_group, feeds_here * 2, n_feed, per_out)]
    reshape x0 -> x1, other arithmetic: none -> 4.29 us  [local(): split = beams.reshape(-1, 2, *beams.shape[1:])]
    squeeze x1 -> x2, local copies, waits for them, and re-layouts: 1.09 us -> 4.25 us  [local(): beams = exchange((split[:, 0], split[:, 1]), 'feed', flip)]
    add x1 -> x0, other arithmetic: 2.68 us -> none  [halve(): summed = kept + lax.ppermute(sent, axis, pairs)]
    unnamed x6 -> x10, local copies, waits for them, and re-layouts: 3.28 us -> 4.78 us
    ppermute x2 -> x4, waiting for transfers between devices: 50.8 us -> 49.9 us  [the longest x2 40.8 us: exchange(): to_high = lax.ppermute(blocks[1], axis, from_low)]
  transfers between devices with their start and end apart: 4 -> 6, of which waited for: 4 -> 6; matrix products, arithmetic and copies ran while one was open for 12% -> 13% of each run, Pallas kernels for 0% -> 0%
where the time goes in v2:
time: 179 us; the launch traced here: 178 us
  waiting for transfers between devices  82.3 us (46%)
  starting transfers between devices  33.1 us (18%)
  local copies, waits for them, and re-layouts  28.2 us (16%)
  other arithmetic  25.4 us (14%)
  matrix products  9.04 us (5%)
    ppermute x2, waiting for transfers between devices, exchange(): to_high = lax.ppermute(blocks[1], axis, from_low)  40.8 us
    all_to_all x1, waiting for transfers between devices, local(): blocks = lax.all_to_all(blocks, 'tm', 0, 0, tiled=True)  18.6 us
    reshape x1, local copies, waits for them, and re-layouts, local(): weights = beam_weights.reshape(per_group, feeds_here * 2, n_feed, per_out)  14.1 us
    all_to_all x1, waiting for transfers between devices, local(): turned = lax.all_to_all(spectra, 'tm', 0, 0, tiled=True)  13.9 us
    all_to_all x1, starting transfers between devices, local(): blocks = lax.all_to_all(blocks, 'tm', 0, 0, tiled=True)  12.6 us
    ppermute x2, waiting for transfers between devices, exchange(): to_low = lax.ppermute(blocks[0], axis, from_high)  9.06 us
    convert_element_type x1, other arithmetic, polyphase(): return running.astype(jnp.bfloat16)  8.27 us
    ppermute x2, starting transfers between devices, exchange(): to_high = lax.ppermute(blocks[1], axis, from_low)  7.45 us
  transfers between devices with their start and end apart: 6, of which 6 were waited for; matrix products, arithmetic and copies ran while one was open for 13% of the time, Pallas kernels for 0%

profile of v2, /device:TPU:1, one launch (start us, length us, event | category | flops | bytes accessed | tf_op | source)
XLA Modules:
  0.0 178.3 jit_solution(4396651604586386547)
XLA Ops:
  0.0 0.0 copy-start.4
  0.0 2.3 %reshape.351 = bf16[64,4,2048]{2,1,0:T(4,128)(2,1)} reshape(bf16[256,2048]{1,0:T(8,128)(2,1)} %param.3) | data formatting | bytes 2097152 | tf_op jit(solution)/shard_map/reshape | solution.py:68
  2.3 12.6 %all-to-all-start = ((bf16[64,4,2048]{2,1,0:T(4,128)(2,1)}), bf16[64,4,2048]{2,1,0:T(4,128)(2,1)S(1)}, u32[]{:S(2)}, u32[]{:S(2)}) async-start(bf16[64,4,2048]{2,1,0:T(4,128)(2,1)} %reshape.351), calls=%async_computation | async-start | bytes 2097152 | tf_op jit(solution)/shard_map/all_to_all | solution.py:69
  14.9 0.0 copy-done.4
  15.0 0.1 fusion.35
  15.1 1.1 negate_select_fusion.3
  16.2 2.0 %fusion.13 = (f32[2048,64]{0,1:T(8,128)S(1)}, f32[2048,64]{0,1:T(8,128)S(1)}) fusion(s32[2048]{0:T(1024)S(1)} %fusion.25), kind=kLoop, calls=%fused_computation.36 | loop fusion | flops 1835008 | bytes 1056768 | tf_op jit(solution)/shard_map/cos | solution.py:30
  18.2 6.2 %multiply_convert_fusion = bf16[2048,32,64]{0,2,1:T(8,128)(2,1)} fusion(f32[2048,64]{0,1:T(8,128)S(1)} %get-tuple-element.31, f32[2048,32]{0,1:T(8,128)S(1)} %get-tuple-element.29, f32[2048,64]{0,1:T(8,128)S(1)} %get-tuple-element.30, f32[2048,32]{0,1:T(8,128)S(1)} %get-tuple-element.28), kind=kLoop, calls=%fused_computation | loop fusion | flops 20971520 | bytes 9961472 | tf_op jit(solution)/shard_map/convert_element_type | solution.py:36
  24.4 18.6 %all-to-all-done = bf16[64,4,2048]{2,1,0:T(4,128)(2,1)S(1)} async-done(((bf16[64,4,2048]{2,1,0:T(4,128)(2,1)}), bf16[64,4,2048]{2,1,0:T(4,128)(2,1)S(1)}, u32[]{:S(2)}, u32[]{:S(2)}) %all-to-all-start) | async-done | bytes 1048608 | tf_op jit(solution)/shard_map/all_to_all | solution.py:69
  43.0 8.3 %add_convert_fusion = bf16[4,64,2048]{2,0,1:T(4,128)(2,1)S(1)} fusion(bf16[4,64,2048]{2,0,1:T(4,128)(2,1)S(1)} %bitcast.67, f32[2048]{0:T(1024)S(1)} %bitcast.84, f32[2048]{0:T(1024)S(1)} %bitcast.85, f32[2048]{0:T(1024)S(1)} %bitcast.71, f32[2048]{0:T(1024)S(1)} %bitcast.72, f32[2048]{0:T(1024)S(1)} %bitcast.73, f32[2048]{0:T(1024)S(1)} %bitcast.74, ...), kind=kLoop, calls=%fused_computation.9 | loop fusion | flops 25165824 | bytes 2228224 | tf_op jit(solution)/shard_map/convert_element_type | solution.py:46
  51.3 0.6 copy.19
  51.9 7.0 %convolution_convert_fusion = bf16[2048,256]{1,0:T(8,128)(2,1)} fusion(bf16[2048,2048]{0,1:T(8,128)(2,1)} %bitcast.65, bf16[256,2048]{1,0:T(8,128)(2,1)S(1)} %bitcast.69), kind=kOutput, calls=%fused_computation.3 | convolution fusion | flops 2148007936 | bytes 10485760 | tf_op jit(solution)/shard_map/jk,mk->jm/dot_general | solution.py:77
  58.9 6.1 %all-to-all-start.1 = ((bf16[64,32,256]{2,1,0:T(8,128)(2,1)}), bf16[64,32,256]{2,1,0:T(8,128)(2,1)S(1)}, u32[]{:S(2)}, u32[]{:S(2)}) async-start(bf16[64,32,256]{2,1,0:T(8,128)(2,1)} %bitcast.23), calls=%async_computation.1 | async-start | bytes 2097152 | tf_op jit(solution)/shard_map/all_to_all | solution.py:87
  65.0 14.1 %reshape.359 = bf16[16,512,4,128]{3,2,1,0:T(4,128)(2,1)} reshape(bf16[16,256,2,512]{3,2,1,0:T(2,128)(2,1)} %param.5) | data formatting | bytes 16777216 | tf_op jit(solution)/shard_map/reshape | solution.py:98
  79.0 13.9 %all-to-all-done.1 = bf16[64,32,256]{2,1,0:T(8,128)(2,1)S(1)} async-done(((bf16[64,32,256]{2,1,0:T(8,128)(2,1)}), bf16[64,32,256]{2,1,0:T(8,128)(2,1)S(1)}, u32[]{:S(2)}, u32[]{:S(2)}) %all-to-all-start.1) | async-done | bytes 1048608 | tf_op jit(solution)/shard_map/all_to_all | solution.py:87
  92.9 0.8 reshape.356
  93.7 0.6 copy.20
  94.3 0.0 copy-start
  94.3 0.3 slice_negate_fusion
  94.6 1.2 maximum_maximum_fusion
  95.8 1.9 %copy-done = bf16[16,512,4,128]{3,2,1,0:T(4,128)(2,1)S(1)} copy-done((bf16[16,512,4,128]{3,2,1,0:T(4,128)(2,1)S(1)}, bf16[16,512,4,128]{3,2,1,0:T(4,128)(2,1)}, u32[]{:S(2)}) %copy-start) | copy-done | bytes 8388632
  97.7 2.0 %fusion = f32[16,128,4,128]{3,1,2,0:T(8,128)S(1)} fusion(bf16[16,512,4,128]{3,2,1,0:T(4,128)(2,1)S(1)} %copy-done, bf16[16,512,128,1]{2,0,1,3:T(8,128)(2,1)S(1)} %bitcast.64), kind=kOutput, calls=%fused_computation.1 | convolution fusion | flops 1073741824 | bytes 14680064 | tf_op jit(solution)/shard_map/ckjb,ckn->jcbn/dot_general | solution.py:99
  99.8 0.0 copy-start.1
  99.8 2.8 %slice_bitcast_fusion = (f32[2,16,128,128]{2,3,0,1:T(8,128)}, f32[2,16,128,128]{2,3,0,1:T(8,128)}) fusion(f32[2,2,16,128,128]{3,4,1,0,2:T(8,128)S(1)} %bitcast.62), kind=kLoop, calls=%fused_computation.4 | loop fusion | bytes 8388608 | tf_op jit(solution)/shard_map/squeeze | solution.py:103
  102.6 0.5 copy-done.1
  103.1 1.3 collective-permute-start
  104.3 5.8 %collective-permute-start.1 = (f32[2,16,128,128]{2,3,0,1:T(8,128)}, f32[2,16,128,128]{2,3,0,1:T(8,128)}, u32[]{:S(2)}, u32[]{:S(2)}) collective-permute-start(f32[2,16,128,128]{2,3,0,1:T(8,128)} %get-tuple-element.6), channel_id=1, source_target_pairs={{1,0},{3,2},{5,4},{7,6},{9,8},{11,10},{13,12},{15,14},{17,16},{19,... | collective-permute-start | bytes 6291464 | tf_op jit(solution)/shard_map/ppermute | solution.py:55
  110.1 0.5 collective-permute-done
  110.6 0.0 copy-start.2
  110.6 1.4 copy-done.2
  111.9 1.0 collective-permute-done.1
  112.9 4.3 %add_bitcast_fusion = f32[1,2,16,128,128]{3,4,1,2,0:T(8,128)S(1)} fusion(f32[2,16,128,128]{2,3,0,1:T(8,128)} %collective-permute-done.1, f32[2,16,128,128]{2,3,0,1:T(8,128)} %copy-done.2, pred[]{:T(512)S(6)} %eq.26, f32[2,2,16,128,128]{3,4,1,0,2:T(8,128)} %bitcast.63), kind=kLoop, calls=%fused_computation.8 | loop fusion | flops 1572864 | bytes 10485761 | tf_op jit(solution)/shard_map/reshape | solution.py:102
  117.2 1.5 slice_bitcast_fusion.2
  118.7 6.2 %collective-permute-start.2 = (f32[1,16,128,128]{2,3,1,0:T(8,128)}, f32[1,16,128,128]{2,3,1,0:T(8,128)S(1)}, u32[]{:S(2)}, u32[]{:S(2)}) collective-permute-start(f32[1,16,128,128]{2,3,1,0:T(8,128)} %get-tuple-element.7), channel_id=1, source_target_pairs={{0,2},{1,3},{4,6},{5,7},{8,10},{9,11},{12,14},{13,15},{16,18},{17,... | collective-permute-start | bytes 3145736 | tf_op jit(solution)/shard_map/ppermute | solution.py:54
  124.8 1.3 collective-permute-start.3
  126.2 40.3 %collective-permute-done.2 = f32[1,16,128,128]{2,3,1,0:T(8,128)S(1)} collective-permute-done((f32[1,16,128,128]{2,3,1,0:T(8,128)}, f32[1,16,128,128]{2,3,1,0:T(8,128)S(1)}, u32[]{:S(2)}, u32[]{:S(2)}) %collective-permute-start.2) | collective-permute-done | bytes 1048608 | tf_op jit(solution)/shard_map/ppermute | solution.py:54
  166.5 0.0 copy-start.3
  166.5 1.0 copy-done.3
  167.5 8.1 %collective-permute-done.3 = f32[1,16,128,128]{2,3,1,0:T(8,128)} collective-permute-done((f32[1,16,128,128]{2,3,1,0:T(8,128)}, f32[1,16,128,128]{2,3,1,0:T(8,128)}, u32[]{:S(2)}, u32[]{:S(2)}) %collective-permute-start.3) | collective-permute-done | bytes 1048608 | tf_op jit(solution)/shard_map/ppermute | solution.py:55
  175.6 1.8 %add_multiply_fusion = f32[1,16,128,128]{2,3,1,0:T(8,128)S(1)} fusion(f32[1,16,128,128]{2,3,1,0:T(8,128)} %collective-permute-done.3, f32[1,16,128,128]{2,3,1,0:T(8,128)} %copy-done.3, pred[]{:T(512)S(6)} %eq.25, f32[1,2,16,128,128]{3,4,1,2,0:T(8,128)S(1)} %add_bitcast_fusion), kind=kLoop, calls=%fused_computation.12 | loop fusion | flops 1048576 | bytes 5242881 | tf_op jit(solution)/shard_map/mul | solution.py:106
  177.4 0.1 reduce_sum.18
  177.5 0.1 bitcast_reduce_fusion
  177.7 0.6 copy.25
  (4 shorter events, 0.0 us)
Async XLA Ops:
  0.0 14.9 %copy-start.4 = (f32[16,2048]{1,0:T(8,128)S(1)}, f32[16,2048]{1,0:T(8,128)}, u32[]{:S(2)}) copy-start(f32[16,2048]{1,0:T(8,128)} %param.4) | copy-start | bytes 393220
  2.3 40.7 %all-to-all-start = ((bf16[64,4,2048]{2,1,0:T(4,128)(2,1)}), bf16[64,4,2048]{2,1,0:T(4,128)(2,1)S(1)}, u32[]{:S(2)}, u32[]{:S(2)}) async-start(bf16[64,4,2048]{2,1,0:T(4,128)(2,1)} %reshape.351), calls=%async_computation | async-start | bytes 2097152 | tf_op jit(solution)/shard_map/all_to_all | solution.py:69
  58.9 34.0 %all-to-all-start.1 = ((bf16[64,32,256]{2,1,0:T(8,128)(2,1)}), bf16[64,32,256]{2,1,0:T(8,128)(2,1)S(1)}, u32[]{:S(2)}, u32[]{:S(2)}) async-start(bf16[64,32,256]{2,1,0:T(8,128)(2,1)} %bitcast.23), calls=%async_computation.1 | async-start | bytes 2097152 | tf_op jit(solution)/shard_map/all_to_all | solution.py:87
  94.3 3.4 %copy-start = (bf16[16,512,4,128]{3,2,1,0:T(4,128)(2,1)S(1)}, bf16[16,512,4,128]{3,2,1,0:T(4,128)(2,1)}, u32[]{:S(2)}) copy-start(bf16[16,512,4,128]{3,2,1,0:T(4,128)(2,1)} %reshape.359) | copy-start | bytes 25165828
  99.8 3.3 %copy-start.1 = (f32[16,128,4,128]{3,1,2,0:T(8,128)}, f32[16,128,4,128]{3,1,2,0:T(8,128)S(1)}, u32[]{:S(2)}) copy-start(f32[16,128,4,128]{3,1,2,0:T(8,128)S(1)} %fusion) | copy-start | bytes 12582916
  103.1 7.5 %collective-permute-start = (f32[2,16,128,128]{2,3,0,1:T(8,128)}, f32[2,16,128,128]{2,3,0,1:T(8,128)S(1)}, u32[]{:S(2)}, u32[]{:S(2)}) collective-permute-start(f32[2,16,128,128]{2,3,0,1:T(8,128)} %get-tuple-element.5), channel_id=1, source_target_pairs={{0,1},{2,3},{4,5},{6,7},{8,9},{10,11},{12,13},{14,15},{16,17},{18,... | collective-permute-start | bytes 6291464 | tf_op jit(solution)/shard_map/ppermute | solution.py:54
  104.3 8.6 %collective-permute-start.1 = (f32[2,16,128,128]{2,3,0,1:T(8,128)}, f32[2,16,128,128]{2,3,0,1:T(8,128)}, u32[]{:S(2)}, u32[]{:S(2)}) collective-permute-start(f32[2,16,128,128]{2,3,0,1:T(8,128)} %get-tuple-element.6), channel_id=1, source_target_pairs={{1,0},{3,2},{5,4},{7,6},{9,8},{11,10},{13,12},{15,14},{17,16},{19,... | collective-permute-start | bytes 6291464 | tf_op jit(solution)/shard_map/ppermute | solution.py:55
  110.6 1.4 copy-start.2
  118.7 47.9 %collective-permute-start.2 = (f32[1,16,128,128]{2,3,1,0:T(8,128)}, f32[1,16,128,128]{2,3,1,0:T(8,128)S(1)}, u32[]{:S(2)}, u32[]{:S(2)}) collective-permute-start(f32[1,16,128,128]{2,3,1,0:T(8,128)} %get-tuple-element.7), channel_id=1, source_target_pairs={{0,2},{1,3},{4,6},{5,7},{8,10},{9,11},{12,14},{13,15},{16,18},{17,... | collective-permute-start | bytes 3145736 | tf_op jit(solution)/shard_map/ppermute | solution.py:54
  124.8 50.8 %collective-permute-start.3 = (f32[1,16,128,128]{2,3,1,0:T(8,128)}, f32[1,16,128,128]{2,3,1,0:T(8,128)}, u32[]{:S(2)}, u32[]{:S(2)}) collective-permute-start(f32[1,16,128,128]{2,3,1,0:T(8,128)} %get-tuple-element.8), channel_id=1, source_target_pairs={{2,0},{3,1},{6,4},{7,5},{10,8},{11,9},{14,12},{15,13},{18,16},{19,... | collective-permute-start | bytes 3145736 | tf_op jit(solution)/shard_map/ppermute | solution.py:55
  166.5 1.0 copy-start.3

commit v3 on v2

--- a/solution.py
+++ b/solution.py
@@ -48,12 +48,10 @@
 
 def exchange(blocks, axis, flip):
     count = lax.axis_size(axis)
-    bit = lax.axis_index(axis) // flip % 2
-    from_low = [(i, i ^ flip) for i in range(count) if i // flip % 2 == 0]
-    from_high = [(i, i ^ flip) for i in range(count) if i // flip % 2 == 1]
-    to_high = lax.ppermute(blocks[1], axis, from_low)
-    to_low = lax.ppermute(blocks[0], axis, from_high)
-    return jnp.where(bit == 0, blocks[0], blocks[1]) + to_high + to_low
+    low = lax.axis_index(axis) // flip % 2 == 0
+    pairs = [(i, i ^ flip) for i in range(count)]
+    received = lax.ppermute(jnp.where(low, blocks[1], blocks[0]), axis, pairs)
+    return jnp.where(low, blocks[0], blocks[1]) + received
 
 
 def local(voltages, coefficients, beam_weights):

time: 179 us -> 164 us (0.916)
  starting transfers between devices: 33.1 us -> 25.3 us
  local copies, waits for them, and re-layouts: 28.2 us -> 22.7 us
  other arithmetic: 25.4 us -> 23.3 us
    ppermute x4 -> x2, starting transfers between devices: 14.5 us -> 6.69 us  [exchange(): received = lax.ppermute(jnp.where(low, blocks[1], blocks[0]), axis, pairs)]
    squeeze x2 -> x0, local copies, waits for them, and re-layouts: 4.25 us -> none  [local(): beams = exchange((split[:, 0], split[:, 1]), 'feed', flip)]
    unnamed x10 -> x6, local copies, waits for them, and re-layouts: 4.78 us -> 3.61 us
    ppermute x4 -> x2, waiting for transfers between devices: 49.9 us -> 50.6 us  [exchange(): received = lax.ppermute(jnp.where(low, blocks[1], blocks[0]), axis, pairs)]
  transfers between devices with their start and end apart: 6 -> 4, of which waited for: 6 -> 4; matrix products, arithmetic and copies ran while one was open for 13% -> 14% of each run, Pallas kernels for 0% -> 0%
where the time goes in v3:
time: 164 us
  waiting for transfers between devices  83.1 us (51%)
  starting transfers between devices  25.3 us (15%)
  other arithmetic  23.3 us (14%)
  local copies, waits for them, and re-layouts  22.7 us (14%)
  matrix products  9.01 us (5%)
    ppermute x2, waiting for transfers between devices, exchange(): received = lax.ppermute(jnp.where(low, blocks[1], blocks[0]), axis, pairs)  50.6 us
    all_to_all x1, waiting for transfers between devices, local(): blocks = lax.all_to_all(blocks, 'tm', 0, 0, tiled=True)  18.6 us
    reshape x1, local copies, waits for them, and re-layouts, local(): weights = beam_weights.reshape(per_group, feeds_here * 2, n_feed, per_out)  14 us
    all_to_all x1, waiting for transfers between devices, local(): turned = lax.all_to_all(spectra, 'tm', 0, 0, tiled=True)  13.9 us
    all_to_all x1, starting transfers between devices, local(): blocks = lax.all_to_all(blocks, 'tm', 0, 0, tiled=True)  12.6 us
    convert_element_type x1, other arithmetic, polyphase(): return running.astype(jnp.bfloat16)  8.27 us
    dot_general x1, matrix products, local(): jnp.einsum('jk,mk->jm', table, filtered.reshape(per_dev * total_frames, f...  6.97 us
    ppermute x2, starting transfers between devices, exchange(): received = lax.ppermute(jnp.where(low, blocks[1], blocks[0]), axis, pairs)  6.69 us
  transfers between devices with their start and end apart: 4, of which 4 were waited for; matrix products, arithmetic and copies ran while one was open for 14% of the time, Pallas kernels for 0%

profile of v3, /device:TPU:1, one launch (start us, length us, event | category | flops | bytes accessed | tf_op | source)
XLA Modules:
  0.0 163.6 jit_solution(5243266005186742420)
XLA Ops:
  0.0 0.0 copy-start.2
  0.0 2.3 %reshape.379 = bf16[64,4,2048]{2,1,0:T(4,128)(2,1)} reshape(bf16[256,2048]{1,0:T(8,128)(2,1)} %param.3) | data formatting | bytes 2097152 | tf_op jit(solution)/shard_map/reshape | solution.py:66
  2.3 12.6 %all-to-all-start = ((bf16[64,4,2048]{2,1,0:T(4,128)(2,1)}), bf16[64,4,2048]{2,1,0:T(4,128)(2,1)S(1)}, u32[]{:S(2)}, u32[]{:S(2)}) async-start(bf16[64,4,2048]{2,1,0:T(4,128)(2,1)} %reshape.379), calls=%async_computation | async-start | bytes 2097152 | tf_op jit(solution)/shard_map/all_to_all | solution.py:67
  14.9 0.0 copy-done.2
  14.9 0.1 fusion.41
  15.0 1.1 negate_select_fusion.3
  16.2 2.0 %fusion.19 = (f32[2048,64]{0,1:T(8,128)S(1)}, f32[2048,64]{0,1:T(8,128)S(1)}) fusion(s32[2048]{0:T(1024)S(1)} %fusion.31), kind=kLoop, calls=%fused_computation.40 | loop fusion | flops 1835008 | bytes 1056768 | tf_op jit(solution)/shard_map/cos | solution.py:30
  18.2 6.2 %multiply_convert_fusion = bf16[2048,32,64]{0,2,1:T(8,128)(2,1)} fusion(f32[2048,64]{0,1:T(8,128)S(1)} %get-tuple-element.27, f32[2048,32]{0,1:T(8,128)S(1)} %get-tuple-element.25, f32[2048,64]{0,1:T(8,128)S(1)} %get-tuple-element.26, f32[2048,32]{0,1:T(8,128)S(1)} %get-tuple-element.24), kind=kLoop, calls=%fused_computation | loop fusion | flops 20971520 | bytes 9961472 | tf_op jit(solution)/shard_map/convert_element_type | solution.py:36
  24.4 18.6 %all-to-all-done = bf16[64,4,2048]{2,1,0:T(4,128)(2,1)S(1)} async-done(((bf16[64,4,2048]{2,1,0:T(4,128)(2,1)}), bf16[64,4,2048]{2,1,0:T(4,128)(2,1)S(1)}, u32[]{:S(2)}, u32[]{:S(2)}) %all-to-all-start) | async-done | bytes 1048608 | tf_op jit(solution)/shard_map/all_to_all | solution.py:67
  43.0 8.3 %add_convert_fusion = bf16[4,64,2048]{2,0,1:T(4,128)(2,1)S(1)} fusion(bf16[4,64,2048]{2,0,1:T(4,128)(2,1)S(1)} %bitcast.92, f32[2048]{0:T(1024)S(1)} %bitcast.108, f32[2048]{0:T(1024)S(1)} %bitcast.109, f32[2048]{0:T(1024)S(1)} %bitcast.95, f32[2048]{0:T(1024)S(1)} %bitcast.96, f32[2048]{0:T(1024)S(1)} %bitcast.97, f32[2048]{0:T(1024)S(1)} %bitcast.98, ...), kind=kLoop, calls=%fused_computation.11 | loop fusion | flops 25165824 | bytes 2228224 | tf_op jit(solution)/shard_map/convert_element_type | solution.py:46
  51.3 0.6 copy.37
  51.8 7.0 %convolution_convert_fusion = bf16[2048,256]{1,0:T(8,128)(2,1)} fusion(bf16[2048,2048]{0,1:T(8,128)(2,1)} %bitcast.89, bf16[256,2048]{1,0:T(8,128)(2,1)S(1)} %bitcast.93), kind=kOutput, calls=%fused_computation.3 | convolution fusion | flops 2148007936 | bytes 10485760 | tf_op jit(solution)/shard_map/jk,mk->jm/dot_general | solution.py:75
  58.8 6.1 %all-to-all-start.1 = ((bf16[64,32,256]{2,1,0:T(8,128)(2,1)}), bf16[64,32,256]{2,1,0:T(8,128)(2,1)S(1)}, u32[]{:S(2)}, u32[]{:S(2)}) async-start(bf16[64,32,256]{2,1,0:T(8,128)(2,1)} %bitcast.23), calls=%async_computation.1 | async-start | bytes 2097152 | tf_op jit(solution)/shard_map/all_to_all | solution.py:85
  64.9 14.0 %reshape.387 = bf16[16,512,4,128]{3,2,1,0:T(4,128)(2,1)} reshape(bf16[16,256,2,512]{3,2,1,0:T(2,128)(2,1)} %param.5) | data formatting | bytes 16777216 | tf_op jit(solution)/shard_map/reshape | solution.py:96
  79.0 13.9 %all-to-all-done.1 = bf16[64,32,256]{2,1,0:T(8,128)(2,1)S(1)} async-done(((bf16[64,32,256]{2,1,0:T(8,128)(2,1)}), bf16[64,32,256]{2,1,0:T(8,128)(2,1)S(1)}, u32[]{:S(2)}, u32[]{:S(2)}) %all-to-all-start.1) | async-done | bytes 1048608 | tf_op jit(solution)/shard_map/all_to_all | solution.py:85
  92.8 0.8 reshape.384
  93.7 0.6 copy.38
  94.3 0.0 copy-start
  94.3 0.3 slice_negate_fusion
  94.6 1.2 maximum_maximum_fusion
  95.7 1.9 %copy-done = bf16[16,512,4,128]{3,2,1,0:T(4,128)(2,1)S(1)} copy-done((bf16[16,512,4,128]{3,2,1,0:T(4,128)(2,1)S(1)}, bf16[16,512,4,128]{3,2,1,0:T(4,128)(2,1)}, u32[]{:S(2)}) %copy-start) | copy-done | bytes 8388632
  97.7 2.0 %fusion = f32[16,128,4,128]{3,1,2,0:T(8,128)S(1)} fusion(bf16[16,512,4,128]{3,2,1,0:T(4,128)(2,1)S(1)} %copy-done, bf16[16,512,128,1]{2,0,1,3:T(8,128)(2,1)S(1)} %bitcast.88), kind=kOutput, calls=%fused_computation.1 | convolution fusion | flops 1073741824 | bytes 14680064 | tf_op jit(solution)/shard_map/ckjb,ckn->jcbn/dot_general | solution.py:97
  99.7 0.0 copy-start.1
  99.7 0.3 select_bitcast_fusion
  100.0 1.7 %copy-done.1 = f32[16,128,4,128]{3,1,2,0:T(8,128)} copy-done((f32[16,128,4,128]{3,1,2,0:T(8,128)}, f32[16,128,4,128]{3,1,2,0:T(8,128)S(1)}, u32[]{:S(2)}) %copy-start.1) | copy-done | bytes 4194328
  101.7 2.4 %collective-permute-start = (f32[2,16,128,128]{2,3,0,1:T(8,128)S(1)}, f32[2,16,128,128]{2,3,0,1:T(8,128)}, u32[]{:S(2)}, u32[]{:S(2)}) collective-permute-start(f32[2,16,128,128]{2,3,0,1:T(8,128)S(1)} %select_bitcast_fusion), channel_id=1, source_target_pairs={{0,1},{1,0},{2,3},{3,2},{4,5},{5,4},{6,7},{7,6},{8,9},{9,8},{10,11... | collective-permute-start | bytes 6291464 | tf_op jit(solution)/shard_map/ppermute | solution.py:53
  104.1 3.9 %collective-permute-done = f32[2,16,128,128]{2,3,0,1:T(8,128)} collective-permute-done((f32[2,16,128,128]{2,3,0,1:T(8,128)S(1)}, f32[2,16,128,128]{2,3,0,1:T(8,128)}, u32[]{:S(2)}, u32[]{:S(2)}) %collective-permute-start) | collective-permute-done | bytes 2097184 | tf_op jit(solution)/shard_map/ppermute | solution.py:53
  108.0 3.4 %fusion.4 = f32[1,2,16,128,128]{3,4,1,2,0:T(8,128)S(1)} fusion(f32[2,16,128,128]{2,3,0,1:T(8,128)} %collective-permute-done, f32[2,2,16,128,128]{3,4,1,0,2:T(8,128)} %bitcast.87, pred[]{:T(512)S(6)} %eq.26), kind=kLoop, calls=%fused_computation.8 | loop fusion | flops 1048576 | bytes 8388609 | tf_op jit(solution)/shard_map/reshape | solution.py:100
  111.4 0.1 select_bitcast_fusion.1
  111.5 4.3 %collective-permute-start.1 = (f32[1,16,128,128]{2,3,1,0:T(8,128)S(1)}, f32[1,16,128,128]{2,3,1,0:T(8,128)S(1)}, u32[]{:S(2)}, u32[]{:S(2)}) collective-permute-start(f32[1,16,128,128]{2,3,1,0:T(8,128)S(1)} %select_bitcast_fusion.1), channel_id=1, source_target_pairs={{0,2},{1,3},{2,0},{3,1},{4,6},{5,7},{6,4},{7,5},{8,10},{9,11},{10,... | collective-permute-start | bytes 3145736 | tf_op jit(solution)/shard_map/ppermute | solution.py:53
  115.8 46.7 %collective-permute-done.1 = f32[1,16,128,128]{2,3,1,0:T(8,128)S(1)} collective-permute-done((f32[1,16,128,128]{2,3,1,0:T(8,128)S(1)}, f32[1,16,128,128]{2,3,1,0:T(8,128)S(1)}, u32[]{:S(2)}, u32[]{:S(2)}) %collective-permute-start.1) | collective-permute-done | bytes 1048608 | tf_op jit(solution)/shard_map/ppermute | solution.py:53
  162.5 0.2 fusion.8
  162.7 0.1 reduce_sum.18
  162.8 0.1 bitcast_reduce_fusion
  163.0 0.6 copy.49
  (4 shorter events, 0.0 us)
Async XLA Ops:
  0.0 14.9 %copy-start.2 = (f32[16,2048]{1,0:T(8,128)S(1)}, f32[16,2048]{1,0:T(8,128)}, u32[]{:S(2)}) copy-start(f32[16,2048]{1,0:T(8,128)} %param.4) | copy-start | bytes 393220
  2.3 40.7 %all-to-all-start = ((bf16[64,4,2048]{2,1,0:T(4,128)(2,1)}), bf16[64,4,2048]{2,1,0:T(4,128)(2,1)S(1)}, u32[]{:S(2)}, u32[]{:S(2)}) async-start(bf16[64,4,2048]{2,1,0:T(4,128)(2,1)} %reshape.379), calls=%async_computation | async-start | bytes 2097152 | tf_op jit(solution)/shard_map/all_to_all | solution.py:67
  58.8 34.0 %all-to-all-start.1 = ((bf16[64,32,256]{2,1,0:T(8,128)(2,1)}), bf16[64,32,256]{2,1,0:T(8,128)(2,1)S(1)}, u32[]{:S(2)}, u32[]{:S(2)}) async-start(bf16[64,32,256]{2,1,0:T(8,128)(2,1)} %bitcast.23), calls=%async_computation.1 | async-start | bytes 2097152 | tf_op jit(solution)/shard_map/all_to_all | solution.py:85
  94.3 3.4 %copy-start = (bf16[16,512,4,128]{3,2,1,0:T(4,128)(2,1)S(1)}, bf16[16,512,4,128]{3,2,1,0:T(4,128)(2,1)}, u32[]{:S(2)}) copy-start(bf16[16,512,4,128]{3,2,1,0:T(4,128)(2,1)} %reshape.387) | copy-start | bytes 25165828
  99.7 1.9 %copy-start.1 = (f32[16,128,4,128]{3,1,2,0:T(8,128)}, f32[16,128,4,128]{3,1,2,0:T(8,128)S(1)}, u32[]{:S(2)}) copy-start(f32[16,128,4,128]{3,1,2,0:T(8,128)S(1)} %fusion) | copy-start | bytes 12582916
  101.7 6.3 %collective-permute-start = (f32[2,16,128,128]{2,3,0,1:T(8,128)S(1)}, f32[2,16,128,128]{2,3,0,1:T(8,128)}, u32[]{:S(2)}, u32[]{:S(2)}) collective-permute-start(f32[2,16,128,128]{2,3,0,1:T(8,128)S(1)} %select_bitcast_fusion), channel_id=1, source_target_pairs={{0,1},{1,0},{2,3},{3,2},{4,5},{5,4},{6,7},{7,6},{8,9},{9,8},{10,11... | collective-permute-start | bytes 6291464 | tf_op jit(solution)/shard_map/ppermute | solution.py:53
  111.5 51.0 %collective-permute-start.1 = (f32[1,16,128,128]{2,3,1,0:T(8,128)S(1)}, f32[1,16,128,128]{2,3,1,0:T(8,128)S(1)}, u32[]{:S(2)}, u32[]{:S(2)}) collective-permute-start(f32[1,16,128,128]{2,3,1,0:T(8,128)S(1)} %select_bitcast_fusion.1), channel_id=1, source_target_pairs={{0,2},{1,3},{2,0},{3,1},{4,6},{5,7},{6,4},{7,5},{8,10},{9,11},{10,... | collective-permute-start | bytes 3145736 | tf_op jit(solution)/shard_map/ppermute | solution.py:53

commit v4 on v3

--- a/solution.py
+++ b/solution.py
@@ -94,17 +94,25 @@
     )
     per_out = beam_weights.shape[3] // n_feed
     weights = beam_weights.reshape(per_group, feeds_here * 2, n_feed, per_out)
-    beams = jnp.einsum("ckjb,ckn->jcbn", weights, paired, preferred_element_type=jnp.float32)
-    flip = 1
-    while flip < n_feed:
-        split = beams.reshape(-1, 2, *beams.shape[1:])
-        beams = exchange((split[:, 0], split[:, 1]), "feed", flip)
-        flip *= 2
-    beams = beams.reshape(per_group, per_out, 2, total_frames)
-    energy = jnp.sum(beams * beams, axis=2)
-    binned = jnp.mean(
-        energy.reshape(per_group, per_out, total_frames // INTEG, INTEG), axis=3
-    )
+    n_parts = 2
+    per_part = per_group // n_parts
+    binned_parts = []
+    for part in range(n_parts):
+        chosen = slice(part * per_part, (part + 1) * per_part)
+        beams = jnp.einsum(
+            "ckjb,ckn->jcbn", weights[chosen], paired[chosen], preferred_element_type=jnp.float32
+        )
+        flip = 1
+        while flip < n_feed:
+            split = beams.reshape(-1, 2, *beams.shape[1:])
+            beams = exchange((split[:, 0], split[:, 1]), "feed", flip)
+            flip *= 2
+        beams = beams.reshape(per_part, per_out, 2, total_frames)
+        energy = jnp.sum(beams * beams, axis=2)
+        binned_parts.append(
+            jnp.mean(energy.reshape(per_part, per_out, total_frames // INTEG, INTEG), axis=3)
+        )
+    binned = jnp.concatenate(binned_parts, axis=0)
     return jnp.transpose(binned, (2, 0, 1))
 
 

time: 164 us -> 161 us (0.982)
  waiting for transfers between devices: 83.1 us -> 67.1 us
  local copies, waits for them, and re-layouts: 22.7 us -> 31.1 us
  starting transfers between devices: 25.3 us -> 27.8 us
  other arithmetic: 23.3 us -> 25.4 us
    slice x0 -> x5, local copies, waits for them, and re-layouts: none -> 24.1 us  [the longest x3 23.6 us: local(): weights[chosen]]
    reshape x1 -> x0, local copies, waits for them, and re-layouts: 14 us -> none  [local(): weights = beam_weights.reshape(per_group, feeds_here * 2, n_feed, per_out)]
    all_to_all x1, waiting for transfers between devices: 13.9 us -> 4.25 us  [local(): turned = lax.all_to_all(spectra, 'tm', 0, 0, tiled=True)]
    ppermute x2 -> x4, waiting for transfers between devices: 50.6 us -> 44.2 us  [exchange(): received = lax.ppermute(jnp.where(low, blocks[1], blocks[0]), axis, pairs)]
    ppermute x2 -> x4, starting transfers between devices: 6.69 us -> 9.21 us  [exchange(): received = lax.ppermute(jnp.where(low, blocks[1], blocks[0]), axis, pairs)]
    unnamed x6, local copies, waits for them, and re-layouts: 3.61 us -> 1.82 us
    slice x0 -> x1, other arithmetic: none -> 1.66 us  [local(): beams = exchange((split[:, 0], split[:, 1]), 'feed', flip)]
    reshape x1 -> x2, other arithmetic: 3.38 us -> 3.08 us  [local(): split = beams.reshape(-1, 2, *beams.shape[1:])]
  transfers between devices with their start and end apart: 4 -> 6, of which waited for: 4 -> 4; matrix products, arithmetic and copies ran while one was open for 14% -> 24% of each run, Pallas kernels for 0% -> 0%
where the time goes in v4:
time: 161 us; the launch traced here: 160 us
  waiting for transfers between devices  67.1 us (42%)
  local copies, waits for them, and re-layouts  31.1 us (19%)
  starting transfers between devices  27.8 us (17%)
  other arithmetic  25.4 us (16%)
  matrix products  8.6 us (5%)
    ppermute x4, waiting for transfers between devices, exchange(): received = lax.ppermute(jnp.where(low, blocks[1], blocks[0]), axis, pairs)  44.2 us
    slice x3, local copies, waits for them, and re-layouts, local(): weights[chosen]  23.6 us
    all_to_all x1, waiting for transfers between devices, local(): blocks = lax.all_to_all(blocks, 'tm', 0, 0, tiled=True)  18.6 us
    all_to_all x1, starting transfers between devices, local(): blocks = lax.all_to_all(blocks, 'tm', 0, 0, tiled=True)  12.6 us
    ppermute x4, starting transfers between devices, exchange(): received = lax.ppermute(jnp.where(low, blocks[1], blocks[0]), axis, pairs)  9.21 us
    convert_element_type x1, other arithmetic, polyphase(): return running.astype(jnp.bfloat16)  8.27 us
    dot_general x1, matrix products, local(): jnp.einsum('jk,mk->jm', table, filtered.reshape(per_dev * total_frames, f...  6.95 us
    convert_element_type x1, other arithmetic, dft_rows(): return table.reshape(cols, frame_len).astype(jnp.bfloat16)  6.18 us
  transfers between devices with their start and end apart: 6, of which 4 were waited for; matrix products, arithmetic and copies ran while one was open for 24% of the time, Pallas kernels for 0%

profile of v4, /device:TPU:1, one launch (start us, length us, event | category | flops | bytes accessed | tf_op | source)
XLA Modules:
  0.0 160.2 jit_solution(168388019510845323)
XLA Ops:
  0.0 0.0 copy-start.2
  0.0 2.3 %reshape.438 = bf16[64,4,2048]{2,1,0:T(4,128)(2,1)} reshape(bf16[256,2048]{1,0:T(8,128)(2,1)} %param.3) | data formatting | bytes 2097152 | tf_op jit(solution)/shard_map/reshape | solution.py:66
  2.3 12.6 %all-to-all-start = ((bf16[64,4,2048]{2,1,0:T(4,128)(2,1)}), bf16[64,4,2048]{2,1,0:T(4,128)(2,1)S(1)}, u32[]{:S(2)}, u32[]{:S(2)}) async-start(bf16[64,4,2048]{2,1,0:T(4,128)(2,1)} %reshape.438), calls=%async_computation | async-start | bytes 2097152 | tf_op jit(solution)/shard_map/all_to_all | solution.py:67
  14.9 0.0 copy-done.2
  14.9 0.1 fusion.49
  15.0 1.1 negate_select_fusion.3
  16.2 2.0 %fusion.23 = (f32[2048,64]{0,1:T(8,128)S(1)}, f32[2048,64]{0,1:T(8,128)S(1)}) fusion(s32[2048]{0:T(1024)S(1)} %fusion.35), kind=kLoop, calls=%fused_computation.50 | loop fusion | flops 1835008 | bytes 1056768 | tf_op jit(solution)/shard_map/cos | solution.py:30
  18.2 6.2 %multiply_convert_fusion = bf16[2048,32,64]{0,2,1:T(8,128)(2,1)} fusion(f32[2048,64]{0,1:T(8,128)S(1)} %get-tuple-element.36, f32[2048,32]{0,1:T(8,128)S(1)} %get-tuple-element.34, f32[2048,64]{0,1:T(8,128)S(1)} %get-tuple-element.35, f32[2048,32]{0,1:T(8,128)S(1)} %get-tuple-element.33), kind=kLoop, calls=%fused_computation | loop fusion | flops 20971520 | bytes 9961472 | tf_op jit(solution)/shard_map/convert_element_type | solution.py:36
  24.4 18.6 %all-to-all-done = bf16[64,4,2048]{2,1,0:T(4,128)(2,1)S(1)} async-done(((bf16[64,4,2048]{2,1,0:T(4,128)(2,1)}), bf16[64,4,2048]{2,1,0:T(4,128)(2,1)S(1)}, u32[]{:S(2)}, u32[]{:S(2)}) %all-to-all-start) | async-done | bytes 1048608 | tf_op jit(solution)/shard_map/all_to_all | solution.py:67
  43.0 8.3 %add_convert_fusion = bf16[4,64,2048]{2,0,1:T(4,128)(2,1)S(1)} fusion(bf16[4,64,2048]{2,0,1:T(4,128)(2,1)S(1)} %bitcast.96, f32[2048]{0:T(1024)S(1)} %bitcast.116, f32[2048]{0:T(1024)S(1)} %bitcast.117, f32[2048]{0:T(1024)S(1)} %bitcast.103, f32[2048]{0:T(1024)S(1)} %bitcast.104, f32[2048]{0:T(1024)S(1)} %bitcast.105, f32[2048]{0:T(1024)S(1)} %bitcast.106, ...), kind=kLoop, calls=%fused_computation.7 | loop fusion | flops 25165824 | bytes 2228224 | tf_op jit(solution)/shard_map/convert_element_type | solution.py:46
  51.3 0.6 copy.53
  51.9 7.0 %convolution_convert_fusion = bf16[2048,256]{1,0:T(8,128)(2,1)} fusion(bf16[2048,2048]{0,1:T(8,128)(2,1)} %bitcast.94, bf16[256,2048]{1,0:T(8,128)(2,1)S(1)} %bitcast.101), kind=kOutput, calls=%fused_computation.5 | convolution fusion | flops 2148007936 | bytes 10485760 | tf_op jit(solution)/shard_map/jk,mk->jm/dot_general | solution.py:75
  58.8 6.1 %all-to-all-start.1 = ((bf16[64,32,256]{2,1,0:T(8,128)(2,1)}), bf16[64,32,256]{2,1,0:T(8,128)(2,1)S(1)}, u32[]{:S(2)}, u32[]{:S(2)}) async-start(bf16[64,32,256]{2,1,0:T(8,128)(2,1)} %bitcast.23), calls=%async_computation.1 | async-start | bytes 2097152 | tf_op jit(solution)/shard_map/all_to_all | solution.py:85
  64.9 8.4 %fusion.45 = (bf16[8,256,2,512]{3,2,1,0:T(2,128)(2,1)}, bf16[8,256,2,512]{3,2,1,0:T(2,128)(2,1)}) fusion(bf16[16,256,2,512]{3,2,1,0:T(2,128)(2,1)} %param.5), kind=kLoop, calls=%fused_computation.88 | loop fusion | bytes 16777216 | tf_op jit(solution)/shard_map/slice | solution.py:103
  73.3 7.7 %reshape.453 = bf16[8,512,4,128]{3,2,1,0:T(4,128)(2,1)} reshape(bf16[8,256,2,512]{3,2,1,0:T(2,128)(2,1)} %get-tuple-element.5) | data formatting | bytes 8388608 | tf_op jit(solution)/shard_map/slice | solution.py:103
  81.0 7.6 %reshape.454 = bf16[8,512,4,128]{3,2,1,0:T(4,128)(2,1)} reshape(bf16[8,256,2,512]{3,2,1,0:T(2,128)(2,1)} %get-tuple-element.6) | data formatting | bytes 8388608 | tf_op jit(solution)/shard_map/slice | solution.py:103
  88.6 4.3 %all-to-all-done.1 = bf16[64,32,256]{2,1,0:T(8,128)(2,1)S(1)} async-done(((bf16[64,32,256]{2,1,0:T(8,128)(2,1)}), bf16[64,32,256]{2,1,0:T(8,128)(2,1)S(1)}, u32[]{:S(2)}, u32[]{:S(2)}) %all-to-all-start.1) | async-done | bytes 1048608 | tf_op jit(solution)/shard_map/all_to_all | solution.py:85
  92.8 0.8 reshape.443
  93.7 0.6 copy.54
  94.3 0.3 slice_negate_fusion
  94.6 1.2 maximum_maximum_fusion
  95.7 0.0 copy-start.1
  95.7 0.4 fusion.47
  96.1 1.8 %copy-done.1 = bf16[8,512,4,128]{3,2,1,0:T(4,128)(2,1)S(1)} copy-done((bf16[8,512,4,128]{3,2,1,0:T(4,128)(2,1)S(1)}, bf16[8,512,4,128]{3,2,1,0:T(4,128)(2,1)}, u32[]{:S(2)}) %copy-start.1) | copy-done | bytes 4194328
  97.9 0.8 fusion.2
  98.8 0.0 copy-start
  98.8 1.7 %fusion.46 = (f32[2,1,8,128,128]{3,4,1,0,2:T(8,128)S(1)}, f32[2,8,128,128]{2,3,0,1:T(8,128)}, f32[2,1,8,128,128]{3,4,1,0,2:T(8,128)}) fusion(f32[2,2,8,128,128]{3,4,1,0,2:T(8,128)S(1)} %bitcast.92, pred[]{:T(512)S(6)} %eq.30), kind=kLoop, calls=%fused_computation.89 | loop fusion | flops 262144 | bytes 5242881 | tf_op jit(solution)/shard_map/slice | solution.py:108
  100.4 2.4 %collective-permute-start = (f32[2,8,128,128]{2,3,0,1:T(8,128)}, f32[2,8,128,128]{2,3,0,1:T(8,128)}, u32[]{:S(2)}, u32[]{:S(2)}) collective-permute-start(f32[2,8,128,128]{2,3,0,1:T(8,128)} %get-tuple-element.8), channel_id=1, source_target_pairs={{0,1},{1,0},{2,3},{3,2},{4,5},{5,4},{6,7},{7,6},{8,9},{9,8},{10,11... | collective-permute-start | bytes 3145736 | tf_op jit(solution)/shard_map/ppermute | solution.py:53
  102.8 0.0 copy-done
  102.8 0.8 fusion
  103.7 0.1 fusion.48
  103.8 1.1 select_bitcast_fusion
  104.9 1.3 collective-permute-start.2
  106.2 0.0 collective-permute-done
  106.2 1.7 %fusion.8 = f32[1,2,8,128,128]{3,4,1,2,0:T(8,128)S(1)} fusion(f32[2,8,128,128]{2,3,0,1:T(8,128)} %collective-permute-done, f32[2,1,8,128,128]{3,4,1,0,2:T(8,128)} %get-tuple-element.9, f32[2,1,8,128,128]{3,4,1,0,2:T(8,128)S(1)} %get-tuple-element.7, pred[]{:T(512)S(6)} %eq.30), kind=kLoop, calls=%fused_computation.15 | loop fusion | flops 524288 | bytes 4194305 | tf_op jit(solution)/shard_map/reshape | solution.py:107
  107.9 0.1 select_bitcast_fusion.3
  107.9 4.3 %collective-permute-start.1 = (f32[1,8,128,128]{2,3,1,0:T(8,128)S(1)}, f32[1,8,128,128]{2,3,1,0:T(8,128)S(1)}, u32[]{:S(2)}, u32[]{:S(2)}) collective-permute-start(f32[1,8,128,128]{2,3,1,0:T(8,128)S(1)} %select_bitcast_fusion.3), channel_id=1, source_target_pairs={{0,2},{1,3},{2,0},{3,1},{4,6},{5,7},{6,4},{7,5},{8,10},{9,11},{10,... | collective-permute-start | bytes 1572872 | tf_op jit(solution)/shard_map/ppermute | solution.py:53
  112.2 0.0 collective-permute-done.2
  112.2 1.4 fusion.5
  113.6 0.1 select_bitcast_fusion.2
  113.7 1.2 collective-permute-start.3
  114.9 27.4 %collective-permute-done.1 = f32[1,8,128,128]{2,3,1,0:T(8,128)S(1)} collective-permute-done((f32[1,8,128,128]{2,3,1,0:T(8,128)S(1)}, f32[1,8,128,128]{2,3,1,0:T(8,128)S(1)}, u32[]{:S(2)}, u32[]{:S(2)}) %collective-permute-start.1) | collective-permute-done | bytes 524320 | tf_op jit(solution)/shard_map/ppermute | solution.py:53
  142.3 0.1 fusion.14
  142.5 0.1 bitcast_reduce_fusion.1
  142.5 16.8 %collective-permute-done.3 = f32[1,8,128,128]{2,3,1,0:T(8,128)S(1)} collective-permute-done((f32[1,8,128,128]{2,3,1,0:T(8,128)S(1)}, f32[1,8,128,128]{2,3,1,0:T(8,128)S(1)}, u32[]{:S(2)}, u32[]{:S(2)}) %collective-permute-start.3) | collective-permute-done | bytes 524320 | tf_op jit(solution)/shard_map/ppermute | solution.py:53
  159.4 0.1 fusion.15
  159.5 0.1 bitcast_reduce_fusion
  159.6 0.6 copy.72
  (7 shorter events, 0.1 us)
Async XLA Ops:
  0.0 14.9 %copy-start.2 = (f32[16,2048]{1,0:T(8,128)S(1)}, f32[16,2048]{1,0:T(8,128)}, u32[]{:S(2)}) copy-start(f32[16,2048]{1,0:T(8,128)} %param.4) | copy-start | bytes 393220
  2.3 40.7 %all-to-all-start = ((bf16[64,4,2048]{2,1,0:T(4,128)(2,1)}), bf16[64,4,2048]{2,1,0:T(4,128)(2,1)S(1)}, u32[]{:S(2)}, u32[]{:S(2)}) async-start(bf16[64,4,2048]{2,1,0:T(4,128)(2,1)} %reshape.438), calls=%async_computation | async-start | bytes 2097152 | tf_op jit(solution)/shard_map/all_to_all | solution.py:67
  58.8 34.0 %all-to-all-start.1 = ((bf16[64,32,256]{2,1,0:T(8,128)(2,1)}), bf16[64,32,256]{2,1,0:T(8,128)(2,1)S(1)}, u32[]{:S(2)}, u32[]{:S(2)}) async-start(bf16[64,32,256]{2,1,0:T(8,128)(2,1)} %bitcast.23), calls=%async_computation.1 | async-start | bytes 2097152 | tf_op jit(solution)/shard_map/all_to_all | solution.py:85
  95.7 2.2 %copy-start.1 = (bf16[8,512,4,128]{3,2,1,0:T(4,128)(2,1)S(1)}, bf16[8,512,4,128]{3,2,1,0:T(4,128)(2,1)}, u32[]{:S(2)}) copy-start(bf16[8,512,4,128]{3,2,1,0:T(4,128)(2,1)} %reshape.453) | copy-start | bytes 12582916
  98.8 4.1 %copy-start = (bf16[8,512,4,128]{3,2,1,0:T(4,128)(2,1)S(1)}, bf16[8,512,4,128]{3,2,1,0:T(4,128)(2,1)}, u32[]{:S(2)}) copy-start(bf16[8,512,4,128]{3,2,1,0:T(4,128)(2,1)} %reshape.454) | copy-start | bytes 12582916
  100.4 5.7 %collective-permute-start = (f32[2,8,128,128]{2,3,0,1:T(8,128)}, f32[2,8,128,128]{2,3,0,1:T(8,128)}, u32[]{:S(2)}, u32[]{:S(2)}) collective-permute-start(f32[2,8,128,128]{2,3,0,1:T(8,128)} %get-tuple-element.8), channel_id=1, source_target_pairs={{0,1},{1,0},{2,3},{3,2},{4,5},{5,4},{6,7},{7,6},{8,9},{9,8},{10,11... | collective-permute-start | bytes 3145736 | tf_op jit(solution)/shard_map/ppermute | solution.py:53
  104.9 7.3 %collective-permute-start.2 = (f32[2,8,128,128]{2,3,1,0:T(8,128)}, f32[2,8,128,128]{2,3,1,0:T(8,128)}, u32[]{:S(2)}, u32[]{:S(2)}) collective-permute-start(f32[2,8,128,128]{2,3,1,0:T(8,128)} %select_bitcast_fusion), channel_id=1, source_target_pairs={{0,1},{1,0},{2,3},{3,2},{4,5},{5,4},{6,7},{7,6},{8,9},{9,8},{10,11... | collective-permute-start | bytes 3145736 | tf_op jit(solution)/shard_map/ppermute | solution.py:53
  107.9 34.4 %collective-permute-start.1 = (f32[1,8,128,128]{2,3,1,0:T(8,128)S(1)}, f32[1,8,128,128]{2,3,1,0:T(8,128)S(1)}, u32[]{:S(2)}, u32[]{:S(2)}) collective-permute-start(f32[1,8,128,128]{2,3,1,0:T(8,128)S(1)} %select_bitcast_fusion.3), channel_id=1, source_target_pairs={{0,2},{1,3},{2,0},{3,1},{4,6},{5,7},{6,4},{7,5},{8,10},{9,11},{10,... | collective-permute-start | bytes 1572872 | tf_op jit(solution)/shard_map/ppermute | solution.py:53
  113.7 45.7 %collective-permute-start.3 = (f32[1,8,128,128]{2,3,1,0:T(8,128)S(1)}, f32[1,8,128,128]{2,3,1,0:T(8,128)S(1)}, u32[]{:S(2)}, u32[]{:S(2)}) collective-permute-start(f32[1,8,128,128]{2,3,1,0:T(8,128)S(1)} %select_bitcast_fusion.2), channel_id=1, source_target_pairs={{0,2},{1,3},{2,0},{3,1},{4,6},{5,7},{6,4},{7,5},{8,10},{9,11},{10,... | collective-permute-start | bytes 1572872 | tf_op jit(solution)/shard_map/ppermute | solution.py:53

commit v5 on v4

--- a/solution.py
+++ b/solution.py
@@ -38,10 +38,10 @@
 
 def polyphase(extended, coefficients, frames):
     tap_count = coefficients.shape[0]
-    running = jnp.zeros((extended.shape[0], frames, extended.shape[2]), jnp.float32)
+    running = jnp.zeros((frames,) + extended.shape[1:], jnp.float32)
     for tap_index in range(tap_count):
         running = running + coefficients[tap_index][None, None, :] * extended[
-            :, tap_index : tap_index + frames, :
+            tap_index : tap_index + frames
         ].astype(jnp.float32)
     return running.astype(jnp.bfloat16)
 
@@ -65,11 +65,13 @@
 
     blocks = voltages.reshape(n_tm, per_dev, samples)
     blocks = lax.all_to_all(blocks, "tm", 0, 0, tiled=True)
-    frames = blocks.reshape(n_tm, per_dev, frames_here, frame_len)
-    frames = jnp.transpose(frames, (1, 0, 2, 3)).reshape(per_dev, total_frames, frame_len)
-    padding = jnp.zeros((per_dev, tap_count - 1, frame_len), frames.dtype)
-    extended = jnp.concatenate([frames, padding], axis=1)
+    frames = jnp.transpose(
+        blocks.reshape(n_tm, per_dev, frames_here, frame_len), (0, 2, 1, 3)
+    ).reshape(total_frames, per_dev, frame_len)
+    padding = jnp.zeros((tap_count - 1, per_dev, frame_len), frames.dtype)
+    extended = jnp.concatenate([frames, padding], axis=0)
     filtered = polyphase(extended, coefficients, total_frames)
+    filtered = jnp.transpose(filtered, (1, 0, 2))
 
     table = dft_rows(frame_len, n_tm)
     spectra = jnp.einsum(

time: 161 us -> 161 us (level)
    convert_element_type x1 -> x0, other arithmetic: 8.27 us -> none  [polyphase(): return running.astype(jnp.bfloat16)]
    transpose x0 -> x1, other arithmetic: none -> 8.27 us  [local(): filtered = jnp.transpose(filtered, (1, 0, 2))]
where the time goes in v5:
time: 161 us; the launch traced here: 160 us
  waiting for transfers between devices  67.1 us (42%)
  local copies, waits for them, and re-layouts  31.1 us (19%)
  starting transfers between devices  27.8 us (17%)
  other arithmetic  25.4 us (16%)
  matrix products  8.6 us (5%)
    ppermute x4, waiting for transfers between devices, exchange(): received = lax.ppermute(jnp.where(low, blocks[1], blocks[0]), axis, pairs)  44.2 us
    slice x3, local copies, waits for them, and re-layouts, local(): weights[chosen]  23.6 us
    all_to_all x1, waiting for transfers between devices, local(): blocks = lax.all_to_all(blocks, 'tm', 0, 0, tiled=True)  18.6 us
    all_to_all x1, starting transfers between devices, local(): blocks = lax.all_to_all(blocks, 'tm', 0, 0, tiled=True)  12.6 us
    ppermute x4, starting transfers between devices, exchange(): received = lax.ppermute(jnp.where(low, blocks[1], blocks[0]), axis, pairs)  9.21 us
    transpose x1, other arithmetic, local(): filtered = jnp.transpose(filtered, (1, 0, 2))  8.27 us
    dot_general x1, matrix products, local(): jnp.einsum('jk,mk->jm', table, filtered.reshape(per_dev * total_frames, f...  6.95 us
    convert_element_type x1, other arithmetic, dft_rows(): return table.reshape(cols, frame_len).astype(jnp.bfloat16)  6.18 us
  transfers between devices with their start and end apart: 6, of which 4 were waited for; matrix products, arithmetic and copies ran while one was open for 24% of the time, Pallas kernels for 0%

profile of v5, /device:TPU:1, one launch (start us, length us, event | category | flops | bytes accessed | tf_op | source)
XLA Modules:
  0.0 160.2 jit_solution(5958959969428193014)
XLA Ops:
  0.0 0.0 copy-start.2
  0.0 2.3 %reshape.432 = bf16[64,4,2048]{2,1,0:T(4,128)(2,1)} reshape(bf16[256,2048]{1,0:T(8,128)(2,1)} %param.3) | data formatting | bytes 2097152 | tf_op jit(solution)/shard_map/reshape | solution.py:66
  2.3 12.6 %all-to-all-start = ((bf16[64,4,2048]{2,1,0:T(4,128)(2,1)}), bf16[64,4,2048]{2,1,0:T(4,128)(2,1)S(1)}, u32[]{:S(2)}, u32[]{:S(2)}) async-start(bf16[64,4,2048]{2,1,0:T(4,128)(2,1)} %reshape.432), calls=%async_computation | async-start | bytes 2097152 | tf_op jit(solution)/shard_map/all_to_all | solution.py:67
  14.9 0.0 copy-done.2
  14.9 0.1 fusion.50
  15.0 1.1 negate_select_fusion.3
  16.2 2.0 %fusion.24 = (f32[2048,64]{0,1:T(8,128)S(1)}, f32[2048,64]{0,1:T(8,128)S(1)}) fusion(s32[2048]{0:T(1024)S(1)} %fusion.36), kind=kLoop, calls=%fused_computation.51 | loop fusion | flops 1835008 | bytes 1056768 | tf_op jit(solution)/shard_map/cos | solution.py:30
  18.2 6.2 %multiply_convert_fusion = bf16[2048,32,64]{0,2,1:T(8,128)(2,1)} fusion(f32[2048,64]{0,1:T(8,128)S(1)} %get-tuple-element.36, f32[2048,32]{0,1:T(8,128)S(1)} %get-tuple-element.34, f32[2048,64]{0,1:T(8,128)S(1)} %get-tuple-element.35, f32[2048,32]{0,1:T(8,128)S(1)} %get-tuple-element.33), kind=kLoop, calls=%fused_computation | loop fusion | flops 20971520 | bytes 9961472 | tf_op jit(solution)/shard_map/convert_element_type | solution.py:36
  24.4 18.6 %all-to-all-done = bf16[64,4,2048]{2,1,0:T(4,128)(2,1)S(1)} async-done(((bf16[64,4,2048]{2,1,0:T(4,128)(2,1)}), bf16[64,4,2048]{2,1,0:T(4,128)(2,1)S(1)}, u32[]{:S(2)}, u32[]{:S(2)}) %all-to-all-start) | async-done | bytes 1048608 | tf_op jit(solution)/shard_map/all_to_all | solution.py:67
  43.0 8.3 %fusion.9 = bf16[4,64,2048]{2,0,1:T(4,128)(2,1)S(1)} fusion(f32[2048]{0:T(1024)S(1)} %bitcast.112, f32[2048]{0:T(1024)S(1)} %bitcast.113, f32[2048]{0:T(1024)S(1)} %bitcast.99, f32[2048]{0:T(1024)S(1)} %bitcast.100, f32[2048]{0:T(1024)S(1)} %bitcast.101, f32[2048]{0:T(1024)S(1)} %bitcast.102, f32[2048]{0:T(1024)S(1)} %bitcast.103, f32[2048]{0:T(1024)S(1)} %bitcast.104, ...), kind=kLoop, calls=%fused_computation.22 | loop fusion | flops 25165824 | bytes 2228224 | tf_op jit(solution)/shard_map/transpose | solution.py:74
  51.3 0.6 copy.53
  51.9 7.0 %convolution_convert_fusion = bf16[2048,256]{1,0:T(8,128)(2,1)} fusion(bf16[2048,2048]{0,1:T(8,128)(2,1)} %bitcast.91, bf16[256,2048]{1,0:T(8,128)(2,1)S(1)} %bitcast.97), kind=kOutput, calls=%fused_computation.5 | convolution fusion | flops 2148007936 | bytes 10485760 | tf_op jit(solution)/shard_map/jk,mk->jm/dot_general | solution.py:77
  58.8 6.1 %all-to-all-start.1 = ((bf16[64,32,256]{2,1,0:T(8,128)(2,1)}), bf16[64,32,256]{2,1,0:T(8,128)(2,1)S(1)}, u32[]{:S(2)}, u32[]{:S(2)}) async-start(bf16[64,32,256]{2,1,0:T(8,128)(2,1)} %bitcast.19), calls=%async_computation.1 | async-start | bytes 2097152 | tf_op jit(solution)/shard_map/all_to_all | solution.py:87
  64.9 8.4 %fusion.46 = (bf16[8,256,2,512]{3,2,1,0:T(2,128)(2,1)}, bf16[8,256,2,512]{3,2,1,0:T(2,128)(2,1)}) fusion(bf16[16,256,2,512]{3,2,1,0:T(2,128)(2,1)} %param.5), kind=kLoop, calls=%fused_computation.89 | loop fusion | bytes 16777216 | tf_op jit(solution)/shard_map/slice | solution.py:105
  73.3 7.7 %reshape.445 = bf16[8,512,4,128]{3,2,1,0:T(4,128)(2,1)} reshape(bf16[8,256,2,512]{3,2,1,0:T(2,128)(2,1)} %get-tuple-element.5) | data formatting | bytes 8388608 | tf_op jit(solution)/shard_map/slice | solution.py:105
  81.0 7.6 %reshape.446 = bf16[8,512,4,128]{3,2,1,0:T(4,128)(2,1)} reshape(bf16[8,256,2,512]{3,2,1,0:T(2,128)(2,1)} %get-tuple-element.6) | data formatting | bytes 8388608 | tf_op jit(solution)/shard_map/slice | solution.py:105
  88.6 4.3 %all-to-all-done.1 = bf16[64,32,256]{2,1,0:T(8,128)(2,1)S(1)} async-done(((bf16[64,32,256]{2,1,0:T(8,128)(2,1)}), bf16[64,32,256]{2,1,0:T(8,128)(2,1)S(1)}, u32[]{:S(2)}, u32[]{:S(2)}) %all-to-all-start.1) | async-done | bytes 1048608 | tf_op jit(solution)/shard_map/all_to_all | solution.py:87
  92.8 0.8 reshape.435
  93.7 0.6 copy.54
  94.3 0.3 slice_negate_fusion
  94.6 1.2 maximum_maximum_fusion
  95.7 0.0 copy-start.1
  95.7 0.4 fusion.48
  96.1 1.8 %copy-done.1 = bf16[8,512,4,128]{3,2,1,0:T(4,128)(2,1)S(1)} copy-done((bf16[8,512,4,128]{3,2,1,0:T(4,128)(2,1)S(1)}, bf16[8,512,4,128]{3,2,1,0:T(4,128)(2,1)}, u32[]{:S(2)}) %copy-start.1) | copy-done | bytes 4194328
  97.9 0.8 fusion.2
  98.8 0.0 copy-start
  98.8 1.7 %fusion.47 = (f32[2,1,8,128,128]{3,4,1,0,2:T(8,128)S(1)}, f32[2,8,128,128]{2,3,0,1:T(8,128)}, f32[2,1,8,128,128]{3,4,1,0,2:T(8,128)}) fusion(f32[2,2,8,128,128]{3,4,1,0,2:T(8,128)S(1)} %bitcast.89, pred[]{:T(512)S(6)} %eq.30), kind=kLoop, calls=%fused_computation.90 | loop fusion | flops 262144 | bytes 5242881 | tf_op jit(solution)/shard_map/slice | solution.py:110
  100.4 2.4 %collective-permute-start = (f32[2,8,128,128]{2,3,0,1:T(8,128)}, f32[2,8,128,128]{2,3,0,1:T(8,128)}, u32[]{:S(2)}, u32[]{:S(2)}) collective-permute-start(f32[2,8,128,128]{2,3,0,1:T(8,128)} %get-tuple-element.8), channel_id=1, source_target_pairs={{0,1},{1,0},{2,3},{3,2},{4,5},{5,4},{6,7},{7,6},{8,9},{9,8},{10,11... | collective-permute-start | bytes 3145736 | tf_op jit(solution)/shard_map/ppermute | solution.py:53
  102.8 0.0 copy-done
  102.8 0.8 fusion
  103.7 0.1 fusion.49
  103.8 1.1 select_bitcast_fusion
  104.9 1.3 collective-permute-start.2
  106.2 0.0 collective-permute-done
  106.2 1.7 %fusion.8 = f32[1,2,8,128,128]{3,4,1,2,0:T(8,128)S(1)} fusion(f32[2,8,128,128]{2,3,0,1:T(8,128)} %collective-permute-done, f32[2,1,8,128,128]{3,4,1,0,2:T(8,128)} %get-tuple-element.9, f32[2,1,8,128,128]{3,4,1,0,2:T(8,128)S(1)} %get-tuple-element.7, pred[]{:T(512)S(6)} %eq.30), kind=kLoop, calls=%fused_computation.15 | loop fusion | flops 524288 | bytes 4194305 | tf_op jit(solution)/shard_map/reshape | solution.py:109
  107.9 0.1 select_bitcast_fusion.3
  107.9 4.3 %collective-permute-start.1 = (f32[1,8,128,128]{2,3,1,0:T(8,128)S(1)}, f32[1,8,128,128]{2,3,1,0:T(8,128)S(1)}, u32[]{:S(2)}, u32[]{:S(2)}) collective-permute-start(f32[1,8,128,128]{2,3,1,0:T(8,128)S(1)} %select_bitcast_fusion.3), channel_id=1, source_target_pairs={{0,2},{1,3},{2,0},{3,1},{4,6},{5,7},{6,4},{7,5},{8,10},{9,11},{10,... | collective-permute-start | bytes 1572872 | tf_op jit(solution)/shard_map/ppermute | solution.py:53
  112.2 0.0 collective-permute-done.2
  112.2 1.4 fusion.5
  113.6 0.1 select_bitcast_fusion.2
  113.7 1.2 collective-permute-start.3
  114.9 27.4 %collective-permute-done.1 = f32[1,8,128,128]{2,3,1,0:T(8,128)S(1)} collective-permute-done((f32[1,8,128,128]{2,3,1,0:T(8,128)S(1)}, f32[1,8,128,128]{2,3,1,0:T(8,128)S(1)}, u32[]{:S(2)}, u32[]{:S(2)}) %collective-permute-start.1) | collective-permute-done | bytes 524320 | tf_op jit(solution)/shard_map/ppermute | solution.py:53
  142.3 0.1 fusion.15
  142.5 0.1 bitcast_reduce_fusion.1
  142.5 16.8 %collective-permute-done.3 = f32[1,8,128,128]{2,3,1,0:T(8,128)S(1)} collective-permute-done((f32[1,8,128,128]{2,3,1,0:T(8,128)S(1)}, f32[1,8,128,128]{2,3,1,0:T(8,128)S(1)}, u32[]{:S(2)}, u32[]{:S(2)}) %collective-permute-start.3) | collective-permute-done | bytes 524320 | tf_op jit(solution)/shard_map/ppermute | solution.py:53
  159.4 0.1 fusion.16
  159.5 0.1 bitcast_reduce_fusion
  159.6 0.6 copy.72
  (7 shorter events, 0.1 us)
Async XLA Ops:
  0.0 14.9 %copy-start.2 = (f32[16,2048]{1,0:T(8,128)S(1)}, f32[16,2048]{1,0:T(8,128)}, u32[]{:S(2)}) copy-start(f32[16,2048]{1,0:T(8,128)} %param.4) | copy-start | bytes 393220
  2.3 40.7 %all-to-all-start = ((bf16[64,4,2048]{2,1,0:T(4,128)(2,1)}), bf16[64,4,2048]{2,1,0:T(4,128)(2,1)S(1)}, u32[]{:S(2)}, u32[]{:S(2)}) async-start(bf16[64,4,2048]{2,1,0:T(4,128)(2,1)} %reshape.432), calls=%async_computation | async-start | bytes 2097152 | tf_op jit(solution)/shard_map/all_to_all | solution.py:67
  58.8 34.0 %all-to-all-start.1 = ((bf16[64,32,256]{2,1,0:T(8,128)(2,1)}), bf16[64,32,256]{2,1,0:T(8,128)(2,1)S(1)}, u32[]{:S(2)}, u32[]{:S(2)}) async-start(bf16[64,32,256]{2,1,0:T(8,128)(2,1)} %bitcast.19), calls=%async_computation.1 | async-start | bytes 2097152 | tf_op jit(solution)/shard_map/all_to_all | solution.py:87
  95.7 2.2 %copy-start.1 = (bf16[8,512,4,128]{3,2,1,0:T(4,128)(2,1)S(1)}, bf16[8,512,4,128]{3,2,1,0:T(4,128)(2,1)}, u32[]{:S(2)}) copy-start(bf16[8,512,4,128]{3,2,1,0:T(4,128)(2,1)} %reshape.445) | copy-start | bytes 12582916
  98.8 4.1 %copy-start = (bf16[8,512,4,128]{3,2,1,0:T(4,128)(2,1)S(1)}, bf16[8,512,4,128]{3,2,1,0:T(4,128)(2,1)}, u32[]{:S(2)}) copy-start(bf16[8,512,4,128]{3,2,1,0:T(4,128)(2,1)} %reshape.446) | copy-start | bytes 12582916
  100.4 5.7 %collective-permute-start = (f32[2,8,128,128]{2,3,0,1:T(8,128)}, f32[2,8,128,128]{2,3,0,1:T(8,128)}, u32[]{:S(2)}, u32[]{:S(2)}) collective-permute-start(f32[2,8,128,128]{2,3,0,1:T(8,128)} %get-tuple-element.8), channel_id=1, source_target_pairs={{0,1},{1,0},{2,3},{3,2},{4,5},{5,4},{6,7},{7,6},{8,9},{9,8},{10,11... | collective-permute-start | bytes 3145736 | tf_op jit(solution)/shard_map/ppermute | solution.py:53
  104.9 7.3 %collective-permute-start.2 = (f32[2,8,128,128]{2,3,1,0:T(8,128)}, f32[2,8,128,128]{2,3,1,0:T(8,128)}, u32[]{:S(2)}, u32[]{:S(2)}) collective-permute-start(f32[2,8,128,128]{2,3,1,0:T(8,128)} %select_bitcast_fusion), channel_id=1, source_target_pairs={{0,1},{1,0},{2,3},{3,2},{4,5},{5,4},{6,7},{7,6},{8,9},{9,8},{10,11... | collective-permute-start | bytes 3145736 | tf_op jit(solution)/shard_map/ppermute | solution.py:53
  107.9 34.4 %collective-permute-start.1 = (f32[1,8,128,128]{2,3,1,0:T(8,128)S(1)}, f32[1,8,128,128]{2,3,1,0:T(8,128)S(1)}, u32[]{:S(2)}, u32[]{:S(2)}) collective-permute-start(f32[1,8,128,128]{2,3,1,0:T(8,128)S(1)} %select_bitcast_fusion.3), channel_id=1, source_target_pairs={{0,2},{1,3},{2,0},{3,1},{4,6},{5,7},{6,4},{7,5},{8,10},{9,11},{10,... | collective-permute-start | bytes 1572872 | tf_op jit(solution)/shard_map/ppermute | solution.py:53
  113.7 45.7 %collective-permute-start.3 = (f32[1,8,128,128]{2,3,1,0:T(8,128)S(1)}, f32[1,8,128,128]{2,3,1,0:T(8,128)S(1)}, u32[]{:S(2)}, u32[]{:S(2)}) collective-permute-start(f32[1,8,128,128]{2,3,1,0:T(8,128)S(1)} %select_bitcast_fusion.2), channel_id=1, source_target_pairs={{0,2},{1,3},{2,0},{3,1},{4,6},{5,7},{6,4},{7,5},{8,10},{9,11},{10,... | collective-permute-start | bytes 1572872 | tf_op jit(solution)/shard_map/ppermute | solution.py:53

commit v6 on v5

--- a/solution.py
+++ b/solution.py
@@ -96,7 +96,7 @@
     )
     per_out = beam_weights.shape[3] // n_feed
     weights = beam_weights.reshape(per_group, feeds_here * 2, n_feed, per_out)
-    n_parts = 2
+    n_parts = 4
     per_part = per_group // n_parts
     binned_parts = []
     for part in range(n_parts):

time: 161 us -> 180 us (1.12)
  other arithmetic: 25.4 us -> 37.6 us
  starting transfers between devices: 27.8 us -> 35.1 us
  waiting for transfers between devices: 67.1 us -> 62.1 us
  local copies, waits for them, and re-layouts: 31.1 us -> 34.7 us
    concatenate x1, other arithmetic: 1.18 us -> 13.6 us  [local(): jnp.concatenate([for_real, for_imag], axis=3)]
    ppermute x4 -> x8, starting transfers between devices: 9.21 us -> 16.5 us  [exchange(): received = lax.ppermute(jnp.where(low, blocks[1], blocks[0]), axis, pairs)]
    ppermute x4 -> x8, waiting for transfers between devices: 44.2 us -> 39.1 us  [exchange(): received = lax.ppermute(jnp.where(low, blocks[1], blocks[0]), axis, pairs)]
    neg x1, other arithmetic: 0.27 us -> 5.2 us  [local(): for_real = jnp.stack([real_part, -imag_part], axis=2)]
    reshape x2, local copies, waits for them, and re-layouts: 1.45 us -> 5.56 us  [local(): turned = turned.reshape(n_tm, per_group, 2, per_dev, total_frames)]
    reshape x2 -> x4, other arithmetic: 3.08 us -> 0.32 us  [local(): split = beams.reshape(-1, 2, *beams.shape[1:])]
    slice x3 -> x5, local copies, waits for them, and re-layouts: 23.6 us -> 23.5 us  [local(): weights[chosen]]
  transfers between devices with their start and end apart: 6 -> 10, of which waited for: 4 -> 6; matrix products, arithmetic and copies ran while one was open for 24% -> 20% of each run, Pallas kernels for 0% -> 0%
where the time goes in v6:
time: 180 us; the launch traced here: 179 us
  waiting for transfers between devices  62.1 us (34%)
  other arithmetic  37.6 us (21%)
  starting transfers between devices  35.1 us (20%)
  local copies, waits for them, and re-layouts  34.7 us (19%)
  matrix products  8.97 us (5%)
    ppermute x8, waiting for transfers between devices, exchange(): received = lax.ppermute(jnp.where(low, blocks[1], blocks[0]), axis, pairs)  39.1 us
    slice x5, local copies, waits for them, and re-layouts, local(): weights[chosen]  23.5 us
    all_to_all x1, waiting for transfers between devices, local(): blocks = lax.all_to_all(blocks, 'tm', 0, 0, tiled=True)  18.6 us
    ppermute x8, starting transfers between devices, exchange(): received = lax.ppermute(jnp.where(low, blocks[1], blocks[0]), axis, pairs)  16.5 us
    concatenate x1, other arithmetic, local(): jnp.concatenate([for_real, for_imag], axis=3)  13.6 us
    all_to_all x1, starting transfers between devices, local(): blocks = lax.all_to_all(blocks, 'tm', 0, 0, tiled=True)  12.6 us
    transpose x1, other arithmetic, local(): filtered = jnp.transpose(filtered, (1, 0, 2))  8.27 us
    dot_general x1, matrix products, local(): jnp.einsum('jk,mk->jm', table, filtered.reshape(per_dev * total_frames, f...  6.96 us
  transfers between devices with their start and end apart: 10, of which 6 were waited for; matrix products, arithmetic and copies ran while one was open for 20% of the time, Pallas kernels for 0%

profile of v6, /device:TPU:1, one launch (start us, length us, event | category | flops | bytes accessed | tf_op | source)
XLA Modules:
  0.0 178.9 jit_solution(14733881706682635593)
XLA Ops:
  0.0 2.3 %reshape.554 = bf16[64,4,2048]{2,1,0:T(4,128)(2,1)} reshape(bf16[256,2048]{1,0:T(8,128)(2,1)} %param.3) | data formatting | bytes 2097152 | tf_op jit(solution)/shard_map/reshape | solution.py:66
  2.3 12.6 %all-to-all-start = ((bf16[64,4,2048]{2,1,0:T(4,128)(2,1)}), bf16[64,4,2048]{2,1,0:T(4,128)(2,1)S(1)}, u32[]{:S(2)}, u32[]{:S(2)}) async-start(bf16[64,4,2048]{2,1,0:T(4,128)(2,1)} %reshape.554), calls=%async_computation | async-start | bytes 2097152 | tf_op jit(solution)/shard_map/all_to_all | solution.py:67
  14.9 0.1 fusion.58
  15.0 1.1 negate_select_fusion.3
  16.2 2.0 %fusion.30 = (f32[2048,64]{0,1:T(8,128)S(1)}, f32[2048,64]{0,1:T(8,128)S(1)}) fusion(s32[2048]{0:T(1024)S(1)} %fusion.42), kind=kLoop, calls=%fused_computation.63 | loop fusion | flops 1835008 | bytes 1056768 | tf_op jit(solution)/shard_map/cos | solution.py:30
  18.2 6.2 %multiply_convert_fusion = bf16[2048,32,64]{0,2,1:T(8,128)(2,1)} fusion(f32[2048,64]{0,1:T(8,128)S(1)} %get-tuple-element.44, f32[2048,32]{0,1:T(8,128)S(1)} %get-tuple-element.42, f32[2048,64]{0,1:T(8,128)S(1)} %get-tuple-element.43, f32[2048,32]{0,1:T(8,128)S(1)} %get-tuple-element.41), kind=kLoop, calls=%fused_computation | loop fusion | flops 20971520 | bytes 9961472 | tf_op jit(solution)/shard_map/convert_element_type | solution.py:36
  24.4 18.6 %all-to-all-done = bf16[64,4,2048]{2,1,0:T(4,128)(2,1)S(1)} async-done(((bf16[64,4,2048]{2,1,0:T(4,128)(2,1)}), bf16[64,4,2048]{2,1,0:T(4,128)(2,1)S(1)}, u32[]{:S(2)}, u32[]{:S(2)}) %all-to-all-start) | async-done | bytes 1048608 | tf_op jit(solution)/shard_map/all_to_all | solution.py:67
  43.0 8.3 %fusion.8 = bf16[4,64,2048]{2,0,1:T(4,128)(2,1)S(1)} fusion(f32[2048]{0:T(1024)S(1)} %bitcast.176, f32[2048]{0:T(1024)S(1)} %bitcast.177, f32[2048]{0:T(1024)S(1)} %bitcast.163, f32[2048]{0:T(1024)S(1)} %bitcast.164, f32[2048]{0:T(1024)S(1)} %bitcast.165, f32[2048]{0:T(1024)S(1)} %bitcast.166, f32[2048]{0:T(1024)S(1)} %bitcast.167, f32[2048]{0:T(1024)S(1)} %bitcast.168, ...), kind=kLoop, calls=%fused_computation.16 | loop fusion | flops 25165824 | bytes 2228224 | tf_op jit(solution)/shard_map/transpose | solution.py:74
  51.3 0.6 copy.69
  51.8 7.0 %convolution_convert_fusion = bf16[2048,256]{1,0:T(8,128)(2,1)} fusion(bf16[2048,2048]{0,1:T(8,128)(2,1)} %bitcast.148, bf16[256,2048]{1,0:T(8,128)(2,1)S(1)} %bitcast.157), kind=kOutput, calls=%fused_computation.1 | convolution fusion | flops 2148007936 | bytes 10485760 | tf_op jit(solution)/shard_map/jk,mk->jm/dot_general | solution.py:77
  58.8 6.1 %all-to-all-start.1 = ((bf16[64,32,256]{2,1,0:T(8,128)(2,1)}), bf16[64,32,256]{2,1,0:T(8,128)(2,1)S(1)}, u32[]{:S(2)}, u32[]{:S(2)}) async-start(bf16[64,32,256]{2,1,0:T(8,128)(2,1)} %bitcast.19), calls=%async_computation.1 | async-start | bytes 2097152 | tf_op jit(solution)/shard_map/all_to_all | solution.py:87
  64.9 9.0 %fusion.52 = (bf16[4,256,2,512]{3,2,1,0:T(2,128)(2,1)}, bf16[4,256,2,512]{3,2,1,0:T(2,128)(2,1)}, bf16[4,256,2,512]{3,2,1,0:T(2,128)(2,1)}, bf16[4,256,2,512]{3,2,1,0:T(2,128)(2,1)S(1)}) fusion(bf16[16,256,2,512]{3,2,1,0:T(2,128)(2,1)} %param.5), kind=kLoop, calls=%fused_computation.107 | loop fusion | bytes 16777216 | tf_op jit(solution)/shard_map/slice | solution.py:105
  73.9 4.4 %slice.231 = bf16[4,512,4,128]{3,2,1,0:T(4,128)(2,1)} reshape(bf16[4,256,2,512]{3,2,1,0:T(2,128)(2,1)} %get-tuple-element.5) | data formatting | bytes 4194304 | tf_op jit(solution)/shard_map/slice | solution.py:105
  78.2 4.4 %slice.239 = bf16[4,512,4,128]{3,2,1,0:T(4,128)(2,1)} reshape(bf16[4,256,2,512]{3,2,1,0:T(2,128)(2,1)} %get-tuple-element.6) | data formatting | bytes 4194304 | tf_op jit(solution)/shard_map/slice | solution.py:105
  82.6 2.6 %slice.247 = bf16[4,512,4,128]{3,2,1,0:T(4,128)(2,1)} reshape(bf16[4,256,2,512]{3,2,1,0:T(2,128)(2,1)S(1)} %get-tuple-element.8) | data formatting | bytes 4194304 | tf_op jit(solution)/shard_map/slice | solution.py:105
  85.2 3.1 %slice.255 = bf16[4,512,4,128]{3,2,1,0:T(4,128)(2,1)S(1)} reshape(bf16[4,256,2,512]{3,2,1,0:T(2,128)(2,1)} %get-tuple-element.7) | data formatting | bytes 4194304 | tf_op jit(solution)/shard_map/slice | solution.py:105
  88.4 4.4 %all-to-all-done.1 = bf16[64,32,256]{2,1,0:T(8,128)(2,1)S(1)} async-done(((bf16[64,32,256]{2,1,0:T(8,128)(2,1)}), bf16[64,32,256]{2,1,0:T(8,128)(2,1)S(1)}, u32[]{:S(2)}, u32[]{:S(2)}) %all-to-all-start.1) | async-done | bytes 1048608 | tf_op jit(solution)/shard_map/all_to_all | solution.py:87
  92.8 1.8 %reshape.557 = bf16[64,16,2,4,64]{4,3,2,1,0:T(4,128)(2,1)} reshape(bf16[64,32,256]{2,1,0:T(8,128)(2,1)S(1)} %all-to-all-done.1) | data formatting | bytes 2097152 | tf_op jit(solution)/shard_map/reshape | solution.py:88
  94.6 3.7 %copy.70 = bf16[64,16,2,4,64]{4,2,3,0,1:T(2,128)(2,1)S(1)} copy(bf16[64,16,2,4,64]{4,3,2,1,0:T(4,128)(2,1)} %reshape.557) | data formatting | bytes 2097152 | tf_op jit(solution)/shard_map/reshape | solution.py:88
  98.4 5.2 %slice_negate_fusion = (bf16[16,256,1,64]{3,2,1,0:T(2,128)(2,1)S(1)}, bf16[16,256,1,64]{3,2,1,0:T(2,128)(2,1)S(1)}, bf16[16,256,1,64]{3,2,1,0:T(2,128)(2,1)S(1)}) fusion(bf16[16,256,2,64]{3,2,1,0:T(2,128)(2,1)S(1)} %bitcast.147), kind=kLoop, calls=%fused_computation.106 | loop fusion | flops 262144 | bytes 2621440 | tf_op jit(solution)/shard_map/neg | solution.py:92
  103.6 13.6 %maximum_maximum_fusion = bf16[16,256,2,128]{3,2,1,0:T(2,128)(2,1)S(1)} fusion(bf16[16,256,1,64]{3,2,1,0:T(2,128)(2,1)S(1)} %get-tuple-element.15, bf16[16,256,1,64]{3,2,1,0:T(2,128)(2,1)S(1)} %get-tuple-element.14, bf16[16,256,1,64]{3,2,1,0:T(2,128)(2,1)S(1)} %get-tuple-element.13), kind=kLoop, calls=%fused_computation.2 | loop fusion | flops 8388608 | bytes 3670016 | tf_op jit(solution)/shard_map/concatenate | solution.py:94
  117.2 1.8 %fusion.53 = (bf16[4,256,2,128]{3,2,1,0:T(2,128)(2,1)S(1)}, bf16[4,256,2,128]{3,2,1,0:T(2,128)(2,1)S(1)}, bf16[4,256,2,128]{3,2,1,0:T(2,128)(2,1)S(1)}, bf16[4,256,2,128]{3,2,1,0:T(2,128)(2,1)S(1)}) fusion(bf16[16,256,2,128]{3,2,1,0:T(2,128)(2,1)S(1)} %maximum_maximum_fusion), kind=kLoop, calls=%fused_computation.108 | loop fusion | bytes 4194304 | tf_op jit(solution)/shard_map/slice | solution.py:105
  119.0 0.5 fusion.6
  119.5 0.2 fusion.54
  119.7 2.5 %collective-permute-start = (f32[2,4,128,128]{2,3,0,1:T(8,128)S(1)}, f32[2,4,128,128]{2,3,0,1:T(8,128)S(1)}, u32[]{:S(2)}, u32[]{:S(2)}) collective-permute-start(f32[2,4,128,128]{2,3,0,1:T(8,128)S(1)} %get-tuple-element.17), channel_id=1, source_target_pairs={{0,1},{1,0},{2,3},{3,2},{4,5},{5,4},{6,7},{7,6},{8,9},{9,8},{10,11... | collective-permute-start | bytes 1572872 | tf_op jit(solution)/shard_map/ppermute | solution.py:53
  122.2 0.5 fusion.4
  122.7 0.1 fusion.55
  122.8 1.4 collective-permute-start.2
  124.3 0.5 fusion.2
  124.8 0.1 fusion.56
  124.9 0.1 select_bitcast_fusion.1
  124.9 1.4 collective-permute-start.4
  126.3 0.5 fusion
  126.9 0.1 fusion.57
  127.0 0.1 collective-permute-start.6
  127.1 0.1 fusion.16
  127.3 4.3 %collective-permute-start.1 = (f32[1,4,128,128]{2,3,1,0:T(8,128)S(1)}, f32[1,4,128,128]{2,3,1,0:T(8,128)S(1)}, u32[]{:S(2)}, u32[]{:S(2)}) collective-permute-start(f32[1,4,128,128]{2,3,1,0:T(8,128)S(1)} %select_bitcast_fusion.7), channel_id=1, source_target_pairs={{0,2},{1,3},{2,0},{3,1},{4,6},{5,7},{6,4},{7,5},{8,10},{9,11},{10,... | collective-permute-start | bytes 786440 | tf_op jit(solution)/shard_map/ppermute | solution.py:53
  131.6 0.1 fusion.15
  131.7 1.2 collective-permute-start.3
  132.9 0.1 fusion.14
  133.1 4.3 %collective-permute-start.5 = (f32[1,4,128,128]{2,3,1,0:T(8,128)S(1)}, f32[1,4,128,128]{2,3,1,0:T(8,128)S(1)}, u32[]{:S(2)}, u32[]{:S(2)}) collective-permute-start(f32[1,4,128,128]{2,3,1,0:T(8,128)S(1)} %select_bitcast_fusion.5), channel_id=1, source_target_pairs={{0,2},{1,3},{2,0},{3,1},{4,6},{5,7},{6,4},{7,5},{8,10},{9,11},{10,... | collective-permute-start | bytes 786440 | tf_op jit(solution)/shard_map/ppermute | solution.py:53
  137.4 0.1 fusion.13
  137.5 1.2 collective-permute-start.7
  138.7 6.7 %collective-permute-done.1 = f32[1,4,128,128]{2,3,1,0:T(8,128)S(1)} collective-permute-done((f32[1,4,128,128]{2,3,1,0:T(8,128)S(1)}, f32[1,4,128,128]{2,3,1,0:T(8,128)S(1)}, u32[]{:S(2)}, u32[]{:S(2)}) %collective-permute-start.1) | collective-permute-done | bytes 262176 | tf_op jit(solution)/shard_map/ppermute | solution.py:53
  145.5 15.5 %collective-permute-done.3 = f32[1,4,128,128]{2,3,1,0:T(8,128)S(1)} collective-permute-done((f32[1,4,128,128]{2,3,1,0:T(8,128)S(1)}, f32[1,4,128,128]{2,3,1,0:T(8,128)S(1)}, u32[]{:S(2)}, u32[]{:S(2)}) %collective-permute-start.3) | collective-permute-done | bytes 262176 | tf_op jit(solution)/shard_map/ppermute | solution.py:53
  161.1 11.4 %collective-permute-done.5 = f32[1,4,128,128]{2,3,1,0:T(8,128)S(1)} collective-permute-done((f32[1,4,128,128]{2,3,1,0:T(8,128)S(1)}, f32[1,4,128,128]{2,3,1,0:T(8,128)S(1)}, u32[]{:S(2)}, u32[]{:S(2)}) %collective-permute-start.5) | collective-permute-done | bytes 262176 | tf_op jit(solution)/shard_map/ppermute | solution.py:53
  172.7 5.4 %collective-permute-done.7 = f32[1,4,128,128]{2,3,1,0:T(8,128)S(1)} collective-permute-done((f32[1,4,128,128]{2,3,1,0:T(8,128)S(1)}, f32[1,4,128,128]{2,3,1,0:T(8,128)S(1)}, u32[]{:S(2)}, u32[]{:S(2)}) %collective-permute-start.7) | collective-permute-done | bytes 262176 | tf_op jit(solution)/shard_map/ppermute | solution.py:53
  178.3 0.6 copy.94
  (36 shorter events, 0.7 us)
Async XLA Ops:
  0.0 14.9 %copy-start.3 = (f32[16,2048]{1,0:T(8,128)S(1)}, f32[16,2048]{1,0:T(8,128)}, u32[]{:S(2)}) copy-start(f32[16,2048]{1,0:T(8,128)} %param.4) | copy-start | bytes 393220
  2.3 40.7 %all-to-all-start = ((bf16[64,4,2048]{2,1,0:T(4,128)(2,1)}), bf16[64,4,2048]{2,1,0:T(4,128)(2,1)S(1)}, u32[]{:S(2)}, u32[]{:S(2)}) async-start(bf16[64,4,2048]{2,1,0:T(4,128)(2,1)} %reshape.554), calls=%async_computation | async-start | bytes 2097152 | tf_op jit(solution)/shard_map/all_to_all | solution.py:67
  58.8 34.0 %all-to-all-start.1 = ((bf16[64,32,256]{2,1,0:T(8,128)(2,1)}), bf16[64,32,256]{2,1,0:T(8,128)(2,1)S(1)}, u32[]{:S(2)}, u32[]{:S(2)}) async-start(bf16[64,32,256]{2,1,0:T(8,128)(2,1)} %bitcast.19), calls=%async_computation.1 | async-start | bytes 2097152 | tf_op jit(solution)/shard_map/all_to_all | solution.py:87
  117.2 1.8 %copy-start.1 = (bf16[4,512,4,128]{3,2,1,0:T(4,128)(2,1)S(1)}, bf16[4,512,4,128]{3,2,1,0:T(4,128)(2,1)}, u32[]{:S(2)}) copy-start(bf16[4,512,4,128]{3,2,1,0:T(4,128)(2,1)} %slice.231) | copy-start | bytes 6291460
  119.5 2.7 %copy-start.2 = (bf16[4,512,4,128]{3,2,1,0:T(4,128)(2,1)S(1)}, bf16[4,512,4,128]{3,2,1,0:T(4,128)(2,1)}, u32[]{:S(2)}) copy-start(bf16[4,512,4,128]{3,2,1,0:T(4,128)(2,1)} %slice.239) | copy-start | bytes 6291460
  119.7 7.4 %collective-permute-start = (f32[2,4,128,128]{2,3,0,1:T(8,128)S(1)}, f32[2,4,128,128]{2,3,0,1:T(8,128)S(1)}, u32[]{:S(2)}, u32[]{:S(2)}) collective-permute-start(f32[2,4,128,128]{2,3,0,1:T(8,128)S(1)} %get-tuple-element.17), channel_id=1, source_target_pairs={{0,1},{1,0},{2,3},{3,2},{4,5},{5,4},{6,7},{7,6},{8,9},{9,8},{10,11... | collective-permute-start | bytes 1572872 | tf_op jit(solution)/shard_map/ppermute | solution.py:53
  122.7 1.6 copy-start
  122.8 8.7 %collective-permute-start.2 = (f32[2,4,128,128]{2,3,1,0:T(8,128)S(1)}, f32[2,4,128,128]{2,3,1,0:T(8,128)S(1)}, u32[]{:S(2)}, u32[]{:S(2)}) collective-permute-start(f32[2,4,128,128]{2,3,1,0:T(8,128)S(1)} %select_bitcast_fusion.2), channel_id=1, source_target_pairs={{0,1},{1,0},{2,3},{3,2},{4,5},{5,4},{6,7},{7,6},{8,9},{9,8},{10,11... | collective-permute-start | bytes 1572872 | tf_op jit(solution)/shard_map/ppermute | solution.py:53
  124.9 8.0 %collective-permute-start.4 = (f32[2,4,128,128]{2,3,1,0:T(8,128)S(1)}, f32[2,4,128,128]{2,3,1,0:T(8,128)S(1)}, u32[]{:S(2)}, u32[]{:S(2)}) collective-permute-start(f32[2,4,128,128]{2,3,1,0:T(8,128)S(1)} %select_bitcast_fusion.1), channel_id=1, source_target_pairs={{0,1},{1,0},{2,3},{3,2},{4,5},{5,4},{6,7},{7,6},{8,9},{9,8},{10,11... | collective-permute-start | bytes 1572872 | tf_op jit(solution)/shard_map/ppermute | solution.py:53
  127.0 10.3 %collective-permute-start.6 = (f32[2,4,128,128]{2,3,1,0:T(8,128)S(1)}, f32[2,4,128,128]{2,3,1,0:T(8,128)S(1)}, u32[]{:S(2)}, u32[]{:S(2)}) collective-permute-start(f32[2,4,128,128]{2,3,1,0:T(8,128)S(1)} %select_bitcast_fusion), channel_id=1, source_target_pairs={{0,1},{1,0},{2,3},{3,2},{4,5},{5,4},{6,7},{7,6},{8,9},{9,8},{10,11... | collective-permute-start | bytes 1572872 | tf_op jit(solution)/shard_map/ppermute | solution.py:53
  127.3 18.2 %collective-permute-start.1 = (f32[1,4,128,128]{2,3,1,0:T(8,128)S(1)}, f32[1,4,128,128]{2,3,1,0:T(8,128)S(1)}, u32[]{:S(2)}, u32[]{:S(2)}) collective-permute-start(f32[1,4,128,128]{2,3,1,0:T(8,128)S(1)} %select_bitcast_fusion.7), channel_id=1, source_target_pairs={{0,2},{1,3},{2,0},{3,1},{4,6},{5,7},{6,4},{7,5},{8,10},{9,11},{10,... | collective-permute-start | bytes 786440 | tf_op jit(solution)/shard_map/ppermute | solution.py:53
  131.7 29.4 %collective-permute-start.3 = (f32[1,4,128,128]{2,3,1,0:T(8,128)S(1)}, f32[1,4,128,128]{2,3,1,0:T(8,128)S(1)}, u32[]{:S(2)}, u32[]{:S(2)}) collective-permute-start(f32[1,4,128,128]{2,3,1,0:T(8,128)S(1)} %select_bitcast_fusion.6), channel_id=1, source_target_pairs={{0,2},{1,3},{2,0},{3,1},{4,6},{5,7},{6,4},{7,5},{8,10},{9,11},{10,... | collective-permute-start | bytes 786440 | tf_op jit(solution)/shard_map/ppermute | solution.py:53
  133.1 39.5 %collective-permute-start.5 = (f32[1,4,128,128]{2,3,1,0:T(8,128)S(1)}, f32[1,4,128,128]{2,3,1,0:T(8,128)S(1)}, u32[]{:S(2)}, u32[]{:S(2)}) collective-permute-start(f32[1,4,128,128]{2,3,1,0:T(8,128)S(1)} %select_bitcast_fusion.5), channel_id=1, source_target_pairs={{0,2},{1,3},{2,0},{3,1},{4,6},{5,7},{6,4},{7,5},{8,10},{9,11},{10,... | collective-permute-start | bytes 786440 | tf_op jit(solution)/shard_map/ppermute | solution.py:53
  137.5 40.7 %collective-permute-start.7 = (f32[1,4,128,128]{2,3,1,0:T(8,128)S(1)}, f32[1,4,128,128]{2,3,1,0:T(8,128)S(1)}, u32[]{:S(2)}, u32[]{:S(2)}) collective-permute-start(f32[1,4,128,128]{2,3,1,0:T(8,128)S(1)} %select_bitcast_fusion.4), channel_id=1, source_target_pairs={{0,2},{1,3},{2,0},{3,1},{4,6},{5,7},{6,4},{7,5},{8,10},{9,11},{10,... | collective-permute-start | bytes 786440 | tf_op jit(solution)/shard_map/ppermute | solution.py:53

commit v7 on v5

--- a/solution.py
+++ b/solution.py
@@ -38,11 +38,12 @@
 
 def polyphase(extended, coefficients, frames):
     tap_count = coefficients.shape[0]
+    widened = extended.astype(jnp.float32)
     running = jnp.zeros((frames,) + extended.shape[1:], jnp.float32)
     for tap_index in range(tap_count):
-        running = running + coefficients[tap_index][None, None, :] * extended[
+        running = running + coefficients[tap_index][None, None, :] * widened[
             tap_index : tap_index + frames
-        ].astype(jnp.float32)
+        ]
     return running.astype(jnp.bfloat16)
 
 

time: 161 us -> 159 us (0.988)
  matrix products: 8.6 us -> 5.28 us
    dot_general x1, matrix products: 6.95 us -> 3.63 us  [local(): jnp.einsum('jk,mk->jm', table, filtered.reshape(per_dev * total_frames, f...]
where the time goes in v7:
time: 159 us; the launch traced here: 158 us
  waiting for transfers between devices  67.1 us (42%)
  local copies, waits for them, and re-layouts  31.1 us (20%)
  starting transfers between devices  27.7 us (17%)
  other arithmetic  26.9 us (17%)
  matrix products  5.28 us (3%)
    ppermute x4, waiting for transfers between devices, exchange(): received = lax.ppermute(jnp.where(low, blocks[1], blocks[0]), axis, pairs)  44.2 us
    slice x3, local copies, waits for them, and re-layouts, local(): weights[chosen]  23.6 us
    all_to_all x1, waiting for transfers between devices, local(): blocks = lax.all_to_all(blocks, 'tm', 0, 0, tiled=True)  18.6 us
    all_to_all x1, starting transfers between devices, local(): blocks = lax.all_to_all(blocks, 'tm', 0, 0, tiled=True)  12.6 us
    ppermute x4, starting transfers between devices, exchange(): received = lax.ppermute(jnp.where(low, blocks[1], blocks[0]), axis, pairs)  9.2 us
    transpose x1, other arithmetic, local(): filtered = jnp.transpose(filtered, (1, 0, 2))  9.2 us
    convert_element_type x1, other arithmetic, dft_rows(): return table.reshape(cols, frame_len).astype(jnp.bfloat16)  6.16 us
    all_to_all x1, starting transfers between devices, local(): turned = lax.all_to_all(spectra, 'tm', 0, 0, tiled=True)  5.9 us
  transfers between devices with their start and end apart: 6, of which 4 were waited for; matrix products, arithmetic and copies ran while one was open for 24% of the time, Pallas kernels for 0%

profile of v7, /device:TPU:1, one launch (start us, length us, event | category | flops | bytes accessed | tf_op | source)
XLA Modules:
  0.0 158.3 jit_solution(15404335737580316552)
XLA Ops:
  0.0 2.3 %reshape.432 = bf16[64,4,2048]{2,1,0:T(4,128)(2,1)} reshape(bf16[256,2048]{1,0:T(8,128)(2,1)} %param.3) | data formatting | bytes 2097152 | tf_op jit(solution)/shard_map/reshape | solution.py:67
  2.3 12.6 %all-to-all-start = ((bf16[64,4,2048]{2,1,0:T(4,128)(2,1)}), bf16[64,4,2048]{2,1,0:T(4,128)(2,1)S(1)}, u32[]{:S(2)}, u32[]{:S(2)}) async-start(bf16[64,4,2048]{2,1,0:T(4,128)(2,1)} %reshape.432), calls=%async_computation | async-start | bytes 2097152 | tf_op jit(solution)/shard_map/all_to_all | solution.py:68
  14.9 0.0 copy-done.2
  14.9 0.1 fusion.66
  15.0 1.1 negate_select_fusion.3
  16.2 2.0 %fusion.40 = (f32[2048,64]{0,1:T(8,128)S(1)}, f32[2048,64]{0,1:T(8,128)S(1)}) fusion(s32[2048]{0:T(1024)S(1)} %fusion.52), kind=kLoop, calls=%fused_computation.79 | loop fusion | flops 1835008 | bytes 1056768 | tf_op jit(solution)/shard_map/cos | solution.py:30
  18.2 6.2 %multiply_convert_fusion = bf16[2048,32,64]{0,2,1:T(8,128)(2,1)} fusion(f32[2048,64]{0,1:T(8,128)S(1)} %get-tuple-element.36, f32[2048,32]{0,1:T(8,128)S(1)} %get-tuple-element.34, f32[2048,64]{0,1:T(8,128)S(1)} %get-tuple-element.35, f32[2048,32]{0,1:T(8,128)S(1)} %get-tuple-element.33), kind=kLoop, calls=%fused_computation | loop fusion | flops 20971520 | bytes 9961472 | tf_op jit(solution)/shard_map/convert_element_type | solution.py:36
  24.4 18.6 %all-to-all-done = bf16[64,4,2048]{2,1,0:T(4,128)(2,1)S(1)} async-done(((bf16[64,4,2048]{2,1,0:T(4,128)(2,1)}), bf16[64,4,2048]{2,1,0:T(4,128)(2,1)S(1)}, u32[]{:S(2)}, u32[]{:S(2)}) %all-to-all-start) | async-done | bytes 1048608 | tf_op jit(solution)/shard_map/all_to_all | solution.py:68
  43.0 0.6 pad_convert_fusion
  43.6 0.0 slice-start.1
  43.6 9.2 %fusion.25 = bf16[4,64,2048]{2,0,1:T(4,128)(2,1)S(1)} fusion(f32[79,4,2048]{2,1,0:T(4,128)S(1)} %pad_convert_fusion, f32[2048]{0:T(1024)S(1)} %bitcast.114, f32[2048]{0:T(1024)S(1)} %bitcast.115, f32[2048]{0:T(1024)S(1)} %bitcast.101, f32[2048]{0:T(1024)S(1)} %bitcast.102, f32[2048]{0:T(1024)S(1)} %bitcast.103, f32[2048]{0:T(1024)S(1)} %bitcast.104, ...), kind=kLoop, calls=%fused_computation.50 | loop fusion | flops 16777216 | bytes 34734080 | tf_op jit(solution)/shard_map/transpose | solution.py:75
  52.9 0.6 copy.53
  53.4 0.0 slice-done
  53.4 0.0 slice-done.1
  53.5 3.6 %convolution_convert_fusion = bf16[2048,256]{1,0:T(8,128)(2,1)} fusion(bf16[2048,2048]{0,1:T(8,128)(2,1)S(1)} %bitcast.93, bf16[256,2048]{1,0:T(8,128)(2,1)S(1)} %bitcast.99), kind=kOutput, calls=%fused_computation.5 | convolution fusion | flops 2148007936 | bytes 10485760 | tf_op jit(solution)/shard_map/jk,mk->jm/dot_general | solution.py:78
  57.1 5.9 %all-to-all-start.1 = ((bf16[64,32,256]{2,1,0:T(8,128)(2,1)}), bf16[64,32,256]{2,1,0:T(8,128)(2,1)S(1)}, u32[]{:S(2)}, u32[]{:S(2)}) async-start(bf16[64,32,256]{2,1,0:T(8,128)(2,1)} %bitcast.19), calls=%async_computation.1 | async-start | bytes 2097152 | tf_op jit(solution)/shard_map/all_to_all | solution.py:88
  63.0 8.4 %fusion.62 = (bf16[8,256,2,512]{3,2,1,0:T(2,128)(2,1)}, bf16[8,256,2,512]{3,2,1,0:T(2,128)(2,1)}) fusion(bf16[16,256,2,512]{3,2,1,0:T(2,128)(2,1)} %param.5), kind=kLoop, calls=%fused_computation.117 | loop fusion | bytes 16777216 | tf_op jit(solution)/shard_map/slice | solution.py:106
  71.4 7.6 %reshape.445 = bf16[8,512,4,128]{3,2,1,0:T(4,128)(2,1)} reshape(bf16[8,256,2,512]{3,2,1,0:T(2,128)(2,1)} %get-tuple-element.5) | data formatting | bytes 8388608 | tf_op jit(solution)/shard_map/slice | solution.py:106
  79.1 7.6 %reshape.446 = bf16[8,512,4,128]{3,2,1,0:T(4,128)(2,1)} reshape(bf16[8,256,2,512]{3,2,1,0:T(2,128)(2,1)} %get-tuple-element.6) | data formatting | bytes 8388608 | tf_op jit(solution)/shard_map/slice | solution.py:106
  86.7 4.3 %all-to-all-done.1 = bf16[64,32,256]{2,1,0:T(8,128)(2,1)S(1)} async-done(((bf16[64,32,256]{2,1,0:T(8,128)(2,1)}), bf16[64,32,256]{2,1,0:T(8,128)(2,1)S(1)}, u32[]{:S(2)}, u32[]{:S(2)}) %all-to-all-start.1) | async-done | bytes 1048608 | tf_op jit(solution)/shard_map/all_to_all | solution.py:88
  90.9 0.8 reshape.435
  91.8 0.6 copy.54
  92.4 0.3 slice_negate_fusion
  92.7 1.2 maximum_maximum_fusion
  93.8 0.4 fusion.64
  94.2 1.8 %copy-done.1 = bf16[8,512,4,128]{3,2,1,0:T(4,128)(2,1)S(1)} copy-done((bf16[8,512,4,128]{3,2,1,0:T(4,128)(2,1)S(1)}, bf16[8,512,4,128]{3,2,1,0:T(4,128)(2,1)}, u32[]{:S(2)}) %copy-start.1) | copy-done | bytes 4194328
  96.0 0.8 fusion.2
  96.9 1.7 %fusion.63 = (f32[2,1,8,128,128]{3,4,1,0,2:T(8,128)S(1)}, f32[2,8,128,128]{2,3,0,1:T(8,128)}, f32[2,1,8,128,128]{3,4,1,0,2:T(8,128)}) fusion(f32[2,2,8,128,128]{3,4,1,0,2:T(8,128)S(1)} %bitcast.89, pred[]{:T(512)S(6)} %eq.30), kind=kLoop, calls=%fused_computation.118 | loop fusion | flops 262144 | bytes 5242881 | tf_op jit(solution)/shard_map/slice | solution.py:111
  98.5 2.4 %collective-permute-start = (f32[2,8,128,128]{2,3,0,1:T(8,128)}, f32[2,8,128,128]{2,3,0,1:T(8,128)}, u32[]{:S(2)}, u32[]{:S(2)}) collective-permute-start(f32[2,8,128,128]{2,3,0,1:T(8,128)} %get-tuple-element.8), channel_id=1, source_target_pairs={{0,1},{1,0},{2,3},{3,2},{4,5},{5,4},{6,7},{7,6},{8,9},{9,8},{10,11... | collective-permute-start | bytes 3145736 | tf_op jit(solution)/shard_map/ppermute | solution.py:54
  100.9 0.8 fusion
  101.8 0.1 fusion.65
  101.9 1.1 select_bitcast_fusion
  103.0 1.3 collective-permute-start.2
  104.3 0.0 collective-permute-done
  104.3 1.7 %fusion.24 = f32[1,2,8,128,128]{3,4,1,2,0:T(8,128)S(1)} fusion(f32[2,8,128,128]{2,3,0,1:T(8,128)} %collective-permute-done, f32[2,1,8,128,128]{3,4,1,0,2:T(8,128)} %get-tuple-element.9, f32[2,1,8,128,128]{3,4,1,0,2:T(8,128)S(1)} %get-tuple-element.7, pred[]{:T(512)S(6)} %eq.30), kind=kLoop, calls=%fused_computation.47 | loop fusion | flops 524288 | bytes 4194305 | tf_op jit(solution)/shard_map/reshape | solution.py:110
  106.0 0.1 select_bitcast_fusion.3
  106.0 4.3 %collective-permute-start.1 = (f32[1,8,128,128]{2,3,1,0:T(8,128)S(1)}, f32[1,8,128,128]{2,3,1,0:T(8,128)S(1)}, u32[]{:S(2)}, u32[]{:S(2)}) collective-permute-start(f32[1,8,128,128]{2,3,1,0:T(8,128)S(1)} %select_bitcast_fusion.3), channel_id=1, source_target_pairs={{0,2},{1,3},{2,0},{3,1},{4,6},{5,7},{6,4},{7,5},{8,10},{9,11},{10,... | collective-permute-start | bytes 1572872 | tf_op jit(solution)/shard_map/ppermute | solution.py:54
  110.3 0.0 collective-permute-done.2
  110.3 1.4 fusion.21
  111.7 0.1 select_bitcast_fusion.2
  111.8 1.2 collective-permute-start.3
  113.0 27.4 %collective-permute-done.1 = f32[1,8,128,128]{2,3,1,0:T(8,128)S(1)} collective-permute-done((f32[1,8,128,128]{2,3,1,0:T(8,128)S(1)}, f32[1,8,128,128]{2,3,1,0:T(8,128)S(1)}, u32[]{:S(2)}, u32[]{:S(2)}) %collective-permute-start.1) | collective-permute-done | bytes 524320 | tf_op jit(solution)/shard_map/ppermute | solution.py:54
  140.4 0.1 fusion.31
  140.5 0.1 bitcast_reduce_fusion.1
  140.6 16.8 %collective-permute-done.3 = f32[1,8,128,128]{2,3,1,0:T(8,128)S(1)} collective-permute-done((f32[1,8,128,128]{2,3,1,0:T(8,128)S(1)}, f32[1,8,128,128]{2,3,1,0:T(8,128)S(1)}, u32[]{:S(2)}, u32[]{:S(2)}) %collective-permute-start.3) | collective-permute-done | bytes 524320 | tf_op jit(solution)/shard_map/ppermute | solution.py:54
  157.4 0.1 fusion.32
  157.6 0.1 bitcast_reduce_fusion
  157.7 0.6 copy.72
  (13 shorter events, 0.1 us)
Async XLA Ops:
  0.0 14.9 %copy-start.2 = (f32[16,2048]{1,0:T(8,128)S(1)}, f32[16,2048]{1,0:T(8,128)}, u32[]{:S(2)}) copy-start(f32[16,2048]{1,0:T(8,128)} %param.4) | copy-start | bytes 393220
  2.3 40.7 %all-to-all-start = ((bf16[64,4,2048]{2,1,0:T(4,128)(2,1)}), bf16[64,4,2048]{2,1,0:T(4,128)(2,1)S(1)}, u32[]{:S(2)}, u32[]{:S(2)}) async-start(bf16[64,4,2048]{2,1,0:T(4,128)(2,1)} %reshape.432), calls=%async_computation | async-start | bytes 2097152 | tf_op jit(solution)/shard_map/all_to_all | solution.py:68
  43.0 10.4 %slice-start = ((s8[8388608]{0:T(1024)(128)(4,1)}), s8[4194304]{0:T(1024)(128)(4,1)S(1)}, s32[]{:S(2)}) async-start(s8[8388608]{0:T(1024)(128)(4,1)} %bitcast.91), calls=%async_computation.2 | async-start | bytes 8388608
  43.6 9.8 %slice-start.1 = ((s8[8388608]{0:T(1024)(128)(4,1)}), s8[4194304]{0:T(1024)(128)(4,1)S(1)}, s32[]{:S(2)}) async-start(s8[8388608]{0:T(1024)(128)(4,1)} %bitcast.91), calls=%async_computation.3 | async-start | bytes 8388608
  57.1 33.8 %all-to-all-start.1 = ((bf16[64,32,256]{2,1,0:T(8,128)(2,1)}), bf16[64,32,256]{2,1,0:T(8,128)(2,1)S(1)}, u32[]{:S(2)}, u32[]{:S(2)}) async-start(bf16[64,32,256]{2,1,0:T(8,128)(2,1)} %bitcast.19), calls=%async_computation.1 | async-start | bytes 2097152 | tf_op jit(solution)/shard_map/all_to_all | solution.py:88
  93.8 2.2 %copy-start.1 = (bf16[8,512,4,128]{3,2,1,0:T(4,128)(2,1)S(1)}, bf16[8,512,4,128]{3,2,1,0:T(4,128)(2,1)}, u32[]{:S(2)}) copy-start(bf16[8,512,4,128]{3,2,1,0:T(4,128)(2,1)} %reshape.445) | copy-start | bytes 12582916
  96.8 4.1 %copy-start = (bf16[8,512,4,128]{3,2,1,0:T(4,128)(2,1)S(1)}, bf16[8,512,4,128]{3,2,1,0:T(4,128)(2,1)}, u32[]{:S(2)}) copy-start(bf16[8,512,4,128]{3,2,1,0:T(4,128)(2,1)} %reshape.446) | copy-start | bytes 12582916
  98.5 5.7 %collective-permute-start = (f32[2,8,128,128]{2,3,0,1:T(8,128)}, f32[2,8,128,128]{2,3,0,1:T(8,128)}, u32[]{:S(2)}, u32[]{:S(2)}) collective-permute-start(f32[2,8,128,128]{2,3,0,1:T(8,128)} %get-tuple-element.8), channel_id=1, source_target_pairs={{0,1},{1,0},{2,3},{3,2},{4,5},{5,4},{6,7},{7,6},{8,9},{9,8},{10,11... | collective-permute-start | bytes 3145736 | tf_op jit(solution)/shard_map/ppermute | solution.py:54
  103.0 7.3 %collective-permute-start.2 = (f32[2,8,128,128]{2,3,1,0:T(8,128)}, f32[2,8,128,128]{2,3,1,0:T(8,128)}, u32[]{:S(2)}, u32[]{:S(2)}) collective-permute-start(f32[2,8,128,128]{2,3,1,0:T(8,128)} %select_bitcast_fusion), channel_id=1, source_target_pairs={{0,1},{1,0},{2,3},{3,2},{4,5},{5,4},{6,7},{7,6},{8,9},{9,8},{10,11... | collective-permute-start | bytes 3145736 | tf_op jit(solution)/shard_map/ppermute | solution.py:54
  106.0 34.4 %collective-permute-start.1 = (f32[1,8,128,128]{2,3,1,0:T(8,128)S(1)}, f32[1,8,128,128]{2,3,1,0:T(8,128)S(1)}, u32[]{:S(2)}, u32[]{:S(2)}) collective-permute-start(f32[1,8,128,128]{2,3,1,0:T(8,128)S(1)} %select_bitcast_fusion.3), channel_id=1, source_target_pairs={{0,2},{1,3},{2,0},{3,1},{4,6},{5,7},{6,4},{7,5},{8,10},{9,11},{10,... | collective-permute-start | bytes 1572872 | tf_op jit(solution)/shard_map/ppermute | solution.py:54
  111.8 45.7 %collective-permute-start.3 = (f32[1,8,128,128]{2,3,1,0:T(8,128)S(1)}, f32[1,8,128,128]{2,3,1,0:T(8,128)S(1)}, u32[]{:S(2)}, u32[]{:S(2)}) collective-permute-start(f32[1,8,128,128]{2,3,1,0:T(8,128)S(1)} %select_bitcast_fusion.2), channel_id=1, source_target_pairs={{0,2},{1,3},{2,0},{3,1},{4,6},{5,7},{6,4},{7,5},{8,10},{9,11},{10,... | collective-permute-start | bytes 1572872 | tf_op jit(solution)/shard_map/ppermute | solution.py:54

commit v8 on v7

--- a/solution.py
+++ b/solution.py
@@ -97,14 +97,12 @@
     )
     per_out = beam_weights.shape[3] // n_feed
     weights = beam_weights.reshape(per_group, feeds_here * 2, n_feed, per_out)
+    beams_all = jnp.einsum("ckjb,ckn->jcbn", weights, paired, preferred_element_type=jnp.float32)
     n_parts = 2
     per_part = per_group // n_parts
     binned_parts = []
     for part in range(n_parts):
-        chosen = slice(part * per_part, (part + 1) * per_part)
-        beams = jnp.einsum(
-            "ckjb,ckn->jcbn", weights[chosen], paired[chosen], preferred_element_type=jnp.float32
-        )
+        beams = beams_all[:, part * per_part : (part + 1) * per_part]
         flip = 1
         while flip < n_feed:
             split = beams.reshape(-1, 2, *beams.shape[1:])

time: 159 us -> 159 us (level)
  waiting for transfers between devices: 67.1 us -> 77.1 us
  local copies, waits for them, and re-layouts: 31.1 us -> 21.7 us
    slice x4 -> x1, local copies, waits for them, and re-layouts: 24 us -> 0.49 us  [local(): beams = beams_all[:, part * per_part:(part + 1) * per_part]]
    reshape x0 -> x1, local copies, waits for them, and re-layouts: none -> 14.1 us  [local(): weights = beam_weights.reshape(per_group, feeds_here * 2, n_feed, per_out)]
    all_to_all x1, waiting for transfers between devices: 4.26 us -> 13.8 us  [local(): turned = lax.all_to_all(spectra, 'tm', 0, 0, tiled=True)]
  transfers between devices with their start and end apart: 6 -> 6, of which waited for: 4 -> 5; matrix products, arithmetic and copies ran while one was open for 24% -> 18% of each run, Pallas kernels for 0% -> 0%
where the time goes in v8:
time: 159 us; the launch traced here: 158 us
  waiting for transfers between devices  77.1 us (48%)
  other arithmetic  26.7 us (17%)
  starting transfers between devices  26.4 us (17%)
  local copies, waits for them, and re-layouts  21.7 us (14%)
  matrix products  5.69 us (4%)
    ppermute x4, waiting for transfers between devices, exchange(): received = lax.ppermute(jnp.where(low, blocks[1], blocks[0]), axis, pairs)  44.6 us
    all_to_all x1, waiting for transfers between devices, local(): blocks = lax.all_to_all(blocks, 'tm', 0, 0, tiled=True)  18.6 us
    reshape x1, local copies, waits for them, and re-layouts, local(): weights = beam_weights.reshape(per_group, feeds_here * 2, n_feed, per_out)  14.1 us
    all_to_all x1, waiting for transfers between devices, local(): turned = lax.all_to_all(spectra, 'tm', 0, 0, tiled=True)  13.8 us
    all_to_all x1, starting transfers between devices, local(): blocks = lax.all_to_all(blocks, 'tm', 0, 0, tiled=True)  12.6 us
    transpose x1, other arithmetic, local(): filtered = jnp.transpose(filtered, (1, 0, 2))  9.2 us
    ppermute x4, starting transfers between devices, exchange(): received = lax.ppermute(jnp.where(low, blocks[1], blocks[0]), axis, pairs)  7.93 us
    convert_element_type x1, other arithmetic, dft_rows(): return table.reshape(cols, frame_len).astype(jnp.bfloat16)  6.17 us
  transfers between devices with their start and end apart: 6, of which 5 were waited for; matrix products, arithmetic and copies ran while one was open for 18% of the time, Pallas kernels for 0%

profile of v8, /device:TPU:1, one launch (start us, length us, event | category | flops | bytes accessed | tf_op | source)
XLA Modules:
  0.0 157.9 jit_solution(2851585873509720760)
XLA Ops:
  0.0 0.0 copy-start.2
  0.0 2.3 %reshape.432 = bf16[64,4,2048]{2,1,0:T(4,128)(2,1)} reshape(bf16[256,2048]{1,0:T(8,128)(2,1)} %param.3) | data formatting | bytes 2097152 | tf_op jit(solution)/shard_map/reshape | solution.py:67
  2.3 12.6 %all-to-all-start = ((bf16[64,4,2048]{2,1,0:T(4,128)(2,1)}), bf16[64,4,2048]{2,1,0:T(4,128)(2,1)S(1)}, u32[]{:S(2)}, u32[]{:S(2)}) async-start(bf16[64,4,2048]{2,1,0:T(4,128)(2,1)} %reshape.432), calls=%async_computation | async-start | bytes 2097152 | tf_op jit(solution)/shard_map/all_to_all | solution.py:68
  14.9 0.0 copy-done.2
  14.9 0.1 fusion.65
  15.0 1.1 negate_select_fusion.3
  16.2 2.0 %fusion.40 = (f32[2048,64]{0,1:T(8,128)S(1)}, f32[2048,64]{0,1:T(8,128)S(1)}) fusion(s32[2048]{0:T(1024)S(1)} %fusion.52), kind=kLoop, calls=%fused_computation.77 | loop fusion | flops 1835008 | bytes 1056768 | tf_op jit(solution)/shard_map/cos | solution.py:30
  18.2 6.2 %multiply_convert_fusion = bf16[2048,32,64]{0,2,1:T(8,128)(2,1)} fusion(f32[2048,64]{0,1:T(8,128)S(1)} %get-tuple-element.34, f32[2048,32]{0,1:T(8,128)S(1)} %get-tuple-element.32, f32[2048,64]{0,1:T(8,128)S(1)} %get-tuple-element.33, f32[2048,32]{0,1:T(8,128)S(1)} %get-tuple-element.31), kind=kLoop, calls=%fused_computation | loop fusion | flops 20971520 | bytes 9961472 | tf_op jit(solution)/shard_map/convert_element_type | solution.py:36
  24.4 18.6 %all-to-all-done = bf16[64,4,2048]{2,1,0:T(4,128)(2,1)S(1)} async-done(((bf16[64,4,2048]{2,1,0:T(4,128)(2,1)}), bf16[64,4,2048]{2,1,0:T(4,128)(2,1)S(1)}, u32[]{:S(2)}, u32[]{:S(2)}) %all-to-all-start) | async-done | bytes 1048608 | tf_op jit(solution)/shard_map/all_to_all | solution.py:68
  43.0 0.6 pad_convert_fusion
  43.6 0.0 slice-start.1
  43.7 9.2 %fusion.25 = bf16[4,64,2048]{2,0,1:T(4,128)(2,1)S(1)} fusion(f32[79,4,2048]{2,1,0:T(4,128)S(1)} %pad_convert_fusion, f32[2048]{0:T(1024)S(1)} %bitcast.108, f32[2048]{0:T(1024)S(1)} %bitcast.109, f32[2048]{0:T(1024)S(1)} %bitcast.95, f32[2048]{0:T(1024)S(1)} %bitcast.96, f32[2048]{0:T(1024)S(1)} %bitcast.97, f32[2048]{0:T(1024)S(1)} %bitcast.98, ...), kind=kLoop, calls=%fused_computation.48 | loop fusion | flops 16777216 | bytes 34734080 | tf_op jit(solution)/shard_map/transpose | solution.py:75
  52.9 0.6 copy.46
  53.4 0.0 slice-done
  53.5 0.0 slice-done.1
  53.5 3.6 %convolution_convert_fusion = bf16[2048,256]{1,0:T(8,128)(2,1)} fusion(bf16[2048,2048]{0,1:T(8,128)(2,1)S(1)} %bitcast.87, bf16[256,2048]{1,0:T(8,128)(2,1)S(1)} %bitcast.93), kind=kOutput, calls=%fused_computation.3 | convolution fusion | flops 2148007936 | bytes 10485760 | tf_op jit(solution)/shard_map/jk,mk->jm/dot_general | solution.py:78
  57.1 5.9 %all-to-all-start.1 = ((bf16[64,32,256]{2,1,0:T(8,128)(2,1)}), bf16[64,32,256]{2,1,0:T(8,128)(2,1)S(1)}, u32[]{:S(2)}, u32[]{:S(2)}) async-start(bf16[64,32,256]{2,1,0:T(8,128)(2,1)} %bitcast.19), calls=%async_computation.1 | async-start | bytes 2097152 | tf_op jit(solution)/shard_map/all_to_all | solution.py:88
  63.0 14.1 %reshape.438 = bf16[16,512,4,128]{3,2,1,0:T(4,128)(2,1)} reshape(bf16[16,256,2,512]{3,2,1,0:T(2,128)(2,1)} %param.5) | data formatting | bytes 16777216 | tf_op jit(solution)/shard_map/reshape | solution.py:99
  77.1 13.8 %all-to-all-done.1 = bf16[64,32,256]{2,1,0:T(8,128)(2,1)S(1)} async-done(((bf16[64,32,256]{2,1,0:T(8,128)(2,1)}), bf16[64,32,256]{2,1,0:T(8,128)(2,1)S(1)}, u32[]{:S(2)}, u32[]{:S(2)}) %all-to-all-start.1) | async-done | bytes 1048608 | tf_op jit(solution)/shard_map/all_to_all | solution.py:88
  90.9 0.8 reshape.435
  91.8 0.6 copy.47
  92.4 0.0 copy-start
  92.4 0.3 slice_negate_fusion
  92.7 1.2 maximum_maximum_fusion
  93.8 1.9 %copy-done = bf16[16,512,4,128]{3,2,1,0:T(4,128)(2,1)S(1)} copy-done((bf16[16,512,4,128]{3,2,1,0:T(4,128)(2,1)S(1)}, bf16[16,512,4,128]{3,2,1,0:T(4,128)(2,1)}, u32[]{:S(2)}) %copy-start) | copy-done | bytes 8388632
  95.8 2.0 %fusion.2 = f32[4,16,128,128]{2,3,0,1:T(8,128)S(1)} fusion(bf16[16,512,4,128]{3,2,1,0:T(4,128)(2,1)S(1)} %copy-done, bf16[16,512,128,1]{2,0,1,3:T(8,128)(2,1)S(1)} %bitcast.84), kind=kOutput, calls=%fused_computation.4 | convolution fusion | flops 1073741824 | bytes 14680064 | tf_op jit(solution)/shard_map/ckjb,ckn->jcbn/dot_general | solution.py:100
  97.8 0.5 fusion.62
  98.3 0.1 fusion.63
  98.5 1.1 select_bitcast_fusion.1
  99.6 2.4 %collective-permute-start = (f32[2,8,128,128]{2,3,1,0:T(8,128)}, f32[2,8,128,128]{2,3,1,0:T(8,128)}, u32[]{:S(2)}, u32[]{:S(2)}) collective-permute-start(f32[2,8,128,128]{2,3,1,0:T(8,128)} %select_bitcast_fusion.1), channel_id=1, source_target_pairs={{0,1},{1,0},{2,3},{3,2},{4,5},{5,4},{6,7},{7,6},{8,9},{9,8},{10,11... | collective-permute-start | bytes 3145736 | tf_op jit(solution)/shard_map/ppermute | solution.py:54
  102.0 1.7 %fusion.64 = (f32[2,1,8,128,128]{3,4,1,0,2:T(8,128)S(1)}, f32[2,8,128,128]{2,3,0,1:T(8,128)}, f32[2,1,8,128,128]{3,4,1,0,2:T(8,128)}) fusion(f32[2,2,8,128,128]{3,4,1,0,2:T(8,128)S(1)} %bitcast.89, pred[]{:T(512)S(6)} %eq.30), kind=kLoop, calls=%fused_computation.117 | loop fusion | flops 262144 | bytes 5242881 | tf_op jit(solution)/shard_map/slice | solution.py:109
  103.7 0.0 collective-permute-start.2
  103.7 0.9 collective-permute-done
  104.6 1.4 fusion.23
  106.0 0.1 select_bitcast_fusion.3
  106.1 4.3 %collective-permute-start.1 = (f32[1,8,128,128]{2,3,1,0:T(8,128)S(1)}, f32[1,8,128,128]{2,3,1,0:T(8,128)S(1)}, u32[]{:S(2)}, u32[]{:S(2)}) collective-permute-start(f32[1,8,128,128]{2,3,1,0:T(8,128)S(1)} %select_bitcast_fusion.3), channel_id=1, source_target_pairs={{0,2},{1,3},{2,0},{3,1},{4,6},{5,7},{6,4},{7,5},{8,10},{9,11},{10,... | collective-permute-start | bytes 1572872 | tf_op jit(solution)/shard_map/ppermute | solution.py:54
  110.4 0.0 collective-permute-done.2
  110.4 0.0 copy-done.1
  110.4 1.4 fusion.24
  111.8 0.1 select_bitcast_fusion.2
  111.9 1.2 collective-permute-start.3
  113.1 26.8 %collective-permute-done.1 = f32[1,8,128,128]{2,3,1,0:T(8,128)S(1)} collective-permute-done((f32[1,8,128,128]{2,3,1,0:T(8,128)S(1)}, f32[1,8,128,128]{2,3,1,0:T(8,128)S(1)}, u32[]{:S(2)}, u32[]{:S(2)}) %collective-permute-start.1) | collective-permute-done | bytes 524320 | tf_op jit(solution)/shard_map/ppermute | solution.py:54
  139.9 0.1 fusion.32
  140.1 0.1 bitcast_reduce_fusion.1
  140.2 16.8 %collective-permute-done.3 = f32[1,8,128,128]{2,3,1,0:T(8,128)S(1)} collective-permute-done((f32[1,8,128,128]{2,3,1,0:T(8,128)S(1)}, f32[1,8,128,128]{2,3,1,0:T(8,128)S(1)}, u32[]{:S(2)}, u32[]{:S(2)}) %collective-permute-start.3) | collective-permute-done | bytes 524320 | tf_op jit(solution)/shard_map/ppermute | solution.py:54
  157.0 0.1 fusion.31
  157.1 0.1 bitcast_reduce_fusion
  157.3 0.6 copy.61
  (10 shorter events, 0.1 us)
Async XLA Ops:
  0.0 14.9 %copy-start.2 = (f32[16,2048]{1,0:T(8,128)S(1)}, f32[16,2048]{1,0:T(8,128)}, u32[]{:S(2)}) copy-start(f32[16,2048]{1,0:T(8,128)} %param.4) | copy-start | bytes 393220
  2.3 40.7 %all-to-all-start = ((bf16[64,4,2048]{2,1,0:T(4,128)(2,1)}), bf16[64,4,2048]{2,1,0:T(4,128)(2,1)S(1)}, u32[]{:S(2)}, u32[]{:S(2)}) async-start(bf16[64,4,2048]{2,1,0:T(4,128)(2,1)} %reshape.432), calls=%async_computation | async-start | bytes 2097152 | tf_op jit(solution)/shard_map/all_to_all | solution.py:68
  43.0 10.4 %slice-start = ((s8[8388608]{0:T(1024)(128)(4,1)}), s8[4194304]{0:T(1024)(128)(4,1)S(1)}, s32[]{:S(2)}) async-start(s8[8388608]{0:T(1024)(128)(4,1)} %bitcast.85), calls=%async_computation.2 | async-start | bytes 8388608
  43.6 9.8 %slice-start.1 = ((s8[8388608]{0:T(1024)(128)(4,1)}), s8[4194304]{0:T(1024)(128)(4,1)S(1)}, s32[]{:S(2)}) async-start(s8[8388608]{0:T(1024)(128)(4,1)} %bitcast.85), calls=%async_computation.3 | async-start | bytes 8388608
  57.1 33.8 %all-to-all-start.1 = ((bf16[64,32,256]{2,1,0:T(8,128)(2,1)}), bf16[64,32,256]{2,1,0:T(8,128)(2,1)S(1)}, u32[]{:S(2)}, u32[]{:S(2)}) async-start(bf16[64,32,256]{2,1,0:T(8,128)(2,1)} %bitcast.19), calls=%async_computation.1 | async-start | bytes 2097152 | tf_op jit(solution)/shard_map/all_to_all | solution.py:88
  92.4 3.4 %copy-start = (bf16[16,512,4,128]{3,2,1,0:T(4,128)(2,1)S(1)}, bf16[16,512,4,128]{3,2,1,0:T(4,128)(2,1)}, u32[]{:S(2)}) copy-start(bf16[16,512,4,128]{3,2,1,0:T(4,128)(2,1)} %reshape.438) | copy-start | bytes 25165828
  99.6 5.0 %collective-permute-start = (f32[2,8,128,128]{2,3,1,0:T(8,128)}, f32[2,8,128,128]{2,3,1,0:T(8,128)}, u32[]{:S(2)}, u32[]{:S(2)}) collective-permute-start(f32[2,8,128,128]{2,3,1,0:T(8,128)} %select_bitcast_fusion.1), channel_id=1, source_target_pairs={{0,1},{1,0},{2,3},{3,2},{4,5},{5,4},{6,7},{7,6},{8,9},{9,8},{10,11... | collective-permute-start | bytes 3145736 | tf_op jit(solution)/shard_map/ppermute | solution.py:54
  103.7 6.7 %collective-permute-start.2 = (f32[2,8,128,128]{2,3,0,1:T(8,128)}, f32[2,8,128,128]{2,3,0,1:T(8,128)}, u32[]{:S(2)}, u32[]{:S(2)}) collective-permute-start(f32[2,8,128,128]{2,3,0,1:T(8,128)} %get-tuple-element.10), channel_id=1, source_target_pairs={{0,1},{1,0},{2,3},{3,2},{4,5},{5,4},{6,7},{7,6},{8,9},{9,8},{10,11... | collective-permute-start | bytes 3145736 | tf_op jit(solution)/shard_map/ppermute | solution.py:54
  103.7 6.7 %copy-start.1 = (f32[2,1,8,128,128]{3,4,1,0,2:T(8,128)S(1)}, f32[2,1,8,128,128]{3,4,1,0,2:T(8,128)}, u32[]{:S(2)}) copy-start(f32[2,1,8,128,128]{3,4,1,0,2:T(8,128)} %get-tuple-element.11) | copy-start | bytes 3145732
  106.1 33.9 %collective-permute-start.1 = (f32[1,8,128,128]{2,3,1,0:T(8,128)S(1)}, f32[1,8,128,128]{2,3,1,0:T(8,128)S(1)}, u32[]{:S(2)}, u32[]{:S(2)}) collective-permute-start(f32[1,8,128,128]{2,3,1,0:T(8,128)S(1)} %select_bitcast_fusion.3), channel_id=1, source_target_pairs={{0,2},{1,3},{2,0},{3,1},{4,6},{5,7},{6,4},{7,5},{8,10},{9,11},{10,... | collective-permute-start | bytes 1572872 | tf_op jit(solution)/shard_map/ppermute | solution.py:54
  111.9 45.2 %collective-permute-start.3 = (f32[1,8,128,128]{2,3,1,0:T(8,128)S(1)}, f32[1,8,128,128]{2,3,1,0:T(8,128)S(1)}, u32[]{:S(2)}, u32[]{:S(2)}) collective-permute-start(f32[1,8,128,128]{2,3,1,0:T(8,128)S(1)} %select_bitcast_fusion.2), channel_id=1, source_target_pairs={{0,2},{1,3},{2,0},{3,1},{4,6},{5,7},{6,4},{7,5},{8,10},{9,11},{10,... | collective-permute-start | bytes 1572872 | tf_op jit(solution)/shard_map/ppermute | solution.py:54

commit v9 on v8

--- a/solution.py
+++ b/solution.py
@@ -66,6 +66,9 @@
 
     blocks = voltages.reshape(n_tm, per_dev, samples)
     blocks = lax.all_to_all(blocks, "tm", 0, 0, tiled=True)
+    per_out = beam_weights.shape[3] // n_feed
+    weights = beam_weights.reshape(beam_weights.shape[0], feeds_here * 2, n_feed, per_out)
+    blocks, weights = lax.optimization_barrier((blocks, weights))
     frames = jnp.transpose(
         blocks.reshape(n_tm, per_dev, frames_here, frame_len), (0, 2, 1, 3)
     ).reshape(total_frames, per_dev, frame_len)
@@ -95,8 +98,6 @@
     paired = jnp.concatenate([for_real, for_imag], axis=3).reshape(
         per_group, feeds_here * 2, 2 * total_frames
     )
-    per_out = beam_weights.shape[3] // n_feed
-    weights = beam_weights.reshape(per_group, feeds_here * 2, n_feed, per_out)
     beams_all = jnp.einsum("ckjb,ckn->jcbn", weights, paired, preferred_element_type=jnp.float32)
     n_parts = 2
     per_part = per_group // n_parts

time: 159 us -> 160 us (level)
  matrix products: 5.69 us -> 9.08 us
  local copies, waits for them, and re-layouts: 21.7 us -> 19.6 us
    all_to_all x1, waiting for transfers between devices: 18.6 us -> 4.47 us  [local(): blocks = lax.all_to_all(blocks, 'tm', 0, 0, tiled=True)]
    all_to_all x1, waiting for transfers between devices: 13.8 us -> 27.9 us  [local(): turned = lax.all_to_all(spectra, 'tm', 0, 0, tiled=True)]
    dot_general x1, matrix products: 2.05 us -> 5.44 us  [local(): jnp.einsum('ckjb,ckn->jcbn', weights, paired, preferred_element_type=jnp....]
    unnamed x10 -> x8, local copies, waits for them, and re-layouts: 1.96 us -> 0.02 us
where the time goes in v9:
time: 160 us; the launch traced here: 159 us
  waiting for transfers between devices  77.1 us (48%)
  other arithmetic  26.7 us (17%)
  starting transfers between devices  26.4 us (16%)
  local copies, waits for them, and re-layouts  19.6 us (12%)
  matrix products  9.08 us (6%)
    ppermute x4, waiting for transfers between devices, exchange(): received = lax.ppermute(jnp.where(low, blocks[1], blocks[0]), axis, pairs)  44.7 us
    all_to_all x1, waiting for transfers between devices, local(): turned = lax.all_to_all(spectra, 'tm', 0, 0, tiled=True)  27.9 us
    reshape x1, local copies, waits for them, and re-layouts, local(): beam_weights.reshape(beam_weights.shape[0], feeds_here * 2, n_feed, per_out)  14.1 us
    all_to_all x1, starting transfers between devices, local(): blocks = lax.all_to_all(blocks, 'tm', 0, 0, tiled=True)  12.6 us
    transpose x1, other arithmetic, local(): filtered = jnp.transpose(filtered, (1, 0, 2))  9.2 us
    ppermute x4, starting transfers between devices, exchange(): received = lax.ppermute(jnp.where(low, blocks[1], blocks[0]), axis, pairs)  7.94 us
    convert_element_type x1, other arithmetic, dft_rows(): return table.reshape(cols, frame_len).astype(jnp.bfloat16)  6.19 us
    all_to_all x1, starting transfers between devices, local(): turned = lax.all_to_all(spectra, 'tm', 0, 0, tiled=True)  5.9 us
  transfers between devices with their start and end apart: 6, of which 5 were waited for; matrix products, arithmetic and copies ran while one was open for 18% of the time, Pallas kernels for 0%

profile of v9, /device:TPU:1, one launch (start us, length us, event | category | flops | bytes accessed | tf_op | source)
XLA Modules:
  0.0 159.1 jit_solution(8103521286897249147)
XLA Ops:
  0.0 2.2 %reshape.432 = bf16[64,4,2048]{2,1,0:T(4,128)(2,1)} reshape(bf16[256,2048]{1,0:T(8,128)(2,1)} %param.3) | data formatting | bytes 2097152 | tf_op jit(solution)/shard_map/reshape | solution.py:67
  2.2 12.6 %all-to-all-start = ((bf16[64,4,2048]{2,1,0:T(4,128)(2,1)}), bf16[64,4,2048]{2,1,0:T(4,128)(2,1)S(1)}, u32[]{:S(2)}, u32[]{:S(2)}) async-start(bf16[64,4,2048]{2,1,0:T(4,128)(2,1)} %reshape.432), calls=%async_computation | async-start | bytes 2097152 | tf_op jit(solution)/shard_map/all_to_all | solution.py:68
  14.8 0.0 copy-start.1
  14.8 14.1 %reshape.433 = bf16[16,512,4,128]{3,2,1,0:T(4,128)(2,1)} reshape(bf16[16,256,2,512]{3,2,1,0:T(2,128)(2,1)} %param.5) | data formatting | bytes 16777216 | tf_op jit(solution)/shard_map/reshape | solution.py:70
  28.9 0.0 copy-done.1
  29.0 0.1 fusion.65
  29.0 1.1 negate_select_fusion.3
  30.2 2.0 %fusion.40 = (f32[2048,64]{0,1:T(8,128)S(1)}, f32[2048,64]{0,1:T(8,128)S(1)}) fusion(s32[2048]{0:T(1024)S(1)} %fusion.52), kind=kLoop, calls=%fused_computation.77 | loop fusion | flops 1835008 | bytes 1056768 | tf_op jit(solution)/shard_map/cos | solution.py:30
  32.2 6.2 %multiply_convert_fusion = bf16[2048,32,64]{0,2,1:T(8,128)(2,1)} fusion(f32[2048,64]{0,1:T(8,128)S(1)} %get-tuple-element.38, f32[2048,32]{0,1:T(8,128)S(1)} %get-tuple-element.36, f32[2048,64]{0,1:T(8,128)S(1)} %get-tuple-element.37, f32[2048,32]{0,1:T(8,128)S(1)} %get-tuple-element.35), kind=kLoop, calls=%fused_computation | loop fusion | flops 20971520 | bytes 9961472 | tf_op jit(solution)/shard_map/convert_element_type | solution.py:36
  38.4 4.5 %all-to-all-done = bf16[64,4,2048]{2,1,0:T(4,128)(2,1)S(1)} async-done(((bf16[64,4,2048]{2,1,0:T(4,128)(2,1)}), bf16[64,4,2048]{2,1,0:T(4,128)(2,1)S(1)}, u32[]{:S(2)}, u32[]{:S(2)}) %all-to-all-start) | async-done | bytes 1048608 | tf_op jit(solution)/shard_map/all_to_all | solution.py:68
  42.9 0.0 slice-start
  42.9 0.6 pad_convert_fusion
  43.5 0.0 slice-start.1
  43.5 9.2 %fusion.25 = bf16[4,64,2048]{2,0,1:T(4,128)(2,1)S(1)} fusion(f32[79,4,2048]{2,1,0:T(4,128)S(1)} %pad_convert_fusion, f32[2048]{0:T(1024)S(1)} %bitcast.108, f32[2048]{0:T(1024)S(1)} %bitcast.109, f32[2048]{0:T(1024)S(1)} %bitcast.95, f32[2048]{0:T(1024)S(1)} %bitcast.96, f32[2048]{0:T(1024)S(1)} %bitcast.97, f32[2048]{0:T(1024)S(1)} %bitcast.98, ...), kind=kLoop, calls=%fused_computation.48 | loop fusion | flops 16777216 | bytes 34734080 | tf_op jit(solution)/shard_map/transpose | solution.py:78
  52.7 0.6 copy.46
  53.3 0.0 slice-done
  53.3 0.0 slice-done.1
  53.4 3.6 %convolution_convert_fusion = bf16[2048,256]{1,0:T(8,128)(2,1)} fusion(bf16[2048,2048]{0,1:T(8,128)(2,1)S(1)} %bitcast.87, bf16[256,2048]{1,0:T(8,128)(2,1)S(1)} %bitcast.93), kind=kOutput, calls=%fused_computation.3 | convolution fusion | flops 2148007936 | bytes 10485760 | tf_op jit(solution)/shard_map/jk,mk->jm/dot_general | solution.py:81
  57.0 5.9 %all-to-all-start.1 = ((bf16[64,32,256]{2,1,0:T(8,128)(2,1)}), bf16[64,32,256]{2,1,0:T(8,128)(2,1)S(1)}, u32[]{:S(2)}, u32[]{:S(2)}) async-start(bf16[64,32,256]{2,1,0:T(8,128)(2,1)} %bitcast.19), calls=%async_computation.1 | async-start | bytes 2097152 | tf_op jit(solution)/shard_map/all_to_all | solution.py:91
  62.9 27.9 %all-to-all-done.1 = bf16[64,32,256]{2,1,0:T(8,128)(2,1)S(1)} async-done(((bf16[64,32,256]{2,1,0:T(8,128)(2,1)}), bf16[64,32,256]{2,1,0:T(8,128)(2,1)S(1)}, u32[]{:S(2)}, u32[]{:S(2)}) %all-to-all-start.1) | async-done | bytes 1048608 | tf_op jit(solution)/shard_map/all_to_all | solution.py:91
  90.8 0.8 reshape.436
  91.7 0.6 copy.47
  92.3 0.3 slice_negate_fusion
  92.6 1.2 maximum_maximum_fusion
  93.7 5.4 %fusion.2 = f32[4,16,128,128]{2,3,0,1:T(8,128)S(1)} fusion(bf16[16,512,4,128]{3,2,1,0:T(4,128)(2,1)} %reshape.433, bf16[16,512,128,1]{2,0,1,3:T(8,128)(2,1)S(1)} %bitcast.84), kind=kOutput, calls=%fused_computation.4 | convolution fusion | flops 1073741824 | bytes 14680064 | tf_op jit(solution)/shard_map/ckjb,ckn->jcbn/dot_general | solution.py:101
  99.2 0.3 fusion.62
  99.5 0.2 fusion.63
  99.7 1.1 select_bitcast_fusion.1
  100.8 2.4 %collective-permute-start = (f32[2,8,128,128]{2,3,1,0:T(8,128)}, f32[2,8,128,128]{2,3,1,0:T(8,128)}, u32[]{:S(2)}, u32[]{:S(2)}) collective-permute-start(f32[2,8,128,128]{2,3,1,0:T(8,128)} %select_bitcast_fusion.1), channel_id=1, source_target_pairs={{0,1},{1,0},{2,3},{3,2},{4,5},{5,4},{6,7},{7,6},{8,9},{9,8},{10,11... | collective-permute-start | bytes 3145736 | tf_op jit(solution)/shard_map/ppermute | solution.py:54
  103.2 1.7 %fusion.64 = (f32[2,1,8,128,128]{3,4,1,0,2:T(8,128)S(1)}, f32[2,8,128,128]{2,3,0,1:T(8,128)}, f32[2,1,8,128,128]{3,4,1,0,2:T(8,128)}) fusion(f32[2,2,8,128,128]{3,4,1,0,2:T(8,128)S(1)} %bitcast.89, pred[]{:T(512)S(6)} %eq.30), kind=kLoop, calls=%fused_computation.117 | loop fusion | flops 262144 | bytes 5242881 | tf_op jit(solution)/shard_map/slice | solution.py:110
  104.8 0.0 collective-permute-start.2
  104.9 0.0 copy-start
  104.9 0.9 collective-permute-done
  105.8 1.4 fusion.23
  107.2 0.1 select_bitcast_fusion.3
  107.3 4.3 %collective-permute-start.1 = (f32[1,8,128,128]{2,3,1,0:T(8,128)S(1)}, f32[1,8,128,128]{2,3,1,0:T(8,128)S(1)}, u32[]{:S(2)}, u32[]{:S(2)}) collective-permute-start(f32[1,8,128,128]{2,3,1,0:T(8,128)S(1)} %select_bitcast_fusion.3), channel_id=1, source_target_pairs={{0,2},{1,3},{2,0},{3,1},{4,6},{5,7},{6,4},{7,5},{8,10},{9,11},{10,... | collective-permute-start | bytes 1572872 | tf_op jit(solution)/shard_map/ppermute | solution.py:54
  111.6 0.0 collective-permute-done.2
  111.6 0.0 copy-done
  111.6 1.4 fusion.24
  113.0 0.1 select_bitcast_fusion.2
  113.0 1.2 collective-permute-start.3
  114.3 26.9 %collective-permute-done.1 = f32[1,8,128,128]{2,3,1,0:T(8,128)S(1)} collective-permute-done((f32[1,8,128,128]{2,3,1,0:T(8,128)S(1)}, f32[1,8,128,128]{2,3,1,0:T(8,128)S(1)}, u32[]{:S(2)}, u32[]{:S(2)}) %collective-permute-start.1) | collective-permute-done | bytes 524320 | tf_op jit(solution)/shard_map/ppermute | solution.py:54
  141.2 0.1 fusion.32
  141.3 0.1 bitcast_reduce_fusion.1
  141.4 16.8 %collective-permute-done.3 = f32[1,8,128,128]{2,3,1,0:T(8,128)S(1)} collective-permute-done((f32[1,8,128,128]{2,3,1,0:T(8,128)S(1)}, f32[1,8,128,128]{2,3,1,0:T(8,128)S(1)}, u32[]{:S(2)}, u32[]{:S(2)}) %collective-permute-start.3) | collective-permute-done | bytes 524320 | tf_op jit(solution)/shard_map/ppermute | solution.py:54
  158.3 0.1 fusion.31
  158.4 0.1 bitcast_reduce_fusion
  158.5 0.6 copy.61
  (8 shorter events, 0.1 us)
Async XLA Ops:
  2.2 40.7 %all-to-all-start = ((bf16[64,4,2048]{2,1,0:T(4,128)(2,1)}), bf16[64,4,2048]{2,1,0:T(4,128)(2,1)S(1)}, u32[]{:S(2)}, u32[]{:S(2)}) async-start(bf16[64,4,2048]{2,1,0:T(4,128)(2,1)} %reshape.432), calls=%async_computation | async-start | bytes 2097152 | tf_op jit(solution)/shard_map/all_to_all | solution.py:68
  14.8 14.1 %copy-start.1 = (f32[16,2048]{1,0:T(8,128)S(1)}, f32[16,2048]{1,0:T(8,128)}, u32[]{:S(2)}) copy-start(f32[16,2048]{1,0:T(8,128)} %param.4) | copy-start | bytes 393220
  42.9 10.4 %slice-start = ((s8[8388608]{0:T(1024)(128)(4,1)}), s8[4194304]{0:T(1024)(128)(4,1)S(1)}, s32[]{:S(2)}) async-start(s8[8388608]{0:T(1024)(128)(4,1)} %bitcast.85), calls=%async_computation.2 | async-start | bytes 8388608
  43.5 9.8 %slice-start.1 = ((s8[8388608]{0:T(1024)(128)(4,1)}), s8[4194304]{0:T(1024)(128)(4,1)S(1)}, s32[]{:S(2)}) async-start(s8[8388608]{0:T(1024)(128)(4,1)} %bitcast.85), calls=%async_computation.3 | async-start | bytes 8388608
  57.0 33.8 %all-to-all-start.1 = ((bf16[64,32,256]{2,1,0:T(8,128)(2,1)}), bf16[64,32,256]{2,1,0:T(8,128)(2,1)S(1)}, u32[]{:S(2)}, u32[]{:S(2)}) async-start(bf16[64,32,256]{2,1,0:T(8,128)(2,1)} %bitcast.19), calls=%async_computation.1 | async-start | bytes 2097152 | tf_op jit(solution)/shard_map/all_to_all | solution.py:91
  100.8 5.0 %collective-permute-start = (f32[2,8,128,128]{2,3,1,0:T(8,128)}, f32[2,8,128,128]{2,3,1,0:T(8,128)}, u32[]{:S(2)}, u32[]{:S(2)}) collective-permute-start(f32[2,8,128,128]{2,3,1,0:T(8,128)} %select_bitcast_fusion.1), channel_id=1, source_target_pairs={{0,1},{1,0},{2,3},{3,2},{4,5},{5,4},{6,7},{7,6},{8,9},{9,8},{10,11... | collective-permute-start | bytes 3145736 | tf_op jit(solution)/shard_map/ppermute | solution.py:54
  104.8 6.7 %collective-permute-start.2 = (f32[2,8,128,128]{2,3,0,1:T(8,128)}, f32[2,8,128,128]{2,3,0,1:T(8,128)}, u32[]{:S(2)}, u32[]{:S(2)}) collective-permute-start(f32[2,8,128,128]{2,3,0,1:T(8,128)} %get-tuple-element.14), channel_id=1, source_target_pairs={{0,1},{1,0},{2,3},{3,2},{4,5},{5,4},{6,7},{7,6},{8,9},{9,8},{10,11... | collective-permute-start | bytes 3145736 | tf_op jit(solution)/shard_map/ppermute | solution.py:54
  104.9 6.7 %copy-start = (f32[2,1,8,128,128]{3,4,1,0,2:T(8,128)S(1)}, f32[2,1,8,128,128]{3,4,1,0,2:T(8,128)}, u32[]{:S(2)}) copy-start(f32[2,1,8,128,128]{3,4,1,0,2:T(8,128)} %get-tuple-element.15) | copy-start | bytes 3145732
  107.3 33.9 %collective-permute-start.1 = (f32[1,8,128,128]{2,3,1,0:T(8,128)S(1)}, f32[1,8,128,128]{2,3,1,0:T(8,128)S(1)}, u32[]{:S(2)}, u32[]{:S(2)}) collective-permute-start(f32[1,8,128,128]{2,3,1,0:T(8,128)S(1)} %select_bitcast_fusion.3), channel_id=1, source_target_pairs={{0,2},{1,3},{2,0},{3,1},{4,6},{5,7},{6,4},{7,5},{8,10},{9,11},{10,... | collective-permute-start | bytes 1572872 | tf_op jit(solution)/shard_map/ppermute | solution.py:54
  113.0 45.2 %collective-permute-start.3 = (f32[1,8,128,128]{2,3,1,0:T(8,128)S(1)}, f32[1,8,128,128]{2,3,1,0:T(8,128)S(1)}, u32[]{:S(2)}, u32[]{:S(2)}) collective-permute-start(f32[1,8,128,128]{2,3,1,0:T(8,128)S(1)} %select_bitcast_fusion.2), channel_id=1, source_target_pairs={{0,2},{1,3},{2,0},{3,1},{4,6},{5,7},{6,4},{7,5},{8,10},{9,11},{10,... | collective-permute-start | bytes 1572872 | tf_op jit(solution)/shard_map/ppermute | solution.py:54

commit v10 on v8

--- a/solution.py
+++ b/solution.py
@@ -98,7 +98,7 @@
     per_out = beam_weights.shape[3] // n_feed
     weights = beam_weights.reshape(per_group, feeds_here * 2, n_feed, per_out)
     beams_all = jnp.einsum("ckjb,ckn->jcbn", weights, paired, preferred_element_type=jnp.float32)
-    n_parts = 2
+    n_parts = 4
     per_part = per_group // n_parts
     binned_parts = []
     for part in range(n_parts):

time: 159 us -> 155 us (0.975)
  starting transfers between devices: 26.4 us -> 32.8 us
  waiting for transfers between devices: 77.1 us -> 71.9 us
  other arithmetic: 26.7 us -> 21.8 us
    ppermute x4 -> x8, starting transfers between devices: 7.93 us -> 14.4 us  [exchange(): received = lax.ppermute(jnp.where(low, blocks[1], blocks[0]), axis, pairs)]
    ppermute x4 -> x8, waiting for transfers between devices: 44.6 us -> 39.5 us  [exchange(): received = lax.ppermute(jnp.where(low, blocks[1], blocks[0]), axis, pairs)]
    reshape x2 -> x4, other arithmetic: 2.8 us -> 0.32 us  [local(): split = beams.reshape(-1, 2, *beams.shape[1:])]
  transfers between devices with their start and end apart: 6 -> 10, of which waited for: 5 -> 7; matrix products, arithmetic and copies ran while one was open for 18% -> 16% of each run, Pallas kernels for 0% -> 0%
where the time goes in v10:
time: 155 us; the launch traced here: 154 us
  waiting for transfers between devices  71.9 us (46%)
  starting transfers between devices  32.8 us (21%)
  other arithmetic  21.8 us (14%)
  local copies, waits for them, and re-layouts  21.7 us (14%)
  matrix products  5.66 us (4%)
    ppermute x8, waiting for transfers between devices, exchange(): received = lax.ppermute(jnp.where(low, blocks[1], blocks[0]), axis, pairs)  39.5 us
    all_to_all x1, waiting for transfers between devices, local(): blocks = lax.all_to_all(blocks, 'tm', 0, 0, tiled=True)  18.6 us
    ppermute x8, starting transfers between devices, exchange(): received = lax.ppermute(jnp.where(low, blocks[1], blocks[0]), axis, pairs)  14.4 us
    reshape x1, local copies, waits for them, and re-layouts, local(): weights = beam_weights.reshape(per_group, feeds_here * 2, n_feed, per_out)  14 us
    all_to_all x1, waiting for transfers between devices, local(): turned = lax.all_to_all(spectra, 'tm', 0, 0, tiled=True)  13.8 us
    all_to_all x1, starting transfers between devices, local(): blocks = lax.all_to_all(blocks, 'tm', 0, 0, tiled=True)  12.6 us
    transpose x1, other arithmetic, local(): filtered = jnp.transpose(filtered, (1, 0, 2))  9.2 us
    convert_element_type x1, other arithmetic, dft_rows(): return table.reshape(cols, frame_len).astype(jnp.bfloat16)  6.18 us
  transfers between devices with their start and end apart: 10, of which 7 were waited for; matrix products, arithmetic and copies ran while one was open for 16% of the time, Pallas kernels for 0%

profile of v10, /device:TPU:1, one launch (start us, length us, event | category | flops | bytes accessed | tf_op | source)
XLA Modules:
  0.0 154.3 jit_solution(11810915332173297778)
XLA Ops:
  0.0 2.3 %reshape.550 = bf16[64,4,2048]{2,1,0:T(4,128)(2,1)} reshape(bf16[256,2048]{1,0:T(8,128)(2,1)} %param.3) | data formatting | bytes 2097152 | tf_op jit(solution)/shard_map/reshape | solution.py:67
  2.3 12.6 %all-to-all-start = ((bf16[64,4,2048]{2,1,0:T(4,128)(2,1)}), bf16[64,4,2048]{2,1,0:T(4,128)(2,1)S(1)}, u32[]{:S(2)}, u32[]{:S(2)}) async-start(bf16[64,4,2048]{2,1,0:T(4,128)(2,1)} %reshape.550), calls=%async_computation | async-start | bytes 2097152 | tf_op jit(solution)/shard_map/all_to_all | solution.py:68
  14.9 0.1 fusion.71
  15.0 1.1 negate_select_fusion.3
  16.2 2.0 %fusion.44 = (f32[2048,64]{0,1:T(8,128)S(1)}, f32[2048,64]{0,1:T(8,128)S(1)}) fusion(s32[2048]{0:T(1024)S(1)} %fusion.56), kind=kLoop, calls=%fused_computation.87 | loop fusion | flops 1835008 | bytes 1056768 | tf_op jit(solution)/shard_map/cos | solution.py:30
  18.2 6.2 %multiply_convert_fusion = bf16[2048,32,64]{0,2,1:T(8,128)(2,1)} fusion(f32[2048,64]{0,1:T(8,128)S(1)} %get-tuple-element.40, f32[2048,32]{0,1:T(8,128)S(1)} %get-tuple-element.38, f32[2048,64]{0,1:T(8,128)S(1)} %get-tuple-element.39, f32[2048,32]{0,1:T(8,128)S(1)} %get-tuple-element.37), kind=kLoop, calls=%fused_computation | loop fusion | flops 20971520 | bytes 9961472 | tf_op jit(solution)/shard_map/convert_element_type | solution.py:36
  24.4 18.6 %all-to-all-done = bf16[64,4,2048]{2,1,0:T(4,128)(2,1)S(1)} async-done(((bf16[64,4,2048]{2,1,0:T(4,128)(2,1)}), bf16[64,4,2048]{2,1,0:T(4,128)(2,1)S(1)}, u32[]{:S(2)}, u32[]{:S(2)}) %all-to-all-start) | async-done | bytes 1048608 | tf_op jit(solution)/shard_map/all_to_all | solution.py:68
  43.0 0.6 pad_convert_fusion
  43.6 9.2 %fusion.22 = bf16[4,64,2048]{2,0,1:T(4,128)(2,1)S(1)} fusion(f32[79,4,2048]{2,1,0:T(4,128)S(1)} %pad_convert_fusion, f32[2048]{0:T(1024)S(1)} %bitcast.148, f32[2048]{0:T(1024)S(1)} %bitcast.149, f32[2048]{0:T(1024)S(1)} %bitcast.135, f32[2048]{0:T(1024)S(1)} %bitcast.136, f32[2048]{0:T(1024)S(1)} %bitcast.137, f32[2048]{0:T(1024)S(1)} %bitcast.138, ...), kind=kLoop, calls=%fused_computation.40 | loop fusion | flops 16777216 | bytes 34734080 | tf_op jit(solution)/shard_map/transpose | solution.py:75
  52.8 0.6 copy.58
  53.4 3.6 %convolution_convert_fusion = bf16[2048,256]{1,0:T(8,128)(2,1)} fusion(bf16[2048,2048]{0,1:T(8,128)(2,1)S(1)} %bitcast.123, bf16[256,2048]{1,0:T(8,128)(2,1)S(1)} %bitcast.129), kind=kOutput, calls=%fused_computation.3 | convolution fusion | flops 2148007936 | bytes 10485760 | tf_op jit(solution)/shard_map/jk,mk->jm/dot_general | solution.py:78
  57.1 5.9 %all-to-all-start.1 = ((bf16[64,32,256]{2,1,0:T(8,128)(2,1)}), bf16[64,32,256]{2,1,0:T(8,128)(2,1)S(1)}, u32[]{:S(2)}, u32[]{:S(2)}) async-start(bf16[64,32,256]{2,1,0:T(8,128)(2,1)} %bitcast.19), calls=%async_computation.1 | async-start | bytes 2097152 | tf_op jit(solution)/shard_map/all_to_all | solution.py:88
  63.0 14.0 %reshape.556 = bf16[16,512,4,128]{3,2,1,0:T(4,128)(2,1)} reshape(bf16[16,256,2,512]{3,2,1,0:T(2,128)(2,1)} %param.5) | data formatting | bytes 16777216 | tf_op jit(solution)/shard_map/reshape | solution.py:99
  77.0 13.8 %all-to-all-done.1 = bf16[64,32,256]{2,1,0:T(8,128)(2,1)S(1)} async-done(((bf16[64,32,256]{2,1,0:T(8,128)(2,1)}), bf16[64,32,256]{2,1,0:T(8,128)(2,1)S(1)}, u32[]{:S(2)}, u32[]{:S(2)}) %all-to-all-start.1) | async-done | bytes 1048608 | tf_op jit(solution)/shard_map/all_to_all | solution.py:88
  90.9 0.8 reshape.553
  91.7 0.6 copy.59
  92.4 0.3 slice_negate_fusion
  92.6 1.2 maximum_maximum_fusion
  93.8 1.9 %copy-done = bf16[16,512,4,128]{3,2,1,0:T(4,128)(2,1)S(1)} copy-done((bf16[16,512,4,128]{3,2,1,0:T(4,128)(2,1)S(1)}, bf16[16,512,4,128]{3,2,1,0:T(4,128)(2,1)}, u32[]{:S(2)}) %copy-start) | copy-done | bytes 8388632
  95.7 2.0 %fusion.2 = f32[4,16,128,128]{2,3,0,1:T(8,128)S(1)} fusion(bf16[16,512,4,128]{3,2,1,0:T(4,128)(2,1)S(1)} %copy-done, bf16[16,512,128,1]{2,0,1,3:T(8,128)(2,1)S(1)} %bitcast.120), kind=kOutput, calls=%fused_computation.4 | convolution fusion | flops 1073741824 | bytes 14680064 | tf_op jit(solution)/shard_map/ckjb,ckn->jcbn/dot_general | solution.py:100
  97.8 0.4 fusion.66
  98.2 0.1 fusion.67
  98.3 0.1 select_bitcast_fusion.3
  98.3 2.5 %collective-permute-start = (f32[2,4,128,128]{2,3,1,0:T(8,128)S(1)}, f32[2,4,128,128]{2,3,1,0:T(8,128)S(1)}, u32[]{:S(2)}, u32[]{:S(2)}) collective-permute-start(f32[2,4,128,128]{2,3,1,0:T(8,128)S(1)} %select_bitcast_fusion.3), channel_id=1, source_target_pairs={{0,1},{1,0},{2,3},{3,2},{4,5},{5,4},{6,7},{7,6},{8,9},{9,8},{10,11... | collective-permute-start | bytes 1572872 | tf_op jit(solution)/shard_map/ppermute | solution.py:54
  100.8 0.1 fusion.68
  100.9 0.1 select_bitcast_fusion.2
  101.0 0.1 collective-permute-start.2
  101.1 0.1 fusion.69
  101.1 0.1 select_bitcast_fusion.1
  101.2 0.6 collective-permute-start.4
  101.8 0.2 fusion.70
  102.0 0.1 collective-permute-start.6
  102.1 0.3 collective-permute-done
  102.3 0.1 fusion.29
  102.5 4.3 %collective-permute-start.1 = (f32[1,4,128,128]{2,3,1,0:T(8,128)S(1)}, f32[1,4,128,128]{2,3,1,0:T(8,128)S(1)}, u32[]{:S(2)}, u32[]{:S(2)}) collective-permute-start(f32[1,4,128,128]{2,3,1,0:T(8,128)S(1)} %select_bitcast_fusion.7), channel_id=1, source_target_pairs={{0,2},{1,3},{2,0},{3,1},{4,6},{5,7},{6,4},{7,5},{8,10},{9,11},{10,... | collective-permute-start | bytes 786440 | tf_op jit(solution)/shard_map/ppermute | solution.py:54
  106.8 0.0 collective-permute-done.2
  106.8 0.1 fusion.28
  106.9 1.2 collective-permute-start.3
  108.1 0.0 collective-permute-done.4
  108.1 0.1 fusion.27
  108.3 4.3 %collective-permute-start.5 = (f32[1,4,128,128]{2,3,1,0:T(8,128)S(1)}, f32[1,4,128,128]{2,3,1,0:T(8,128)S(1)}, u32[]{:S(2)}, u32[]{:S(2)}) collective-permute-start(f32[1,4,128,128]{2,3,1,0:T(8,128)S(1)} %select_bitcast_fusion.5), channel_id=1, source_target_pairs={{0,2},{1,3},{2,0},{3,1},{4,6},{5,7},{6,4},{7,5},{8,10},{9,11},{10,... | collective-permute-start | bytes 786440 | tf_op jit(solution)/shard_map/ppermute | solution.py:54
  112.6 0.1 fusion.30
  112.7 1.2 collective-permute-start.7
  113.9 6.8 %collective-permute-done.1 = f32[1,4,128,128]{2,3,1,0:T(8,128)S(1)} collective-permute-done((f32[1,4,128,128]{2,3,1,0:T(8,128)S(1)}, f32[1,4,128,128]{2,3,1,0:T(8,128)S(1)}, u32[]{:S(2)}, u32[]{:S(2)}) %collective-permute-start.1) | collective-permute-done | bytes 262176 | tf_op jit(solution)/shard_map/ppermute | solution.py:54
  120.9 15.5 %collective-permute-done.3 = f32[1,4,128,128]{2,3,1,0:T(8,128)S(1)} collective-permute-done((f32[1,4,128,128]{2,3,1,0:T(8,128)S(1)}, f32[1,4,128,128]{2,3,1,0:T(8,128)S(1)}, u32[]{:S(2)}, u32[]{:S(2)}) %collective-permute-start.3) | collective-permute-done | bytes 262176 | tf_op jit(solution)/shard_map/ppermute | solution.py:54
  136.4 11.4 %collective-permute-done.5 = f32[1,4,128,128]{2,3,1,0:T(8,128)S(1)} collective-permute-done((f32[1,4,128,128]{2,3,1,0:T(8,128)S(1)}, f32[1,4,128,128]{2,3,1,0:T(8,128)S(1)}, u32[]{:S(2)}, u32[]{:S(2)}) %collective-permute-start.5) | collective-permute-done | bytes 262176 | tf_op jit(solution)/shard_map/ppermute | solution.py:54
  148.1 5.4 %collective-permute-done.7 = f32[1,4,128,128]{2,3,1,0:T(8,128)S(1)} collective-permute-done((f32[1,4,128,128]{2,3,1,0:T(8,128)S(1)}, f32[1,4,128,128]{2,3,1,0:T(8,128)S(1)}, u32[]{:S(2)}, u32[]{:S(2)}) %collective-permute-start.7) | collective-permute-done | bytes 262176 | tf_op jit(solution)/shard_map/ppermute | solution.py:54
  153.6 0.6 copy.77
  (31 shorter events, 0.6 us)
Async XLA Ops:
  0.0 14.9 %copy-start.1 = (f32[16,2048]{1,0:T(8,128)S(1)}, f32[16,2048]{1,0:T(8,128)}, u32[]{:S(2)}) copy-start(f32[16,2048]{1,0:T(8,128)} %param.4) | copy-start | bytes 393220
  2.3 40.7 %all-to-all-start = ((bf16[64,4,2048]{2,1,0:T(4,128)(2,1)}), bf16[64,4,2048]{2,1,0:T(4,128)(2,1)S(1)}, u32[]{:S(2)}, u32[]{:S(2)}) async-start(bf16[64,4,2048]{2,1,0:T(4,128)(2,1)} %reshape.550), calls=%async_computation | async-start | bytes 2097152 | tf_op jit(solution)/shard_map/all_to_all | solution.py:68
  43.0 10.4 %slice-start = ((s8[8388608]{0:T(1024)(128)(4,1)}), s8[4194304]{0:T(1024)(128)(4,1)S(1)}, s32[]{:S(2)}) async-start(s8[8388608]{0:T(1024)(128)(4,1)} %bitcast.121), calls=%async_computation.2 | async-start | bytes 8388608
  43.6 9.8 %slice-start.1 = ((s8[8388608]{0:T(1024)(128)(4,1)}), s8[4194304]{0:T(1024)(128)(4,1)S(1)}, s32[]{:S(2)}) async-start(s8[8388608]{0:T(1024)(128)(4,1)} %bitcast.121), calls=%async_computation.3 | async-start | bytes 8388608
  57.1 33.8 %all-to-all-start.1 = ((bf16[64,32,256]{2,1,0:T(8,128)(2,1)}), bf16[64,32,256]{2,1,0:T(8,128)(2,1)S(1)}, u32[]{:S(2)}, u32[]{:S(2)}) async-start(bf16[64,32,256]{2,1,0:T(8,128)(2,1)} %bitcast.19), calls=%async_computation.1 | async-start | bytes 2097152 | tf_op jit(solution)/shard_map/all_to_all | solution.py:88
  92.3 3.4 %copy-start = (bf16[16,512,4,128]{3,2,1,0:T(4,128)(2,1)S(1)}, bf16[16,512,4,128]{3,2,1,0:T(4,128)(2,1)}, u32[]{:S(2)}) copy-start(bf16[16,512,4,128]{3,2,1,0:T(4,128)(2,1)} %reshape.556) | copy-start | bytes 25165828
  98.3 4.0 %collective-permute-start = (f32[2,4,128,128]{2,3,1,0:T(8,128)S(1)}, f32[2,4,128,128]{2,3,1,0:T(8,128)S(1)}, u32[]{:S(2)}, u32[]{:S(2)}) collective-permute-start(f32[2,4,128,128]{2,3,1,0:T(8,128)S(1)} %select_bitcast_fusion.3), channel_id=1, source_target_pairs={{0,1},{1,0},{2,3},{3,2},{4,5},{5,4},{6,7},{7,6},{8,9},{9,8},{10,11... | collective-permute-start | bytes 1572872 | tf_op jit(solution)/shard_map/ppermute | solution.py:54
  101.0 5.8 %collective-permute-start.2 = (f32[2,4,128,128]{2,3,1,0:T(8,128)S(1)}, f32[2,4,128,128]{2,3,1,0:T(8,128)S(1)}, u32[]{:S(2)}, u32[]{:S(2)}) collective-permute-start(f32[2,4,128,128]{2,3,1,0:T(8,128)S(1)} %select_bitcast_fusion.2), channel_id=1, source_target_pairs={{0,1},{1,0},{2,3},{3,2},{4,5},{5,4},{6,7},{7,6},{8,9},{9,8},{10,11... | collective-permute-start | bytes 1572872 | tf_op jit(solution)/shard_map/ppermute | solution.py:54
  101.2 6.9 %collective-permute-start.4 = (f32[2,4,128,128]{2,3,1,0:T(8,128)S(1)}, f32[2,4,128,128]{2,3,1,0:T(8,128)S(1)}, u32[]{:S(2)}, u32[]{:S(2)}) collective-permute-start(f32[2,4,128,128]{2,3,1,0:T(8,128)S(1)} %select_bitcast_fusion.1), channel_id=1, source_target_pairs={{0,1},{1,0},{2,3},{3,2},{4,5},{5,4},{6,7},{7,6},{8,9},{9,8},{10,11... | collective-permute-start | bytes 1572872 | tf_op jit(solution)/shard_map/ppermute | solution.py:54
  102.0 10.6 %collective-permute-start.6 = (f32[2,4,128,128]{2,3,0,1:T(8,128)S(1)}, f32[2,4,128,128]{2,3,0,1:T(8,128)S(1)}, u32[]{:S(2)}, u32[]{:S(2)}) collective-permute-start(f32[2,4,128,128]{2,3,0,1:T(8,128)S(1)} %get-tuple-element.19), channel_id=1, source_target_pairs={{0,1},{1,0},{2,3},{3,2},{4,5},{5,4},{6,7},{7,6},{8,9},{9,8},{10,11... | collective-permute-start | bytes 1572872 | tf_op jit(solution)/shard_map/ppermute | solution.py:54
  102.5 18.3 %collective-permute-start.1 = (f32[1,4,128,128]{2,3,1,0:T(8,128)S(1)}, f32[1,4,128,128]{2,3,1,0:T(8,128)S(1)}, u32[]{:S(2)}, u32[]{:S(2)}) collective-permute-start(f32[1,4,128,128]{2,3,1,0:T(8,128)S(1)} %select_bitcast_fusion.7), channel_id=1, source_target_pairs={{0,2},{1,3},{2,0},{3,1},{4,6},{5,7},{6,4},{7,5},{8,10},{9,11},{10,... | collective-permute-start | bytes 786440 | tf_op jit(solution)/shard_map/ppermute | solution.py:54
  106.9 29.5 %collective-permute-start.3 = (f32[1,4,128,128]{2,3,1,0:T(8,128)S(1)}, f32[1,4,128,128]{2,3,1,0:T(8,128)S(1)}, u32[]{:S(2)}, u32[]{:S(2)}) collective-permute-start(f32[1,4,128,128]{2,3,1,0:T(8,128)S(1)} %select_bitcast_fusion.6), channel_id=1, source_target_pairs={{0,2},{1,3},{2,0},{3,1},{4,6},{5,7},{6,4},{7,5},{8,10},{9,11},{10,... | collective-permute-start | bytes 786440 | tf_op jit(solution)/shard_map/ppermute | solution.py:54
  108.3 39.6 %collective-permute-start.5 = (f32[1,4,128,128]{2,3,1,0:T(8,128)S(1)}, f32[1,4,128,128]{2,3,1,0:T(8,128)S(1)}, u32[]{:S(2)}, u32[]{:S(2)}) collective-permute-start(f32[1,4,128,128]{2,3,1,0:T(8,128)S(1)} %select_bitcast_fusion.5), channel_id=1, source_target_pairs={{0,2},{1,3},{2,0},{3,1},{4,6},{5,7},{6,4},{7,5},{8,10},{9,11},{10,... | collective-permute-start | bytes 786440 | tf_op jit(solution)/shard_map/ppermute | solution.py:54
  112.7 40.8 %collective-permute-start.7 = (f32[1,4,128,128]{2,3,1,0:T(8,128)S(1)}, f32[1,4,128,128]{2,3,1,0:T(8,128)S(1)}, u32[]{:S(2)}, u32[]{:S(2)}) collective-permute-start(f32[1,4,128,128]{2,3,1,0:T(8,128)S(1)} %select_bitcast_fusion.4), channel_id=1, source_target_pairs={{0,2},{1,3},{2,0},{3,1},{4,6},{5,7},{6,4},{7,5},{8,10},{9,11},{10,... | collective-permute-start | bytes 786440 | tf_op jit(solution)/shard_map/ppermute | solution.py:54

commit v11 on v10

--- a/solution.py
+++ b/solution.py
@@ -98,7 +98,7 @@
     per_out = beam_weights.shape[3] // n_feed
     weights = beam_weights.reshape(per_group, feeds_here * 2, n_feed, per_out)
     beams_all = jnp.einsum("ckjb,ckn->jcbn", weights, paired, preferred_element_type=jnp.float32)
-    n_parts = 4
+    n_parts = 8
     per_part = per_group // n_parts
     binned_parts = []
     for part in range(n_parts):

time: 155 us -> 156 us (level)
  starting transfers between devices: 32.8 us -> 53.3 us
  waiting for transfers between devices: 71.9 us -> 52.4 us
    ppermute x8 -> x16, starting transfers between devices: 14.4 us -> 34.9 us  [exchange(): received = lax.ppermute(jnp.where(low, blocks[1], blocks[0]), axis, pairs)]
    ppermute x8 -> x16, waiting for transfers between devices: 39.5 us -> 19.9 us  [exchange(): received = lax.ppermute(jnp.where(low, blocks[1], blocks[0]), axis, pairs)]
  transfers between devices with their start and end apart: 10 -> 18, of which waited for: 7 -> 8; matrix products, arithmetic and copies ran while one was open for 16% -> 16% of each run, Pallas kernels for 0% -> 0%
where the time goes in v11:
time: 156 us
  starting transfers between devices  53.3 us (34%)
  waiting for transfers between devices  52.4 us (34%)
  other arithmetic  21.9 us (14%)
  local copies, waits for them, and re-layouts  21.7 us (14%)
  matrix products  5.69 us (4%)
    ppermute x16, starting transfers between devices, exchange(): received = lax.ppermute(jnp.where(low, blocks[1], blocks[0]), axis, pairs)  34.9 us
    ppermute x16, waiting for transfers between devices, exchange(): received = lax.ppermute(jnp.where(low, blocks[1], blocks[0]), axis, pairs)  19.9 us
    all_to_all x1, waiting for transfers between devices, local(): blocks = lax.all_to_all(blocks, 'tm', 0, 0, tiled=True)  18.6 us
    reshape x1, local copies, waits for them, and re-layouts, local(): weights = beam_weights.reshape(per_group, feeds_here * 2, n_feed, per_out)  14 us
    all_to_all x1, waiting for transfers between devices, local(): turned = lax.all_to_all(spectra, 'tm', 0, 0, tiled=True)  13.9 us
    all_to_all x1, starting transfers between devices, local(): blocks = lax.all_to_all(blocks, 'tm', 0, 0, tiled=True)  12.6 us
    transpose x1, other arithmetic, local(): filtered = jnp.transpose(filtered, (1, 0, 2))  9.2 us
    convert_element_type x1, other arithmetic, dft_rows(): return table.reshape(cols, frame_len).astype(jnp.bfloat16)  6.17 us
  transfers between devices with their start and end apart: 18, of which 8 were waited for; matrix products, arithmetic and copies ran while one was open for 16% of the time, Pallas kernels for 0%

profile of v11, /device:TPU:1, one launch (start us, length us, event | category | flops | bytes accessed | tf_op | source)
XLA Modules:
  0.0 155.7 jit_solution(15123172711299039074)
XLA Ops:
  0.0 2.3 %reshape.786 = bf16[64,4,2048]{2,1,0:T(4,128)(2,1)} reshape(bf16[256,2048]{1,0:T(8,128)(2,1)} %param.3) | data formatting | bytes 2097152 | tf_op jit(solution)/shard_map/reshape | solution.py:67
  2.4 12.6 %all-to-all-start = ((bf16[64,4,2048]{2,1,0:T(4,128)(2,1)}), bf16[64,4,2048]{2,1,0:T(4,128)(2,1)S(1)}, u32[]{:S(2)}, u32[]{:S(2)}) async-start(bf16[64,4,2048]{2,1,0:T(4,128)(2,1)} %reshape.786), calls=%async_computation | async-start | bytes 2097152 | tf_op jit(solution)/shard_map/all_to_all | solution.py:68
  15.0 0.1 fusion.83
  15.1 1.1 negate_select_fusion.3
  16.2 2.0 %fusion.42 = (f32[2048,64]{0,1:T(8,128)S(1)}, f32[2048,64]{0,1:T(8,128)S(1)}) fusion(s32[2048]{0:T(1024)S(1)} %fusion.64), kind=kLoop, calls=%fused_computation.85 | loop fusion | flops 1835008 | bytes 1056768 | tf_op jit(solution)/shard_map/cos | solution.py:30
  18.2 6.2 %multiply_convert_fusion = bf16[2048,32,64]{0,2,1:T(8,128)(2,1)} fusion(f32[2048,64]{0,1:T(8,128)S(1)} %get-tuple-element.52, f32[2048,32]{0,1:T(8,128)S(1)} %get-tuple-element.50, f32[2048,64]{0,1:T(8,128)S(1)} %get-tuple-element.51, f32[2048,32]{0,1:T(8,128)S(1)} %get-tuple-element.49), kind=kLoop, calls=%fused_computation | loop fusion | flops 20971520 | bytes 9961472 | tf_op jit(solution)/shard_map/convert_element_type | solution.py:36
  24.4 18.6 %all-to-all-done = bf16[64,4,2048]{2,1,0:T(4,128)(2,1)S(1)} async-done(((bf16[64,4,2048]{2,1,0:T(4,128)(2,1)}), bf16[64,4,2048]{2,1,0:T(4,128)(2,1)S(1)}, u32[]{:S(2)}, u32[]{:S(2)}) %all-to-all-start) | async-done | bytes 1048608 | tf_op jit(solution)/shard_map/all_to_all | solution.py:68
  43.0 0.6 pad_convert_fusion
  43.7 9.2 %fusion.22 = bf16[4,64,2048]{2,0,1:T(4,128)(2,1)S(1)} fusion(f32[79,4,2048]{2,1,0:T(4,128)S(1)} %pad_convert_fusion, f32[2048]{0:T(1024)S(1)} %bitcast.228, f32[2048]{0:T(1024)S(1)} %bitcast.229, f32[2048]{0:T(1024)S(1)} %bitcast.215, f32[2048]{0:T(1024)S(1)} %bitcast.216, f32[2048]{0:T(1024)S(1)} %bitcast.217, f32[2048]{0:T(1024)S(1)} %bitcast.218, ...), kind=kLoop, calls=%fused_computation.40 | loop fusion | flops 16777216 | bytes 34734080 | tf_op jit(solution)/shard_map/transpose | solution.py:75
  52.9 0.6 copy.82
  53.5 3.6 %convolution_convert_fusion = bf16[2048,256]{1,0:T(8,128)(2,1)} fusion(bf16[2048,2048]{0,1:T(8,128)(2,1)S(1)} %bitcast.194, bf16[256,2048]{1,0:T(8,128)(2,1)S(1)} %bitcast.204), kind=kOutput, calls=%fused_computation.3 | convolution fusion | flops 2148007936 | bytes 10485760 | tf_op jit(solution)/shard_map/jk,mk->jm/dot_general | solution.py:78
  57.1 5.9 %all-to-all-start.1 = ((bf16[64,32,256]{2,1,0:T(8,128)(2,1)}), bf16[64,32,256]{2,1,0:T(8,128)(2,1)S(1)}, u32[]{:S(2)}, u32[]{:S(2)}) async-start(bf16[64,32,256]{2,1,0:T(8,128)(2,1)} %bitcast.19), calls=%async_computation.1 | async-start | bytes 2097152 | tf_op jit(solution)/shard_map/all_to_all | solution.py:88
  63.1 14.0 %reshape.792 = bf16[16,512,4,128]{3,2,1,0:T(4,128)(2,1)} reshape(bf16[16,256,2,512]{3,2,1,0:T(2,128)(2,1)} %param.5) | data formatting | bytes 16777216 | tf_op jit(solution)/shard_map/reshape | solution.py:99
  77.1 13.9 %all-to-all-done.1 = bf16[64,32,256]{2,1,0:T(8,128)(2,1)S(1)} async-done(((bf16[64,32,256]{2,1,0:T(8,128)(2,1)}), bf16[64,32,256]{2,1,0:T(8,128)(2,1)S(1)}, u32[]{:S(2)}, u32[]{:S(2)}) %all-to-all-start.1) | async-done | bytes 1048608 | tf_op jit(solution)/shard_map/all_to_all | solution.py:88
  91.0 0.8 reshape.789
  91.8 0.6 copy.83
  92.4 0.3 slice_negate_fusion
  92.7 1.2 maximum_maximum_fusion
  93.9 1.9 %copy-done = bf16[16,512,4,128]{3,2,1,0:T(4,128)(2,1)S(1)} copy-done((bf16[16,512,4,128]{3,2,1,0:T(4,128)(2,1)S(1)}, bf16[16,512,4,128]{3,2,1,0:T(4,128)(2,1)}, u32[]{:S(2)}) %copy-start) | copy-done | bytes 8388632
  95.8 2.0 %fusion.2 = f32[4,16,128,128]{2,3,0,1:T(8,128)S(1)} fusion(bf16[16,512,4,128]{3,2,1,0:T(4,128)(2,1)S(1)} %copy-done, bf16[16,512,128,1]{2,0,1,3:T(8,128)(2,1)S(1)} %bitcast.191), kind=kOutput, calls=%fused_computation.4 | convolution fusion | flops 1073741824 | bytes 14680064 | tf_op jit(solution)/shard_map/ckjb,ckn->jcbn/dot_general | solution.py:100
  97.9 0.4 fusion.74
  98.3 2.5 %collective-permute-start.14 = (f32[2,2,128,128]{2,3,0,1:T(8,128)S(1)}, f32[2,2,128,128]{2,3,0,1:T(8,128)S(1)}, u32[]{:S(2)}, u32[]{:S(2)}) collective-permute-start(f32[2,2,128,128]{2,3,0,1:T(8,128)S(1)} %get-tuple-element.17), channel_id=1, source_target_pairs={{0,1},{1,0},{2,3},{3,2},{4,5},{5,4},{6,7},{7,6},{8,9},{9,8},{10,11... | collective-permute-start | bytes 786440 | tf_op jit(solution)/shard_map/ppermute | solution.py:54
  100.9 0.1 collective-permute-start.12
  101.0 0.6 collective-permute-start.10
  101.7 0.1 collective-permute-start.8
  101.9 0.6 collective-permute-start.6
  102.7 0.1 collective-permute-start.4
  102.8 0.1 fusion.40
  102.9 0.8 collective-permute-start.2
  103.8 0.1 collective-permute-start
  104.0 4.3 %collective-permute-start.15 = (f32[1,2,128,128]{2,3,1,0:T(8,128)S(1)}, f32[1,2,128,128]{2,3,1,0:T(8,128)S(1)}, u32[]{:S(2)}, u32[]{:S(2)}) collective-permute-start(f32[1,2,128,128]{2,3,1,0:T(8,128)S(1)} %select_bitcast_fusion.8), channel_id=1, source_target_pairs={{0,2},{1,3},{2,0},{3,1},{4,6},{5,7},{6,4},{7,5},{8,10},{9,11},{10,... | collective-permute-start | bytes 393224 | tf_op jit(solution)/shard_map/ppermute | solution.py:54
  108.4 1.2 collective-permute-start.13
  109.6 0.1 fusion.36
  109.7 4.3 %collective-permute-start.11 = (f32[1,2,128,128]{2,3,1,0:T(8,128)S(1)}, f32[1,2,128,128]{2,3,1,0:T(8,128)S(1)}, u32[]{:S(2)}, u32[]{:S(2)}) collective-permute-start(f32[1,2,128,128]{2,3,1,0:T(8,128)S(1)} %select_bitcast_fusion.10), channel_id=1, source_target_pairs={{0,2},{1,3},{2,0},{3,1},{4,6},{5,7},{6,4},{7,5},{8,10},{9,11},{10,... | collective-permute-start | bytes 393224 | tf_op jit(solution)/shard_map/ppermute | solution.py:54
  114.0 0.1 fusion.37
  114.1 1.2 collective-permute-start.9
  115.3 0.1 fusion.38
  115.4 4.3 %collective-permute-start.7 = (f32[1,2,128,128]{2,3,1,0:T(8,128)S(1)}, f32[1,2,128,128]{2,3,1,0:T(8,128)S(1)}, u32[]{:S(2)}, u32[]{:S(2)}) collective-permute-start(f32[1,2,128,128]{2,3,1,0:T(8,128)S(1)} %select_bitcast_fusion.12), channel_id=1, source_target_pairs={{0,2},{1,3},{2,0},{3,1},{4,6},{5,7},{6,4},{7,5},{8,10},{9,11},{10,... | collective-permute-start | bytes 393224 | tf_op jit(solution)/shard_map/ppermute | solution.py:54
  119.8 2.2 %collective-permute-start.5 = (f32[1,2,128,128]{2,3,1,0:T(8,128)S(1)}, f32[1,2,128,128]{2,3,1,0:T(8,128)S(1)}, u32[]{:S(2)}, u32[]{:S(2)}) collective-permute-start(f32[1,2,128,128]{2,3,1,0:T(8,128)S(1)} %select_bitcast_fusion.13), channel_id=1, source_target_pairs={{0,2},{1,3},{2,0},{3,1},{4,6},{5,7},{6,4},{7,5},{8,10},{9,11},{10,... | collective-permute-start | bytes 393224 | tf_op jit(solution)/shard_map/ppermute | solution.py:54
  122.1 0.1 collective-permute-done.13
  122.2 6.1 %collective-permute-start.3 = (f32[1,2,128,128]{2,3,1,0:T(8,128)S(1)}, f32[1,2,128,128]{2,3,1,0:T(8,128)S(1)}, u32[]{:S(2)}, u32[]{:S(2)}) collective-permute-start(f32[1,2,128,128]{2,3,1,0:T(8,128)S(1)} %select_bitcast_fusion.14), channel_id=1, source_target_pairs={{0,2},{1,3},{2,0},{3,1},{4,6},{5,7},{6,4},{7,5},{8,10},{9,11},{10,... | collective-permute-start | bytes 393224 | tf_op jit(solution)/shard_map/ppermute | solution.py:54
  128.3 3.2 %collective-permute-done.11 = f32[1,2,128,128]{2,3,1,0:T(8,128)S(1)} collective-permute-done((f32[1,2,128,128]{2,3,1,0:T(8,128)S(1)}, f32[1,2,128,128]{2,3,1,0:T(8,128)S(1)}, u32[]{:S(2)}, u32[]{:S(2)}) %collective-permute-start.11) | collective-permute-done | bytes 131104 | tf_op jit(solution)/shard_map/ppermute | solution.py:54
  131.5 6.2 %collective-permute-start.1 = (f32[1,2,128,128]{2,3,1,0:T(8,128)S(1)}, f32[1,2,128,128]{2,3,1,0:T(8,128)S(1)}, u32[]{:S(2)}, u32[]{:S(2)}) collective-permute-start(f32[1,2,128,128]{2,3,1,0:T(8,128)S(1)} %select_bitcast_fusion.15), channel_id=1, source_target_pairs={{0,2},{1,3},{2,0},{3,1},{4,6},{5,7},{6,4},{7,5},{8,10},{9,11},{10,... | collective-permute-start | bytes 393224 | tf_op jit(solution)/shard_map/ppermute | solution.py:54
  137.9 8.5 %collective-permute-done.7 = f32[1,2,128,128]{2,3,1,0:T(8,128)S(1)} collective-permute-done((f32[1,2,128,128]{2,3,1,0:T(8,128)S(1)}, f32[1,2,128,128]{2,3,1,0:T(8,128)S(1)}, u32[]{:S(2)}, u32[]{:S(2)}) %collective-permute-start.7) | collective-permute-done | bytes 131104 | tf_op jit(solution)/shard_map/ppermute | solution.py:54
  146.5 2.7 %collective-permute-done.5 = f32[1,2,128,128]{2,3,1,0:T(8,128)S(1)} collective-permute-done((f32[1,2,128,128]{2,3,1,0:T(8,128)S(1)}, f32[1,2,128,128]{2,3,1,0:T(8,128)S(1)}, u32[]{:S(2)}, u32[]{:S(2)}) %collective-permute-start.5) | collective-permute-done | bytes 131104 | tf_op jit(solution)/shard_map/ppermute | solution.py:54
  149.4 2.7 %collective-permute-done.3 = f32[1,2,128,128]{2,3,1,0:T(8,128)S(1)} collective-permute-done((f32[1,2,128,128]{2,3,1,0:T(8,128)S(1)}, f32[1,2,128,128]{2,3,1,0:T(8,128)S(1)}, u32[]{:S(2)}, u32[]{:S(2)}) %collective-permute-start.3) | collective-permute-done | bytes 131104 | tf_op jit(solution)/shard_map/ppermute | solution.py:54
  152.1 2.7 %collective-permute-done.1 = f32[1,2,128,128]{2,3,1,0:T(8,128)S(1)} collective-permute-done((f32[1,2,128,128]{2,3,1,0:T(8,128)S(1)}, f32[1,2,128,128]{2,3,1,0:T(8,128)S(1)}, u32[]{:S(2)}, u32[]{:S(2)}) %collective-permute-start.1) | collective-permute-done | bytes 131104 | tf_op jit(solution)/shard_map/ppermute | solution.py:54
  155.0 0.6 copy.109
  (80 shorter events, 1.4 us)
Async XLA Ops:
  0.0 15.0 %copy-start.1 = (f32[16,2048]{1,0:T(8,128)S(1)}, f32[16,2048]{1,0:T(8,128)}, u32[]{:S(2)}) copy-start(f32[16,2048]{1,0:T(8,128)} %param.4) | copy-start | bytes 393220
  2.4 40.7 %all-to-all-start = ((bf16[64,4,2048]{2,1,0:T(4,128)(2,1)}), bf16[64,4,2048]{2,1,0:T(4,128)(2,1)S(1)}, u32[]{:S(2)}, u32[]{:S(2)}) async-start(bf16[64,4,2048]{2,1,0:T(4,128)(2,1)} %reshape.786), calls=%async_computation | async-start | bytes 2097152 | tf_op jit(solution)/shard_map/all_to_all | solution.py:68
  43.0 10.4 %slice-start = ((s8[8388608]{0:T(1024)(128)(4,1)}), s8[4194304]{0:T(1024)(128)(4,1)S(1)}, s32[]{:S(2)}) async-start(s8[8388608]{0:T(1024)(128)(4,1)} %bitcast.192), calls=%async_computation.2 | async-start | bytes 8388608
  43.7 9.8 %slice-start.1 = ((s8[8388608]{0:T(1024)(128)(4,1)}), s8[4194304]{0:T(1024)(128)(4,1)S(1)}, s32[]{:S(2)}) async-start(s8[8388608]{0:T(1024)(128)(4,1)} %bitcast.192), calls=%async_computation.3 | async-start | bytes 8388608
  57.1 33.8 %all-to-all-start.1 = ((bf16[64,32,256]{2,1,0:T(8,128)(2,1)}), bf16[64,32,256]{2,1,0:T(8,128)(2,1)S(1)}, u32[]{:S(2)}, u32[]{:S(2)}) async-start(bf16[64,32,256]{2,1,0:T(8,128)(2,1)} %bitcast.19), calls=%async_computation.1 | async-start | bytes 2097152 | tf_op jit(solution)/shard_map/all_to_all | solution.py:88
  92.4 3.4 %copy-start = (bf16[16,512,4,128]{3,2,1,0:T(4,128)(2,1)S(1)}, bf16[16,512,4,128]{3,2,1,0:T(4,128)(2,1)}, u32[]{:S(2)}) copy-start(bf16[16,512,4,128]{3,2,1,0:T(4,128)(2,1)} %reshape.792) | copy-start | bytes 25165828
  98.3 4.4 %collective-permute-start.14 = (f32[2,2,128,128]{2,3,0,1:T(8,128)S(1)}, f32[2,2,128,128]{2,3,0,1:T(8,128)S(1)}, u32[]{:S(2)}, u32[]{:S(2)}) collective-permute-start(f32[2,2,128,128]{2,3,0,1:T(8,128)S(1)} %get-tuple-element.17), channel_id=1, source_target_pairs={{0,1},{1,0},{2,3},{3,2},{4,5},{5,4},{6,7},{7,6},{8,9},{9,8},{10,11... | collective-permute-start | bytes 786440 | tf_op jit(solution)/shard_map/ppermute | solution.py:54
  100.9 2.0 %collective-permute-start.12 = (f32[2,2,128,128]{2,3,1,0:T(8,128)S(1)}, f32[2,2,128,128]{2,3,1,0:T(8,128)S(1)}, u32[]{:S(2)}, u32[]{:S(2)}) collective-permute-start(f32[2,2,128,128]{2,3,1,0:T(8,128)S(1)} %select_bitcast_fusion.1), channel_id=1, source_target_pairs={{0,1},{1,0},{2,3},{3,2},{4,5},{5,4},{6,7},{7,6},{8,9},{9,8},{10,11... | collective-permute-start | bytes 786440 | tf_op jit(solution)/shard_map/ppermute | solution.py:54
  101.0 2.7 %collective-permute-start.10 = (f32[2,2,128,128]{2,3,1,0:T(8,128)S(1)}, f32[2,2,128,128]{2,3,1,0:T(8,128)S(1)}, u32[]{:S(2)}, u32[]{:S(2)}) collective-permute-start(f32[2,2,128,128]{2,3,1,0:T(8,128)S(1)} %select_bitcast_fusion.2), channel_id=1, source_target_pairs={{0,1},{1,0},{2,3},{3,2},{4,5},{5,4},{6,7},{7,6},{8,9},{9,8},{10,11... | collective-permute-start | bytes 786440 | tf_op jit(solution)/shard_map/ppermute | solution.py:54
  101.7 2.3 %collective-permute-start.8 = (f32[2,2,128,128]{2,3,1,0:T(8,128)S(1)}, f32[2,2,128,128]{2,3,1,0:T(8,128)S(1)}, u32[]{:S(2)}, u32[]{:S(2)}) collective-permute-start(f32[2,2,128,128]{2,3,1,0:T(8,128)S(1)} %select_bitcast_fusion.3), channel_id=1, source_target_pairs={{0,1},{1,0},{2,3},{3,2},{4,5},{5,4},{6,7},{7,6},{8,9},{9,8},{10,11... | collective-permute-start | bytes 786440 | tf_op jit(solution)/shard_map/ppermute | solution.py:54
  101.9 6.5 %collective-permute-start.6 = (f32[2,2,128,128]{2,3,1,0:T(8,128)S(1)}, f32[2,2,128,128]{2,3,1,0:T(8,128)S(1)}, u32[]{:S(2)}, u32[]{:S(2)}) collective-permute-start(f32[2,2,128,128]{2,3,1,0:T(8,128)S(1)} %select_bitcast_fusion.4), channel_id=1, source_target_pairs={{0,1},{1,0},{2,3},{3,2},{4,5},{5,4},{6,7},{7,6},{8,9},{9,8},{10,11... | collective-permute-start | bytes 786440 | tf_op jit(solution)/shard_map/ppermute | solution.py:54
  102.7 7.0 %collective-permute-start.4 = (f32[2,2,128,128]{2,3,1,0:T(8,128)S(1)}, f32[2,2,128,128]{2,3,1,0:T(8,128)S(1)}, u32[]{:S(2)}, u32[]{:S(2)}) collective-permute-start(f32[2,2,128,128]{2,3,1,0:T(8,128)S(1)} %select_bitcast_fusion.5), channel_id=1, source_target_pairs={{0,1},{1,0},{2,3},{3,2},{4,5},{5,4},{6,7},{7,6},{8,9},{9,8},{10,11... | collective-permute-start | bytes 786440 | tf_op jit(solution)/shard_map/ppermute | solution.py:54
  102.9 11.2 %collective-permute-start.2 = (f32[2,2,128,128]{2,3,1,0:T(8,128)S(1)}, f32[2,2,128,128]{2,3,1,0:T(8,128)S(1)}, u32[]{:S(2)}, u32[]{:S(2)}) collective-permute-start(f32[2,2,128,128]{2,3,1,0:T(8,128)S(1)} %select_bitcast_fusion.6), channel_id=1, source_target_pairs={{0,1},{1,0},{2,3},{3,2},{4,5},{5,4},{6,7},{7,6},{8,9},{9,8},{10,11... | collective-permute-start | bytes 786440 | tf_op jit(solution)/shard_map/ppermute | solution.py:54
  103.8 11.7 %collective-permute-start = (f32[2,2,128,128]{2,3,1,0:T(8,128)S(1)}, f32[2,2,128,128]{2,3,1,0:T(8,128)S(1)}, u32[]{:S(2)}, u32[]{:S(2)}) collective-permute-start(f32[2,2,128,128]{2,3,1,0:T(8,128)S(1)} %select_bitcast_fusion.7), channel_id=1, source_target_pairs={{0,1},{1,0},{2,3},{3,2},{4,5},{5,4},{6,7},{7,6},{8,9},{9,8},{10,11... | collective-permute-start | bytes 786440 | tf_op jit(solution)/shard_map/ppermute | solution.py:54
  104.0 15.8 %collective-permute-start.15 = (f32[1,2,128,128]{2,3,1,0:T(8,128)S(1)}, f32[1,2,128,128]{2,3,1,0:T(8,128)S(1)}, u32[]{:S(2)}, u32[]{:S(2)}) collective-permute-start(f32[1,2,128,128]{2,3,1,0:T(8,128)S(1)} %select_bitcast_fusion.8), channel_id=1, source_target_pairs={{0,2},{1,3},{2,0},{3,1},{4,6},{5,7},{6,4},{7,5},{8,10},{9,11},{10,... | collective-permute-start | bytes 393224 | tf_op jit(solution)/shard_map/ppermute | solution.py:54
  108.4 13.8 %collective-permute-start.13 = (f32[1,2,128,128]{2,3,1,0:T(8,128)S(1)}, f32[1,2,128,128]{2,3,1,0:T(8,128)S(1)}, u32[]{:S(2)}, u32[]{:S(2)}) collective-permute-start(f32[1,2,128,128]{2,3,1,0:T(8,128)S(1)} %select_bitcast_fusion.9), channel_id=1, source_target_pairs={{0,2},{1,3},{2,0},{3,1},{4,6},{5,7},{6,4},{7,5},{8,10},{9,11},{10,... | collective-permute-start | bytes 393224 | tf_op jit(solution)/shard_map/ppermute | solution.py:54
  109.7 21.8 %collective-permute-start.11 = (f32[1,2,128,128]{2,3,1,0:T(8,128)S(1)}, f32[1,2,128,128]{2,3,1,0:T(8,128)S(1)}, u32[]{:S(2)}, u32[]{:S(2)}) collective-permute-start(f32[1,2,128,128]{2,3,1,0:T(8,128)S(1)} %select_bitcast_fusion.10), channel_id=1, source_target_pairs={{0,2},{1,3},{2,0},{3,1},{4,6},{5,7},{6,4},{7,5},{8,10},{9,11},{10,... | collective-permute-start | bytes 393224 | tf_op jit(solution)/shard_map/ppermute | solution.py:54
  114.1 23.7 %collective-permute-start.9 = (f32[1,2,128,128]{2,3,1,0:T(8,128)S(1)}, f32[1,2,128,128]{2,3,1,0:T(8,128)S(1)}, u32[]{:S(2)}, u32[]{:S(2)}) collective-permute-start(f32[1,2,128,128]{2,3,1,0:T(8,128)S(1)} %select_bitcast_fusion.11), channel_id=1, source_target_pairs={{0,2},{1,3},{2,0},{3,1},{4,6},{5,7},{6,4},{7,5},{8,10},{9,11},{10,... | collective-permute-start | bytes 393224 | tf_op jit(solution)/shard_map/ppermute | solution.py:54
  115.4 31.0 %collective-permute-start.7 = (f32[1,2,128,128]{2,3,1,0:T(8,128)S(1)}, f32[1,2,128,128]{2,3,1,0:T(8,128)S(1)}, u32[]{:S(2)}, u32[]{:S(2)}) collective-permute-start(f32[1,2,128,128]{2,3,1,0:T(8,128)S(1)} %select_bitcast_fusion.12), channel_id=1, source_target_pairs={{0,2},{1,3},{2,0},{3,1},{4,6},{5,7},{6,4},{7,5},{8,10},{9,11},{10,... | collective-permute-start | bytes 393224 | tf_op jit(solution)/shard_map/ppermute | solution.py:54
  119.8 29.4 %collective-permute-start.5 = (f32[1,2,128,128]{2,3,1,0:T(8,128)S(1)}, f32[1,2,128,128]{2,3,1,0:T(8,128)S(1)}, u32[]{:S(2)}, u32[]{:S(2)}) collective-permute-start(f32[1,2,128,128]{2,3,1,0:T(8,128)S(1)} %select_bitcast_fusion.13), channel_id=1, source_target_pairs={{0,2},{1,3},{2,0},{3,1},{4,6},{5,7},{6,4},{7,5},{8,10},{9,11},{10,... | collective-permute-start | bytes 393224 | tf_op jit(solution)/shard_map/ppermute | solution.py:54
  122.2 29.9 %collective-permute-start.3 = (f32[1,2,128,128]{2,3,1,0:T(8,128)S(1)}, f32[1,2,128,128]{2,3,1,0:T(8,128)S(1)}, u32[]{:S(2)}, u32[]{:S(2)}) collective-permute-start(f32[1,2,128,128]{2,3,1,0:T(8,128)S(1)} %select_bitcast_fusion.14), channel_id=1, source_target_pairs={{0,2},{1,3},{2,0},{3,1},{4,6},{5,7},{6,4},{7,5},{8,10},{9,11},{10,... | collective-permute-start | bytes 393224 | tf_op jit(solution)/shard_map/ppermute | solution.py:54
  131.5 23.3 %collective-permute-start.1 = (f32[1,2,128,128]{2,3,1,0:T(8,128)S(1)}, f32[1,2,128,128]{2,3,1,0:T(8,128)S(1)}, u32[]{:S(2)}, u32[]{:S(2)}) collective-permute-start(f32[1,2,128,128]{2,3,1,0:T(8,128)S(1)} %select_bitcast_fusion.15), channel_id=1, source_target_pairs={{0,2},{1,3},{2,0},{3,1},{4,6},{5,7},{6,4},{7,5},{8,10},{9,11},{10,... | collective-permute-start | bytes 393224 | tf_op jit(solution)/shard_map/ppermute | solution.py:54

commit v12 on v11

--- a/solution.py
+++ b/solution.py
@@ -98,11 +98,11 @@
     per_out = beam_weights.shape[3] // n_feed
     weights = beam_weights.reshape(per_group, feeds_here * 2, n_feed, per_out)
     beams_all = jnp.einsum("ckjb,ckn->jcbn", weights, paired, preferred_element_type=jnp.float32)
-    n_parts = 8
-    per_part = per_group // n_parts
+    bounds = [0, per_group // 8, per_group // 4, per_group // 2, per_group]
     binned_parts = []
-    for part in range(n_parts):
-        beams = beams_all[:, part * per_part : (part + 1) * per_part]
+    for start, stop in zip(bounds[:-1], bounds[1:]):
+        per_part = stop - start
+        beams = beams_all[:, start:stop]
         flip = 1
         while flip < n_feed:
             split = beams.reshape(-1, 2, *beams.shape[1:])

time: 156 us -> 161 us (1.032)
  waiting for transfers between devices: 52.4 us -> 74.8 us
  starting transfers between devices: 53.3 us -> 32.6 us
  other arithmetic: 21.9 us -> 25.8 us
    ppermute x16 -> x8, waiting for transfers between devices: 19.9 us -> 42.4 us  [exchange(): received = lax.ppermute(jnp.where(low, blocks[1], blocks[0]), axis, pairs)]
    ppermute x16 -> x8, starting transfers between devices: 34.9 us -> 14.2 us  [exchange(): received = lax.ppermute(jnp.where(low, blocks[1], blocks[0]), axis, pairs)]
    reshape x8 -> x4, other arithmetic: 0.43 us -> 2.59 us  [local(): split = beams.reshape(-1, 2, *beams.shape[1:])]
    select_n x15 -> x7, other arithmetic: 0.36 us -> 2.08 us  [exchange(): received = lax.ppermute(jnp.where(low, blocks[1], blocks[0]), axis, pairs)]
  transfers between devices with their start and end apart: 18 -> 10, of which waited for: 8 -> 6; matrix products, arithmetic and copies ran while one was open for 16% -> 18% of each run, Pallas kernels for 0% -> 0%
where the time goes in v12:
time: 161 us
  waiting for transfers between devices  74.8 us (46%)
  starting transfers between devices  32.6 us (20%)
  other arithmetic  25.8 us (16%)
  local copies, waits for them, and re-layouts  21.4 us (13%)
  matrix products  5.67 us (4%)
    ppermute x8, waiting for transfers between devices, exchange(): received = lax.ppermute(jnp.where(low, blocks[1], blocks[0]), axis, pairs)  42.4 us
    all_to_all x1, waiting for transfers between devices, local(): blocks = lax.all_to_all(blocks, 'tm', 0, 0, tiled=True)  18.6 us
    ppermute x8, starting transfers between devices, exchange(): received = lax.ppermute(jnp.where(low, blocks[1], blocks[0]), axis, pairs)  14.2 us
    reshape x1, local copies, waits for them, and re-layouts, local(): weights = beam_weights.reshape(per_group, feeds_here * 2, n_feed, per_out)  14.1 us
    all_to_all x1, waiting for transfers between devices, local(): turned = lax.all_to_all(spectra, 'tm', 0, 0, tiled=True)  13.8 us
    all_to_all x1, starting transfers between devices, local(): blocks = lax.all_to_all(blocks, 'tm', 0, 0, tiled=True)  12.6 us
    transpose x1, other arithmetic, local(): filtered = jnp.transpose(filtered, (1, 0, 2))  9.2 us
    convert_element_type x1, other arithmetic, dft_rows(): return table.reshape(cols, frame_len).astype(jnp.bfloat16)  6.17 us
  transfers between devices with their start and end apart: 10, of which 6 were waited for; matrix products, arithmetic and copies ran while one was open for 18% of the time, Pallas kernels for 0%

profile of v12, /device:TPU:1, one launch (start us, length us, event | category | flops | bytes accessed | tf_op | source)
XLA Modules:
  0.0 160.7 jit_solution(15246345027811478749)
XLA Ops:
  0.0 2.3 %reshape.550 = bf16[64,4,2048]{2,1,0:T(4,128)(2,1)} reshape(bf16[256,2048]{1,0:T(8,128)(2,1)} %param.3) | data formatting | bytes 2097152 | tf_op jit(solution)/shard_map/reshape | solution.py:67
  2.3 12.6 %all-to-all-start = ((bf16[64,4,2048]{2,1,0:T(4,128)(2,1)}), bf16[64,4,2048]{2,1,0:T(4,128)(2,1)S(1)}, u32[]{:S(2)}, u32[]{:S(2)}) async-start(bf16[64,4,2048]{2,1,0:T(4,128)(2,1)} %reshape.550), calls=%async_computation | async-start | bytes 2097152 | tf_op jit(solution)/shard_map/all_to_all | solution.py:68
  14.9 0.1 fusion.77
  15.0 1.1 negate_select_fusion.3
  16.2 2.0 %fusion.48 = (f32[2048,64]{0,1:T(8,128)S(1)}, f32[2048,64]{0,1:T(8,128)S(1)}) fusion(s32[2048]{0:T(1024)S(1)} %fusion.64), kind=kLoop, calls=%fused_computation.88 | loop fusion | flops 1835008 | bytes 1056768 | tf_op jit(solution)/shard_map/cos | solution.py:30
  18.2 6.2 %multiply_convert_fusion = bf16[2048,32,64]{0,2,1:T(8,128)(2,1)} fusion(f32[2048,64]{0,1:T(8,128)S(1)} %get-tuple-element.34, f32[2048,32]{0,1:T(8,128)S(1)} %get-tuple-element.32, f32[2048,64]{0,1:T(8,128)S(1)} %get-tuple-element.33, f32[2048,32]{0,1:T(8,128)S(1)} %get-tuple-element.31), kind=kLoop, calls=%fused_computation | loop fusion | flops 20971520 | bytes 9961472 | tf_op jit(solution)/shard_map/convert_element_type | solution.py:36
  24.4 18.6 %all-to-all-done = bf16[64,4,2048]{2,1,0:T(4,128)(2,1)S(1)} async-done(((bf16[64,4,2048]{2,1,0:T(4,128)(2,1)}), bf16[64,4,2048]{2,1,0:T(4,128)(2,1)S(1)}, u32[]{:S(2)}, u32[]{:S(2)}) %all-to-all-start) | async-done | bytes 1048608 | tf_op jit(solution)/shard_map/all_to_all | solution.py:68
  43.0 0.6 pad_convert_fusion
  43.6 0.0 slice-start.1
  43.6 9.2 %fusion.25 = bf16[4,64,2048]{2,0,1:T(4,128)(2,1)S(1)} fusion(f32[79,4,2048]{2,1,0:T(4,128)S(1)} %pad_convert_fusion, f32[2048]{0:T(1024)S(1)} %bitcast.214, f32[2048]{0:T(1024)S(1)} %bitcast.215, f32[2048]{0:T(1024)S(1)} %bitcast.201, f32[2048]{0:T(1024)S(1)} %bitcast.202, f32[2048]{0:T(1024)S(1)} %bitcast.203, f32[2048]{0:T(1024)S(1)} %bitcast.204, ...), kind=kLoop, calls=%fused_computation.45 | loop fusion | flops 16777216 | bytes 34734080 | tf_op jit(solution)/shard_map/transpose | solution.py:75
  52.9 0.6 copy.94
  53.5 3.6 %convolution_convert_fusion = bf16[2048,256]{1,0:T(8,128)(2,1)} fusion(bf16[2048,2048]{0,1:T(8,128)(2,1)S(1)} %bitcast.191, bf16[256,2048]{1,0:T(8,128)(2,1)S(1)} %bitcast.196), kind=kOutput, calls=%fused_computation.3 | convolution fusion | flops 2148007936 | bytes 10485760 | tf_op jit(solution)/shard_map/jk,mk->jm/dot_general | solution.py:78
  57.1 5.9 %all-to-all-start.1 = ((bf16[64,32,256]{2,1,0:T(8,128)(2,1)}), bf16[64,32,256]{2,1,0:T(8,128)(2,1)S(1)}, u32[]{:S(2)}, u32[]{:S(2)}) async-start(bf16[64,32,256]{2,1,0:T(8,128)(2,1)} %bitcast.19), calls=%async_computation.1 | async-start | bytes 2097152 | tf_op jit(solution)/shard_map/all_to_all | solution.py:88
  63.0 14.1 %reshape.556 = bf16[16,512,4,128]{3,2,1,0:T(4,128)(2,1)} reshape(bf16[16,256,2,512]{3,2,1,0:T(2,128)(2,1)} %param.5) | data formatting | bytes 16777216 | tf_op jit(solution)/shard_map/reshape | solution.py:99
  77.1 13.8 %all-to-all-done.1 = bf16[64,32,256]{2,1,0:T(8,128)(2,1)S(1)} async-done(((bf16[64,32,256]{2,1,0:T(8,128)(2,1)}), bf16[64,32,256]{2,1,0:T(8,128)(2,1)S(1)}, u32[]{:S(2)}, u32[]{:S(2)}) %all-to-all-start.1) | async-done | bytes 1048608 | tf_op jit(solution)/shard_map/all_to_all | solution.py:88
  90.9 0.8 reshape.553
  91.8 0.6 copy.95
  92.4 0.3 slice_negate_fusion
  92.7 1.2 maximum_maximum_fusion
  93.8 1.9 %copy-done = bf16[16,512,4,128]{3,2,1,0:T(4,128)(2,1)S(1)} copy-done((bf16[16,512,4,128]{3,2,1,0:T(4,128)(2,1)S(1)}, bf16[16,512,4,128]{3,2,1,0:T(4,128)(2,1)}, u32[]{:S(2)}) %copy-start) | copy-done | bytes 8388632
  95.8 2.0 %fusion.2 = f32[4,16,128,128]{2,3,0,1:T(8,128)S(1)} fusion(bf16[16,512,4,128]{3,2,1,0:T(4,128)(2,1)S(1)} %copy-done, bf16[16,512,128,1]{2,0,1,3:T(8,128)(2,1)S(1)} %bitcast.186), kind=kOutput, calls=%fused_computation.4 | convolution fusion | flops 1073741824 | bytes 14680064 | tf_op jit(solution)/shard_map/ckjb,ckn->jcbn/dot_general | solution.py:100
  97.8 0.1 fusion.74
  97.9 0.1 slice.244
  98.0 0.1 slice.249
  98.2 2.5 %collective-permute-start = (f32[2,2,128,128]{2,3,1,0:T(8,128)S(1)}, f32[2,2,128,128]{2,3,1,0:T(8,128)S(1)}, u32[]{:S(2)}, u32[]{:S(2)}) collective-permute-start(f32[2,2,128,128]{2,3,1,0:T(8,128)S(1)} %select_bitcast_fusion.5), channel_id=1, source_target_pairs={{0,1},{1,0},{2,3},{3,2},{4,5},{5,4},{6,7},{7,6},{8,9},{9,8},{10,11... | collective-permute-start | bytes 786440 | tf_op jit(solution)/shard_map/ppermute | solution.py:54
  100.7 0.1 fusion.76
  100.8 0.1 collective-permute-start.2
  100.9 0.8 select_bitcast_fusion.2
  101.7 0.5 collective-permute-start.4
  102.2 1.1 select_bitcast_fusion
  103.3 0.0 collective-permute-start.6
  103.4 4.3 %collective-permute-start.1 = (f32[1,2,128,128]{2,3,1,0:T(8,128)S(1)}, f32[1,2,128,128]{2,3,1,0:T(8,128)S(1)}, u32[]{:S(2)}, u32[]{:S(2)}) collective-permute-start(f32[1,2,128,128]{2,3,1,0:T(8,128)S(1)} %select_bitcast_fusion.7), channel_id=1, source_target_pairs={{0,2},{1,3},{2,0},{3,1},{4,6},{5,7},{6,4},{7,5},{8,10},{9,11},{10,... | collective-permute-start | bytes 393224 | tf_op jit(solution)/shard_map/ppermute | solution.py:54
  107.7 0.0 collective-permute-done.2
  107.8 1.2 collective-permute-start.3
  109.0 6.3 %collective-permute-done.1 = f32[1,2,128,128]{2,3,1,0:T(8,128)S(1)} collective-permute-done((f32[1,2,128,128]{2,3,1,0:T(8,128)S(1)}, f32[1,2,128,128]{2,3,1,0:T(8,128)S(1)}, u32[]{:S(2)}, u32[]{:S(2)}) %collective-permute-start.1) | collective-permute-done | bytes 131104 | tf_op jit(solution)/shard_map/ppermute | solution.py:54
  115.4 5.0 %collective-permute-done.3 = f32[1,2,128,128]{2,3,1,0:T(8,128)S(1)} collective-permute-done((f32[1,2,128,128]{2,3,1,0:T(8,128)S(1)}, f32[1,2,128,128]{2,3,1,0:T(8,128)S(1)}, u32[]{:S(2)}, u32[]{:S(2)}) %collective-permute-start.3) | collective-permute-done | bytes 131104 | tf_op jit(solution)/shard_map/ppermute | solution.py:54
  120.5 0.0 collective-permute-done.4
  120.5 1.1 fusion.34
  121.7 3.7 %collective-permute-start.5 = (f32[1,4,128,128]{2,3,1,0:T(8,128)S(1)}, f32[1,4,128,128]{2,3,1,0:T(8,128)S(1)}, u32[]{:S(2)}, u32[]{:S(2)}) collective-permute-start(f32[1,4,128,128]{2,3,1,0:T(8,128)S(1)} %select_bitcast_fusion.3), channel_id=1, source_target_pairs={{0,2},{1,3},{2,0},{3,1},{4,6},{5,7},{6,4},{7,5},{8,10},{9,11},{10,... | collective-permute-start | bytes 786440 | tf_op jit(solution)/shard_map/ppermute | solution.py:54
  125.4 0.0 collective-permute-done.6
  125.4 1.4 fusion.24
  126.8 0.1 select_bitcast_fusion.1
  126.9 1.8 %collective-permute-start.7 = (f32[1,8,128,128]{2,3,1,0:T(8,128)S(1)}, f32[1,8,128,128]{2,3,1,0:T(8,128)S(1)}, u32[]{:S(2)}, u32[]{:S(2)}) collective-permute-start(f32[1,8,128,128]{2,3,1,0:T(8,128)S(1)} %select_bitcast_fusion.1), channel_id=1, source_target_pairs={{0,2},{1,3},{2,0},{3,1},{4,6},{5,7},{6,4},{7,5},{8,10},{9,11},{10,... | collective-permute-start | bytes 1572872 | tf_op jit(solution)/shard_map/ppermute | solution.py:54
  128.7 19.9 %collective-permute-done.5 = f32[1,4,128,128]{2,3,1,0:T(8,128)S(1)} collective-permute-done((f32[1,4,128,128]{2,3,1,0:T(8,128)S(1)}, f32[1,4,128,128]{2,3,1,0:T(8,128)S(1)}, u32[]{:S(2)}, u32[]{:S(2)}) %collective-permute-start.5) | collective-permute-done | bytes 262176 | tf_op jit(solution)/shard_map/ppermute | solution.py:54
  148.7 11.1 %collective-permute-done.7 = f32[1,8,128,128]{2,3,1,0:T(8,128)S(1)} collective-permute-done((f32[1,8,128,128]{2,3,1,0:T(8,128)S(1)}, f32[1,8,128,128]{2,3,1,0:T(8,128)S(1)}, u32[]{:S(2)}, u32[]{:S(2)}) %collective-permute-start.7) | collective-permute-done | bytes 524320 | tf_op jit(solution)/shard_map/ppermute | solution.py:54
  159.8 0.1 fusion.31
  159.9 0.1 bitcast_reduce_fusion
  160.0 0.6 copy.125
  (32 shorter events, 0.5 us)
Async XLA Ops:
  0.0 14.9 %copy-start.1 = (f32[16,2048]{1,0:T(8,128)S(1)}, f32[16,2048]{1,0:T(8,128)}, u32[]{:S(2)}) copy-start(f32[16,2048]{1,0:T(8,128)} %param.4) | copy-start | bytes 393220
  2.3 40.7 %all-to-all-start = ((bf16[64,4,2048]{2,1,0:T(4,128)(2,1)}), bf16[64,4,2048]{2,1,0:T(4,128)(2,1)S(1)}, u32[]{:S(2)}, u32[]{:S(2)}) async-start(bf16[64,4,2048]{2,1,0:T(4,128)(2,1)} %reshape.550), calls=%async_computation | async-start | bytes 2097152 | tf_op jit(solution)/shard_map/all_to_all | solution.py:68
  43.0 10.4 %slice-start = ((s8[8388608]{0:T(1024)(128)(4,1)}), s8[4194304]{0:T(1024)(128)(4,1)S(1)}, s32[]{:S(2)}) async-start(s8[8388608]{0:T(1024)(128)(4,1)} %bitcast.189), calls=%async_computation.2 | async-start | bytes 8388608
  43.6 9.8 %slice-start.1 = ((s8[8388608]{0:T(1024)(128)(4,1)}), s8[4194304]{0:T(1024)(128)(4,1)S(1)}, s32[]{:S(2)}) async-start(s8[8388608]{0:T(1024)(128)(4,1)} %bitcast.189), calls=%async_computation.3 | async-start | bytes 8388608
  57.1 33.8 %all-to-all-start.1 = ((bf16[64,32,256]{2,1,0:T(8,128)(2,1)}), bf16[64,32,256]{2,1,0:T(8,128)(2,1)S(1)}, u32[]{:S(2)}, u32[]{:S(2)}) async-start(bf16[64,32,256]{2,1,0:T(8,128)(2,1)} %bitcast.19), calls=%async_computation.1 | async-start | bytes 2097152 | tf_op jit(solution)/shard_map/all_to_all | solution.py:88
  92.4 3.4 %copy-start = (bf16[16,512,4,128]{3,2,1,0:T(4,128)(2,1)S(1)}, bf16[16,512,4,128]{3,2,1,0:T(4,128)(2,1)}, u32[]{:S(2)}) copy-start(bf16[16,512,4,128]{3,2,1,0:T(4,128)(2,1)} %reshape.556) | copy-start | bytes 25165828
  98.2 5.1 %collective-permute-start = (f32[2,2,128,128]{2,3,1,0:T(8,128)S(1)}, f32[2,2,128,128]{2,3,1,0:T(8,128)S(1)}, u32[]{:S(2)}, u32[]{:S(2)}) collective-permute-start(f32[2,2,128,128]{2,3,1,0:T(8,128)S(1)} %select_bitcast_fusion.5), channel_id=1, source_target_pairs={{0,1},{1,0},{2,3},{3,2},{4,5},{5,4},{6,7},{7,6},{8,9},{9,8},{10,11... | collective-permute-start | bytes 786440 | tf_op jit(solution)/shard_map/ppermute | solution.py:54
  100.8 6.9 %collective-permute-start.2 = (f32[2,2,128,128]{2,3,0,1:T(8,128)S(1)}, f32[2,2,128,128]{2,3,0,1:T(8,128)S(1)}, u32[]{:S(2)}, u32[]{:S(2)}) collective-permute-start(f32[2,2,128,128]{2,3,0,1:T(8,128)S(1)} %get-tuple-element.13), channel_id=1, source_target_pairs={{0,1},{1,0},{2,3},{3,2},{4,5},{5,4},{6,7},{7,6},{8,9},{9,8},{10,11... | collective-permute-start | bytes 786440 | tf_op jit(solution)/shard_map/ppermute | solution.py:54
  101.7 18.8 %collective-permute-start.4 = (f32[2,4,128,128]{2,3,0,1:T(8,128)}, f32[2,4,128,128]{2,3,0,1:T(8,128)}, u32[]{:S(2)}, u32[]{:S(2)}) collective-permute-start(f32[2,4,128,128]{2,3,0,1:T(8,128)} %select_bitcast_fusion.2), channel_id=1, source_target_pairs={{0,1},{1,0},{2,3},{3,2},{4,5},{5,4},{6,7},{7,6},{8,9},{9,8},{10,11... | collective-permute-start | bytes 1572872 | tf_op jit(solution)/shard_map/ppermute | solution.py:54
  103.3 22.1 %collective-permute-start.6 = (f32[2,8,128,128]{2,3,0,1:T(8,128)}, f32[2,8,128,128]{2,3,0,1:T(8,128)}, u32[]{:S(2)}, u32[]{:S(2)}) collective-permute-start(f32[2,8,128,128]{2,3,0,1:T(8,128)} %select_bitcast_fusion), channel_id=1, source_target_pairs={{0,1},{1,0},{2,3},{3,2},{4,5},{5,4},{6,7},{7,6},{8,9},{9,8},{10,11... | collective-permute-start | bytes 3145736 | tf_op jit(solution)/shard_map/ppermute | solution.py:54
  103.4 12.0 %collective-permute-start.1 = (f32[1,2,128,128]{2,3,1,0:T(8,128)S(1)}, f32[1,2,128,128]{2,3,1,0:T(8,128)S(1)}, u32[]{:S(2)}, u32[]{:S(2)}) collective-permute-start(f32[1,2,128,128]{2,3,1,0:T(8,128)S(1)} %select_bitcast_fusion.7), channel_id=1, source_target_pairs={{0,2},{1,3},{2,0},{3,1},{4,6},{5,7},{6,4},{7,5},{8,10},{9,11},{10,... | collective-permute-start | bytes 393224 | tf_op jit(solution)/shard_map/ppermute | solution.py:54
  107.8 12.6 %collective-permute-start.3 = (f32[1,2,128,128]{2,3,1,0:T(8,128)S(1)}, f32[1,2,128,128]{2,3,1,0:T(8,128)S(1)}, u32[]{:S(2)}, u32[]{:S(2)}) collective-permute-start(f32[1,2,128,128]{2,3,1,0:T(8,128)S(1)} %select_bitcast_fusion.6), channel_id=1, source_target_pairs={{0,2},{1,3},{2,0},{3,1},{4,6},{5,7},{6,4},{7,5},{8,10},{9,11},{10,... | collective-permute-start | bytes 393224 | tf_op jit(solution)/shard_map/ppermute | solution.py:54
  121.7 26.9 %collective-permute-start.5 = (f32[1,4,128,128]{2,3,1,0:T(8,128)S(1)}, f32[1,4,128,128]{2,3,1,0:T(8,128)S(1)}, u32[]{:S(2)}, u32[]{:S(2)}) collective-permute-start(f32[1,4,128,128]{2,3,1,0:T(8,128)S(1)} %select_bitcast_fusion.3), channel_id=1, source_target_pairs={{0,2},{1,3},{2,0},{3,1},{4,6},{5,7},{6,4},{7,5},{8,10},{9,11},{10,... | collective-permute-start | bytes 786440 | tf_op jit(solution)/shard_map/ppermute | solution.py:54
  126.9 33.0 %collective-permute-start.7 = (f32[1,8,128,128]{2,3,1,0:T(8,128)S(1)}, f32[1,8,128,128]{2,3,1,0:T(8,128)S(1)}, u32[]{:S(2)}, u32[]{:S(2)}) collective-permute-start(f32[1,8,128,128]{2,3,1,0:T(8,128)S(1)} %select_bitcast_fusion.1), channel_id=1, source_target_pairs={{0,2},{1,3},{2,0},{3,1},{4,6},{5,7},{6,4},{7,5},{8,10},{9,11},{10,... | collective-permute-start | bytes 1572872 | tf_op jit(solution)/shard_map/ppermute | solution.py:54
